TPU v7x, 512 devices: a whole 4x8x8 slice. The times are simulated.
512 devices in a mesh: tensor: 8 (over y), expert: 64 (over x, z, core).
Axes of the slice: x: 4, y: 8, z: 8, core: 2. Of those that a mesh axis runs over, the one named last changes fastest.
Arguments:
- attn_partial: bfloat16 [8, 4096, 4096], P('tensor', 'expert'), may hold values from -6 to 6
- norm_gain: float32 [4096], replicated, may hold values from 0.1 to 1.9
- expert_ids: int32 [4096, 8], P('expert'), may hold values from 0 to 63, all different within a row; in each aligned block of 8 rows (0 to 7, 8 to 15, ...) at most 2 rows name the same one
- route_weights: float32 [4096, 8], P('expert'), may hold values from 0.1 to 1
- gate_proj: bfloat16 [64, 4096, 1024], P('expert', None, 'tensor'), may hold values from -0.09375 to 0.09375
- up_proj: bfloat16 [64, 4096, 1024], P('expert', None, 'tensor'), may hold values from -0.09375 to 0.09375
- down_proj: bfloat16 [64, 1024, 4096], P('expert', None, 'tensor'), may hold values from -0.1875 to 0.1875
Outputs:
- combined: bfloat16 [4096, 4096], P(('expert', 'tensor'))
Inputs may be any that keep to these rules, and one draw needn't show every extreme that they name: `expert_ids`: each row names 8 different experts. In each aligned block of 8 rows (the rows of one device in the output's order) no expert is named by more than 2 rows, a bound that some block reaches.
All inputs are finite; a program needn't handle non-finite values.
Results may differ from a plain program's by a relative error of at most 0.025.
Values may be sent and summed in bfloat16 or wider, within the bound.
No kernel may reach another device: no remote copies, remote signals or barrier semaphores. Data moves between devices by JAX's collectives and lax.ppermute only.
A program may use at most 64 MiB of HBM per device.

v0:
```python
import math

import jax
import jax.numpy as jnp
from jax import lax
from jax.sharding import PartitionSpec as P

QB = 128


def normalize_quantize(summed, norm_gain, block_width):
    row_count, feature_width = summed.shape
    mean_sq = jnp.mean(summed * summed, axis=-1, keepdims=True)
    normed = summed * lax.rsqrt(mean_sq + 1e-06) * norm_gain
    blocks = normed.reshape(row_count, feature_width // block_width, block_width)
    scales = ((jnp.max(jnp.abs(blocks), axis=-1) + 1e-06) / 448.0).astype(jnp.bfloat16)
    values = (blocks / scales.astype(jnp.float32)[:, :, None]).astype(jnp.bfloat16)
    return (values.reshape(row_count, feature_width), scales)


def route_slots(grouped_ids, expert_total):
    labels = jnp.arange(expert_total, dtype=jnp.int32)
    member = jnp.sum((grouped_ids[..., None] == labels).astype(jnp.int32), axis=-2)
    earlier = jnp.cumsum(member, axis=-2) - member
    return (member, earlier)


def place_rows(values, scales, member, earlier, capacity):
    places = jnp.arange(capacity, dtype=jnp.int32)
    chosen = (earlier[..., None] == places) & (member[..., None] > 0)
    chosen_bf = chosen.astype(jnp.bfloat16)
    send_values = jnp.einsum(
        "brec,brd->ebcd", chosen_bf, values, preferred_element_type=jnp.float32
    ).astype(jnp.bfloat16)
    send_scales = jnp.einsum(
        "brec,brn->ebcn", chosen_bf, scales, preferred_element_type=jnp.float32
    ).astype(jnp.bfloat16)
    return (send_values, send_scales)


def expert_front(values, scales, gate_matrix, up_matrix, block_width):
    row_count, feature_width = values.shape
    block_count = feature_width // block_width
    block_rows = math.gcd(row_count, 256)

    def front_block(inputs_pair):
        part_values, part_scales = inputs_pair
        pieces = part_values.reshape(block_rows, block_count, block_width).astype(jnp.float32)
        restored = (pieces * part_scales.astype(jnp.float32)[:, :, None]).astype(jnp.bfloat16)
        restored = restored.reshape(block_rows, feature_width)
        gate_act = jnp.dot(restored, gate_matrix, preferred_element_type=jnp.float32)
        up_act = jnp.dot(restored, up_matrix, preferred_element_type=jnp.float32)
        return (jax.nn.silu(gate_act) * up_act).astype(jnp.bfloat16)

    stacked = (
        values.reshape(row_count // block_rows, block_rows, feature_width),
        scales.reshape(row_count // block_rows, block_rows, block_count),
    )
    hidden = lax.map(front_block, stacked)
    return hidden.reshape(row_count, -1)


def on_device(attn_partial, norm_gain, expert_ids, route_weights, gate_proj, up_proj, down_proj):
    tensor_count = lax.axis_size("tensor")
    expert_count = lax.axis_size("expert")
    tensor_index = lax.axis_index("tensor")
    group_tokens = expert_ids.shape[0]
    top_count = expert_ids.shape[1]
    row_count = group_tokens // tensor_count
    feature_width = attn_partial.shape[2]
    block_count = feature_width // QB
    capacity = max(2, (2 * row_count * top_count + expert_count - 1) // expert_count)
    gate_matrix = gate_proj[0]
    up_matrix = up_proj[0]
    down_matrix = down_proj[0]
    hidden_share = gate_matrix.shape[1]
    column_share = down_matrix.shape[1]
    own_start = tensor_index * row_count
    own_ids = lax.dynamic_slice_in_dim(expert_ids, own_start, row_count, 0)
    own_weights = lax.dynamic_slice_in_dim(route_weights, own_start, row_count, 0)
    partial_sum = attn_partial[0].astype(jnp.float32)
    summed = lax.psum(partial_sum.astype(jnp.bfloat16), "tensor").astype(jnp.float32)
    values, scales = normalize_quantize(summed, norm_gain, QB)
    group_ids = expert_ids.reshape(tensor_count, row_count, top_count)
    member, earlier = route_slots(group_ids, expert_count)
    send_values, send_scales = place_rows(
        values.reshape(tensor_count, row_count, feature_width),
        scales.reshape(tensor_count, row_count, block_count),
        member,
        earlier,
        capacity,
    )
    recv_values, recv_scales = (
        lax.all_to_all(send_values, "expert", split_axis=0, concat_axis=0, tiled=True),
        lax.all_to_all(send_scales, "expert", split_axis=0, concat_axis=0, tiled=True),
    )
    hidden = expert_front(
        recv_values.reshape(-1, feature_width),
        recv_scales.reshape(-1, block_count),
        gate_matrix,
        up_matrix,
        QB,
    )
    hidden = hidden.reshape(expert_count, tensor_count, capacity, hidden_share)
    own_member = lax.dynamic_index_in_dim(member, tensor_index, 0, keepdims=False)
    own_earlier = lax.dynamic_index_in_dim(earlier, tensor_index, 0, keepdims=False)
    slot_total = expert_count * tensor_count * capacity
    expert_sum = jnp.dot(
        lax.all_gather(hidden.reshape(slot_total, hidden_share), "tensor", axis=1, tiled=True),
        down_matrix,
        preferred_element_type=jnp.float32,
    )
    expert_rows = expert_sum.astype(jnp.bfloat16).reshape(
        expert_count, tensor_count, capacity, column_share
    )
    returned = lax.all_to_all(
        lax.all_to_all(expert_rows, "tensor", split_axis=1, concat_axis=3, tiled=True),
        "expert",
        split_axis=0,
        concat_axis=0,
        tiled=True,
    )
    returned = returned.reshape(expert_count, capacity, feature_width)
    labels = jnp.arange(expert_count, dtype=jnp.int32)
    pair_weight = jnp.sum(
        jnp.where(own_ids[..., None] == labels, own_weights[..., None], 0.0), axis=1
    )
    places = jnp.arange(capacity, dtype=jnp.int32)
    mixing = jnp.where(
        (own_earlier[..., None] == places) & (own_member[..., None] > 0),
        pair_weight[..., None],
        0.0,
    )
    combined = jnp.einsum(
        "rec,ecd->rd", mixing, returned.astype(jnp.float32), precision=lax.Precision.HIGHEST
    )
    return combined.astype(jnp.bfloat16)


def solution(mesh):
    return jax.shard_map(
        on_device,
        mesh=mesh,
        in_specs=(
            P("tensor", "expert", None),
            P(),
            P("expert", None),
            P("expert", None),
            P("expert", None, "tensor"),
            P("expert", None, "tensor"),
            P("expert", None, "tensor"),
        ),
        out_specs=P(("expert", "tensor"), None),
        check_vma=False,
    )
```

profile of v0, /device:TPU:1, one launch (start us, length us, event | category | flops | bytes accessed | tf_op | source)
XLA Modules:
  0.0 508.3 jit_solution(14410074035324619564)
XLA Ops:
  8.3 80.7 %all-reduce.2.cloned.1.call-done = bf16[64,4096]{1,0:T(8,128)(2,1)} async-done(((bf16[64,4096]{1,0:T(8,128)(2,1)}), bf16[64,4096]{1,0:T(8,128)(2,1)}) %all-reduce.2.cloned.1.call-update) | async-done | bytes 524304 | tf_op jit(solution)/shard_map/psum | solution.py:82
  89.0 1.2 fusion.9
  90.3 1.3 fusion.14
  92.2 1.3 div.31
  93.5 1.4 div.32
  96.2 16.2 %all-to-all-start.1 = ((bf16[64,2,256]{2,1,0:T(2,128)(2,1)}), bf16[64,2,256]{2,1,0:T(2,128)(2,1)S(1)}, u32[]{:S(2)}, u32[]{:S(2)}) async-start(bf16[64,2,256]{2,1,0:T(2,128)(2,1)} %reshape.82), calls=%async_computation.1 | async-start | bytes 131072 | tf_op jit(solution)/shard_map/all_to_all | solution.py:95
  112.4 2.4 convert_bitcast_fusion
  114.8 16.0 %copy.37 = bf16[64,8,2,4096]{3,2,1,0:T(2,128)(2,1)} copy(bf16[64,8,2,4096]{3,0,2,1:T(8,128)(2,1)S(1)} %convert_bitcast_fusion) | data formatting | bytes 16777216 | tf_op jit(solution)/shard_map/convert_element_type | solution.py:34
  130.7 10.5 %all-to-all-start = ((bf16[64,8,2,4096]{3,2,1,0:T(2,128)(2,1)}), bf16[64,8,2,4096]{3,2,1,0:T(2,128)(2,1)}, u32[]{:S(2)}, u32[]{:S(2)}) async-start(bf16[64,8,2,4096]{3,2,1,0:T(2,128)(2,1)} %copy.37), calls=%async_computation | async-start | bytes 16777216 | tf_op jit(solution)/shard_map/all_to_all | solution.py:94
  141.7 185.3 %all-to-all-done = bf16[64,8,2,4096]{3,2,1,0:T(2,128)(2,1)} async-done(((bf16[64,8,2,4096]{3,2,1,0:T(2,128)(2,1)}), bf16[64,8,2,4096]{3,2,1,0:T(2,128)(2,1)}, u32[]{:S(2)}, u32[]{:S(2)}) %all-to-all-start) | async-done | bytes 8388640 | tf_op jit(solution)/shard_map/all_to_all | solution.py:94
  327.0 13.1 %reshape_reshape.7 = bf16[4,256,4096]{2,1,0:T(8,128)(2,1)} reshape(bf16[64,8,2,4096]{3,2,1,0:T(2,128)(2,1)} %all-to-all-done) | data formatting | bytes 16777216 | tf_op jit(solution)/shard_map/reshape;reshape | solution.py:56
  340.1 41.2 %while.10 = (s32[]{:T(128)}, bf16[4,256,128]{2,1,0:T(8,128)(2,1)}, bf16[4,256,4096]{2,1,0:T(8,128)(2,1)}, bf16[4,256,32]{2,1,0:T(8,128)(2,1)S(1)}, bf16[4096,128...) while((s32[]{:T(128)}, bf16[4,256,128]{2,1,0:T(8,128)(2,1)}, ...), condition=%wide.region_7.8_spmd, body=%wide.region_6.7_spmd.sunk | while | flops 543367168 | bytes 19285584 | solution.py:59
  340.1 1.1 mul.111
  341.3 4.3 fusion.55
  345.5 4.9 fusion.56
  350.4 1.1 mul.111
  351.6 4.3 fusion.55
  355.8 4.9 fusion.56
  360.8 1.1 mul.111
  361.9 4.3 fusion.55
  366.2 4.9 fusion.56
  371.1 1.1 mul.111
  372.2 4.3 fusion.55
  376.5 4.9 fusion.56
  381.4 38.7 %all-gather.2.cloned.1.call-done = bf16[1024,1024]{1,0:T(8,128)(2,1)} async-done(((bf16[1024,128]{1,0:T(8,128)(2,1)}), bf16[1024,1024]{1,0:T(8,128)(2,1)}) %all-gather.2.cloned.1.call-update) | async-done | bytes 2097168 | tf_op jit(solution)/shard_map/all_gather | solution.py:109
  420.1 2.8 convolution_convert_fusion
  424.2 25.7 %all_to_all.33 = bf16[64,8,2,512]{3,2,0,1:T(2,128)(2,1)S(1)} all-to-all(bf16[64,8,2,512]{3,2,0,1:T(2,128)(2,1)S(1)} %copy.39), channel_id=1, replica_groups=mesh['tensor'=8,'expert'=64] {'tensor'}, dimensions={1} | all-to-all | bytes 2097152 | tf_op jit(solution)/shard_map/all_to_all | solution.py:117
  449.9 1.1 copy.46
  451.0 1.6 reshape.81
  452.6 18.1 %all-to-all-start.3 = ((bf16[64,1,2,4096]{3,2,1,0:T(2,128)(2,1)}), bf16[64,1,2,4096]{3,2,1,0:T(2,128)(2,1)S(1)}, u32[]{:S(2)}, u32[]{:S(2)}) async-start(bf16[64,1,2,4096]{3,2,1,0:T(2,128)(2,1)} %reshape.81), calls=%async_computation.3 | async-start | bytes 2097152 | tf_op jit(solution)/shard_map/all_to_all | solution.py:116
  471.1 28.1 %all-to-all-done.3 = bf16[64,1,2,4096]{3,2,1,0:T(2,128)(2,1)S(1)} async-done(((bf16[64,1,2,4096]{3,2,1,0:T(2,128)(2,1)}), bf16[64,1,2,4096]{3,2,1,0:T(2,128)(2,1)S(1)}, u32[]{:S(2)}, u32[]{:S(2)}) %all-to-all-start.3) | async-done | bytes 1048608 | tf_op jit(solution)/shard_map/all_to_all | solution.py:116
  499.3 2.2 fusion.7
  (46 shorter events, 5.6 us)
Async XLA Ops:
  6.5 413.6 %copy-start = (bf16[1,1024,512]{2,1,0:T(8,128)(2,1)S(1)}, bf16[1,1024,512]{2,1,0:T(8,128)(2,1)}, u32[]{:S(2)}) copy-start(bf16[1,1024,512]{2,1,0:T(8,128)(2,1)} %param.15) | copy-start | bytes 3145732
  6.5 82.5 %all-reduce.2.cloned.1.call-start = ((), (), s32[]{:S(2)}) async-start(), calls=%async_computation.4 | async-start | bytes 1048576 | tf_op jit(solution)/shard_map/psum | solution.py:82
  90.3 22.1 %copy-start.3 = (bf16[64,4096]{1,0:T(8,128)(2,1)S(1)}, bf16[64,4096]{1,0:T(8,128)(2,1)}, u32[]{:S(2)}) copy-start(bf16[64,4096]{1,0:T(8,128)(2,1)} %all-reduce.2.cloned.1.call-done) | copy-start | bytes 1572868
  90.3 22.1 %copy-start.4 = (f32[4096]{0:T(1024)S(1)}, f32[4096]{0:T(1024)}, u32[]{:S(2)}) copy-start(f32[4096]{0:T(1024)} %param.10) | copy-start | bytes 49156
  96.2 34.6 %all-to-all-start.1 = ((bf16[64,2,256]{2,1,0:T(2,128)(2,1)}), bf16[64,2,256]{2,1,0:T(2,128)(2,1)S(1)}, u32[]{:S(2)}, u32[]{:S(2)}) async-start(bf16[64,2,256]{2,1,0:T(2,128)(2,1)} %reshape.82), calls=%async_computation.1 | async-start | bytes 131072 | tf_op jit(solution)/shard_map/all_to_all | solution.py:95
  130.7 196.3 %all-to-all-start = ((bf16[64,8,2,4096]{3,2,1,0:T(2,128)(2,1)}), bf16[64,8,2,4096]{3,2,1,0:T(2,128)(2,1)}, u32[]{:S(2)}, u32[]{:S(2)}) async-start(bf16[64,8,2,4096]{3,2,1,0:T(2,128)(2,1)} %copy.37), calls=%async_computation | async-start | bytes 16777216 | tf_op jit(solution)/shard_map/all_to_all | solution.py:94
  141.3 278.9 %all-gather.2.cloned.1.call-start = ((), (), s32[]{:S(2)}) async-start(), calls=%async_computation.5 | async-start | bytes 2359296 | tf_op jit(solution)/shard_map/all_gather | solution.py:109
  141.7 198.4 %copy-start.1 = (bf16[1,4096,128]{2,1,0:T(8,128)(2,1)S(1)}, bf16[1,4096,128]{2,1,0:T(8,128)(2,1)}, u32[]{:S(2)}) copy-start(bf16[1,4096,128]{2,1,0:T(8,128)(2,1)} %param.14) | copy-start | bytes 3145732
  141.7 198.4 %copy-start.2 = (bf16[1,4096,128]{2,1,0:T(8,128)(2,1)S(1)}, bf16[1,4096,128]{2,1,0:T(8,128)(2,1)}, u32[]{:S(2)}) copy-start(bf16[1,4096,128]{2,1,0:T(8,128)(2,1)} %param.13) | copy-start | bytes 3145732
  424.1 46.6 %copy-start.5 = (s32[64,8]{0,1:T(8,128)S(1)}, s32[64,8]{0,1:T(8,128)}, u32[]{:S(2)}) copy-start(s32[64,8]{0,1:T(8,128)} %param.11) | copy-start | bytes 6148
  424.2 46.7 %copy-start.6 = (f32[64,8]{0,1:T(8,128)S(1)}, f32[64,8]{0,1:T(8,128)}, u32[]{:S(2)}) copy-start(f32[64,8]{0,1:T(8,128)} %param.12) | copy-start | bytes 6148
  452.6 46.6 %all-to-all-start.3 = ((bf16[64,1,2,4096]{3,2,1,0:T(2,128)(2,1)}), bf16[64,1,2,4096]{3,2,1,0:T(2,128)(2,1)S(1)}, u32[]{:S(2)}, u32[]{:S(2)}) async-start(bf16[64,1,2,4096]{3,2,1,0:T(2,128)(2,1)} %reshape.81), calls=%async_computation.3 | async-start | bytes 2097152 | tf_op jit(solution)/shard_map/all_to_all | solution.py:116
Sparse Core Ops, SparseCore 0:
  9.7 79.3 all-reduce.1
  381.5 38.5 all-gather.1
where the time goes:
time: 509 us; the launch traced here: 508 us
  waiting for transfers between devices  334 us (66%)
  starting transfers between devices  45 us (9%)
  matrix products  44.2 us (9%)
  local copies, waits for them, and re-layouts  42.7 us (8%)
  blocking collectives  25.7 us (5%)
  between operations  13.6 us (3%)
    all_to_all x1, waiting for transfers between devices, on_device(): lax.all_to_all(send_values, 'expert', split_axis=0, concat_axis=0, tiled=...  185 us
    psum x1, waiting for transfers between devices, on_device(): lax.psum(partial_sum.astype(jnp.bfloat16), 'tensor').astype(jnp.float32)  80.7 us
    all_gather x1, waiting for transfers between devices, on_device(): lax.all_gather(hidden.reshape(slot_total, hidden_share), 'tensor', axis=1...  38.7 us
    all_to_all x1, waiting for transfers between devices, on_device(): lax.all_to_all(lax.all_to_all(expert_rows, 'tensor', split_axis=1, concat...  28.1 us
    all_to_all x1, blocking collectives, on_device(): lax.all_to_all(expert_rows, 'tensor', split_axis=1, concat_axis=3, tiled=...  25.7 us
    dot_general x4, matrix products, front_block(): up_act = jnp.dot(restored, up_matrix, preferred_element_type=jnp.float32)  19.6 us
    all_to_all x1, starting transfers between devices, on_device(): lax.all_to_all(lax.all_to_all(expert_rows, 'tensor', split_axis=1, concat...  18.1 us
    dot_general x4, matrix products, front_block(): jnp.dot(restored, gate_matrix, preferred_element_type=jnp.float32)  17 us
  transfers between devices with their start and end apart: 5, of which 4 were waited for; matrix products, arithmetic and copies ran while one was open for 4% of the time, Pallas kernels for 0%

commit v1 on v0

v1 whole, which is shorter than its diff:
```python
import jax
import jax.numpy as jnp
from jax import lax
from jax.sharding import PartitionSpec as P

QB = 128


def normalize_dequant(summed, norm_gain, block_width):
    row_count, feature_width = summed.shape
    mean_sq = jnp.mean(summed * summed, axis=-1, keepdims=True)
    normed = summed * lax.rsqrt(mean_sq + 1e-06) * norm_gain
    blocks = normed.reshape(row_count, feature_width // block_width, block_width)
    scales = ((jnp.max(jnp.abs(blocks), axis=-1) + 1e-06) / 448.0).astype(jnp.bfloat16)
    scale_f = scales.astype(jnp.float32)[:, :, None]
    values = (blocks / scale_f).astype(jnp.bfloat16)
    restored = (values.astype(jnp.float32) * scale_f).astype(jnp.bfloat16)
    return restored.reshape(row_count, feature_width)


def on_device(attn_partial, norm_gain, expert_ids, route_weights, gate_proj, up_proj, down_proj):
    tensor_count = lax.axis_size("tensor")
    expert_count = lax.axis_size("expert")
    tensor_index = lax.axis_index("tensor")
    group_tokens = expert_ids.shape[0]
    top_count = expert_ids.shape[1]
    row_count = group_tokens // tensor_count
    feature_width = attn_partial.shape[2]
    capacity = max(2, (2 * row_count * top_count + expert_count - 1) // expert_count)
    gate_matrix = gate_proj[0]
    up_matrix = up_proj[0]
    down_matrix = down_proj[0]
    column_share = down_matrix.shape[1]
    own_start = tensor_index * row_count
    own_ids = lax.dynamic_slice_in_dim(expert_ids, own_start, row_count, 0)
    own_weights = lax.dynamic_slice_in_dim(route_weights, own_start, row_count, 0)

    parts = lax.all_to_all(
        attn_partial[0].reshape(tensor_count, row_count, feature_width),
        "tensor", split_axis=0, concat_axis=0, tiled=True,
    )
    summed = jnp.sum(parts.astype(jnp.float32), axis=0)
    restored = normalize_dequant(summed, norm_gain, QB)

    labels = jnp.arange(expert_count, dtype=jnp.int32)
    hit = own_ids[..., None] == labels
    member = jnp.sum(hit.astype(jnp.int32), axis=1)
    earlier = jnp.cumsum(member, axis=0) - member
    places = jnp.arange(capacity, dtype=jnp.int32)
    chosen = (earlier[..., None] == places) & (member[..., None] > 0)
    send = jnp.einsum(
        "rec,rd->ecd", chosen.astype(jnp.bfloat16), restored, preferred_element_type=jnp.float32
    ).astype(jnp.bfloat16)
    recv = lax.all_to_all(send, "expert", split_axis=0, concat_axis=0, tiled=True)
    rows = lax.all_gather(recv, "tensor", axis=0, tiled=False)
    slot_total = tensor_count * expert_count * capacity
    rows = rows.reshape(slot_total, feature_width)
    gate_act = jnp.dot(rows, gate_matrix, preferred_element_type=jnp.float32)
    up_act = jnp.dot(rows, up_matrix, preferred_element_type=jnp.float32)
    hidden = (jax.nn.silu(gate_act) * up_act).astype(jnp.bfloat16)
    expert_sum = jnp.dot(
        lax.all_gather(hidden, "tensor", axis=1, tiled=True),
        down_matrix,
        preferred_element_type=jnp.float32,
    )
    expert_rows = expert_sum.astype(jnp.bfloat16).reshape(
        tensor_count, expert_count, capacity, column_share
    )
    returned = lax.all_to_all(
        lax.all_to_all(expert_rows, "tensor", split_axis=0, concat_axis=3, tiled=True),
        "expert",
        split_axis=1,
        concat_axis=1,
        tiled=True,
    )
    returned = returned.reshape(expert_count, capacity, feature_width)
    pair_weight = jnp.sum(jnp.where(hit, own_weights[..., None], 0.0), axis=1)
    mixing = jnp.where(chosen, pair_weight[..., None], 0.0)
    combined = jnp.einsum(
        "rec,ecd->rd", mixing, returned.astype(jnp.float32), precision=lax.Precision.HIGHEST
    )
    return combined.astype(jnp.bfloat16)


def solution(mesh):
    return jax.shard_map(
        on_device,
        mesh=mesh,
        in_specs=(
            P("tensor", "expert", None),
            P(),
            P("expert", None),
            P("expert", None),
            P("expert", None, "tensor"),
            P("expert", None, "tensor"),
            P("expert", None, "tensor"),
        ),
        out_specs=P(("expert", "tensor"), None),
        check_vma=False,
    )
```

time: 509 us -> 321 us (0.63)
  waiting for transfers between devices: 334 us -> 175 us
  blocking collectives: 25.7 us -> 71 us
  matrix products: 44.2 us -> 15.1 us
  local copies, waits for them, and re-layouts: 42.7 us -> 18.6 us
  starting transfers between devices: 45 us -> 25.9 us
    all_to_all x3 -> x2, waiting for transfers between devices: 213 us -> 42.2 us  [the longest x1 28.3 us: on_device(): lax.all_to_all(lax.all_to_all(expert_rows, 'tensor', split_axis=0, concat...]
    all_gather x1 -> x2, waiting for transfers between devices: 38.7 us -> 132 us  [the longest x1 87.9 us: on_device(): rows = lax.all_gather(recv, 'tensor', axis=0, tiled=False)]
    psum x1 -> x0, waiting for transfers between devices: 80.7 us -> none  [on_device(): lax.psum(partial_sum.astype(jnp.bfloat16), 'tensor').astype(jnp.float32)]
    all_to_all x1 -> x2, blocking collectives: 25.7 us -> 71 us  [the longest x1 45.3 us: on_device(): lax.all_to_all(send, 'expert', split_axis=0, concat_axis=0, tiled=True)]
    dot_general x11 -> x4, matrix products: 42.1 us -> 13 us  [the longest x1 5.86 us: on_device(): gate_act = jnp.dot(rows, gate_matrix, preferred_element_type=jnp.float32)]
    all_to_all x3 -> x2, starting transfers between devices: 44.8 us -> 25.9 us  [the longest x1 18.1 us: on_device(): lax.all_to_all(lax.all_to_all(expert_rows, 'tensor', split_axis=0, concat...]
    convert_element_type x2, local copies, waits for them, and re-layouts: 16.2 us -> 1.17 us  [the longest x1 1.09 us: on_device(): send = jnp.einsum('rec,rd->ecd', chosen.astype(jnp.bfloat16), restored, p...]
    another operation x1 -> x0, local copies, waits for them, and re-layouts: 13.1 us -> none  [expert_front(): values.reshape(row_count // block_rows, block_rows, feature_width)]
  transfers between devices with their start and end apart: 5 -> 4, of which waited for: 4 -> 4; matrix products, arithmetic and copies ran while one was open for 4% -> 0% of each run, Pallas kernels for 0% -> 0%
where the time goes in v1:
time: 321 us; the launch traced here: 320 us
  waiting for transfers between devices  175 us (55%)
  blocking collectives  71 us (22%)
  starting transfers between devices  25.9 us (8%)
  local copies, waits for them, and re-layouts  18.6 us (6%)
  matrix products  15.1 us (5%)
  between operations  13.5 us (4%)
    all_gather x1, waiting for transfers between devices, on_device(): rows = lax.all_gather(recv, 'tensor', axis=0, tiled=False)  87.9 us
    all_to_all x1, blocking collectives, on_device(): lax.all_to_all(send, 'expert', split_axis=0, concat_axis=0, tiled=True)  45.3 us
    all_gather x1, waiting for transfers between devices, on_device(): lax.all_gather(hidden, 'tensor', axis=1, tiled=True)  44.5 us
    all_to_all x1, waiting for transfers between devices, on_device(): lax.all_to_all(lax.all_to_all(expert_rows, 'tensor', split_axis=0, concat...  28.3 us
    all_to_all x1, blocking collectives, on_device(): lax.all_to_all(expert_rows, 'tensor', split_axis=0, concat_axis=3, tiled=...  25.8 us
    all_to_all x1, starting transfers between devices, on_device(): lax.all_to_all(lax.all_to_all(expert_rows, 'tensor', split_axis=0, concat...  18.1 us
    all_to_all x1, waiting for transfers between devices, on_device(): lax.all_to_all(attn_partial[0].reshape(tensor_count, row_count, feature_w...  13.9 us
    reshape x1, local copies, waits for them, and re-layouts, on_device(): rows = rows.reshape(slot_total, feature_width)  13.1 us
  transfers between devices with their start and end apart: 4, of which 4 were waited for; matrix products, arithmetic and copies ran while one was open for 0% of the time, Pallas kernels for 0%

profile of v1, /device:TPU:1, one launch (start us, length us, event | category | flops | bytes accessed | tf_op | source)
XLA Modules:
  0.0 320.2 jit_solution(14053400340128236630)
XLA Ops:
  6.5 7.8 %all-to-all-start = ((bf16[8,8,4096]{2,1,0:T(8,128)(2,1)}), bf16[8,8,4096]{2,1,0:T(8,128)(2,1)S(1)}, u32[]{:S(2)}, u32[]{:S(2)}) async-start(bf16[8,8,4096]{2,1,0:T(8,128)(2,1)} %bitcast.51), calls=%async_computation | async-start | bytes 1048576 | tf_op jit(solution)/shard_map/all_to_all | solution.py:38
  14.3 0.0 all-gather.6.cloned.1.call-start
  14.4 0.8 constant_dynamic-slice_fusion.1
  15.1 0.1 copy.36
  15.2 0.1 convert_reduce_fusion.1
  15.3 13.9 %all-to-all-done = bf16[8,8,4096]{2,1,0:T(8,128)(2,1)S(1)} async-done(((bf16[8,8,4096]{2,1,0:T(8,128)(2,1)}), bf16[8,8,4096]{2,1,0:T(8,128)(2,1)S(1)}, u32[]{:S(2)}, u32[]{:S(2)}) %all-to-all-start) | async-done | bytes 524320 | tf_op jit(solution)/shard_map/all_to_all | solution.py:38
  29.3 0.1 convert_reduce_fusion
  29.3 0.1 multiply_reduce_fusion
  29.5 0.9 fusion.12
  30.4 0.1 copy.38
  30.5 0.1 copy.39
  30.6 1.2 convolution_convert_fusion
  31.8 1.1 copy.40
  32.9 45.3 %all_to_all.33 = bf16[64,2,4096]{2,1,0:T(2,128)(2,1)} all-to-all(bf16[64,2,4096]{2,1,0:T(2,128)(2,1)S(1)} %copy.40), channel_id=1, replica_groups=mesh['tensor'=8,'expert'=64] {'expert'}, dimensions={0} | all-to-all | bytes 2097152 | tf_op jit(solution)/shard_map/all_to_all | solution.py:54
  78.2 0.0 all-gather.4.cloned.1.call-start
  78.2 87.9 %all-gather.6.cloned.1.call-done = bf16[512,2,4096]{2,1,0:T(2,128)(2,1)} async-done(((bf16[64,2,4096]{2,1,0:T(2,128)(2,1)}), bf16[512,2,4096]{2,1,0:T(2,128)(2,1)}) %all-gather.6.cloned.1.call-update) | async-done | bytes 8388624 | tf_op jit(solution)/shard_map/all_gather | solution.py:55
  166.1 13.1 %reshape.59 = bf16[1024,4096]{1,0:T(8,128)(2,1)} reshape(bf16[512,2,4096]{2,1,0:T(2,128)(2,1)} %all-gather.6.cloned.1.call-done) | data formatting | bytes 16777216 | tf_op jit(solution)/shard_map/reshape | solution.py:57
  179.2 5.9 %fusion.5 = f32[1024,128]{1,0:T(8,128)S(1)} fusion(bf16[1024,4096]{1,0:T(8,128)(2,1)} %reshape.59, bf16[1,4096,128]{2,1,0:T(8,128)(2,1)S(1)} %copy-done.3), kind=kOutput, calls=%fused_computation.9 | convolution fusion | flops 1073741824 | bytes 9961472 | tf_op jit(solution)/shard_map/dot_general | solution.py:58
  185.1 0.1 copy-done.4
  185.2 3.1 fusion.1
  188.3 44.5 %all-gather.4.cloned.1.call-done = bf16[1024,1024]{1,0:T(8,128)(2,1)} async-done(((bf16[1024,128]{1,0:T(8,128)(2,1)}), bf16[1024,1024]{1,0:T(8,128)(2,1)}) %all-gather.4.cloned.1.call-update) | async-done | bytes 2097168 | tf_op jit(solution)/shard_map/all_gather | solution.py:62
  232.8 2.8 convolution_convert_fusion.1
  235.7 0.4 reshape.60
  236.1 25.8 %all_to_all.34 = bf16[8,64,2,512]{3,2,1,0:T(2,128)(2,1)S(1)} all-to-all(bf16[8,64,2,512]{3,2,1,0:T(2,128)(2,1)S(1)} %reshape.60), channel_id=1, replica_groups=mesh['tensor'=8,'expert'=64] {'tensor'}, dimensions={0} | all-to-all | bytes 2097152 | tf_op jit(solution)/shard_map/all_to_all | solution.py:70
  261.9 1.1 copy.41
  263.0 1.6 all_to_all.27
  264.6 18.1 %all-to-all-start.3 = ((bf16[1,64,2,4096]{3,2,0,1:T(2,128)(2,1)}), bf16[1,64,2,4096]{3,2,0,1:T(2,128)(2,1)S(1)}, u32[]{:S(2)}, u32[]{:S(2)}) async-start(bf16[1,64,2,4096]{3,2,0,1:T(2,128)(2,1)} %all_to_all.27), calls=%async_computation.3 | async-start | bytes 2097152 | tf_op jit(solution)/shard_map/all_to_all | solution.py:69
  282.7 0.1 constant_dynamic-slice_fusion
  282.8 0.1 copy.37
  282.9 0.1 select_reduce_fusion
  282.9 28.3 %all-to-all-done.3 = bf16[1,64,2,4096]{3,2,0,1:T(2,128)(2,1)S(1)} async-done(((bf16[1,64,2,4096]{3,2,0,1:T(2,128)(2,1)}), bf16[1,64,2,4096]{3,2,0,1:T(2,128)(2,1)S(1)}, u32[]{:S(2)}, u32[]{:S(2)}) %all-to-all-start.3) | async-done | bytes 1048608 | tf_op jit(solution)/shard_map/all_to_all | solution.py:69
  311.2 2.2 fusion
  (16 shorter events, 0.1 us)
Async XLA Ops:
  6.5 226.3 %copy-start = (bf16[1,1024,512]{2,1,0:T(8,128)(2,1)S(1)}, bf16[1,1024,512]{2,1,0:T(8,128)(2,1)}, u32[]{:S(2)}) copy-start(bf16[1,1024,512]{2,1,0:T(8,128)(2,1)} %param.13) | copy-start | bytes 3145732
  6.5 22.7 %all-to-all-start = ((bf16[8,8,4096]{2,1,0:T(8,128)(2,1)}), bf16[8,8,4096]{2,1,0:T(8,128)(2,1)S(1)}, u32[]{:S(2)}, u32[]{:S(2)}) async-start(bf16[8,8,4096]{2,1,0:T(8,128)(2,1)} %bitcast.51), calls=%async_computation | async-start | bytes 1048576 | tf_op jit(solution)/shard_map/all_to_all | solution.py:38
  14.3 151.8 %all-gather.6.cloned.1.call-start = ((), (), s32[]{:S(2)}) async-start(), calls=%async_computation.5 | async-start | bytes 9437184 | tf_op jit(solution)/shard_map/all_gather | solution.py:55
  78.2 101.1 %copy-start.3 = (bf16[1,4096,128]{2,1,0:T(8,128)(2,1)S(1)}, bf16[1,4096,128]{2,1,0:T(8,128)(2,1)}, u32[]{:S(2)}) copy-start(bf16[1,4096,128]{2,1,0:T(8,128)(2,1)} %param.11) | copy-start | bytes 3145732
  78.2 154.6 %all-gather.4.cloned.1.call-start = ((), (), s32[]{:S(2)}) async-start(), calls=%async_computation.4 | async-start | bytes 2359296 | tf_op jit(solution)/shard_map/all_gather | solution.py:62
  179.2 5.9 %copy-start.1 = (bf16[1024,4096]{1,0:T(8,128)(2,1)S(1)}, bf16[1024,4096]{1,0:T(8,128)(2,1)}, u32[]{:S(2)}) copy-start(bf16[1024,4096]{1,0:T(8,128)(2,1)} %reshape.59) | copy-start | bytes 25165828
  179.2 6.0 %copy-start.4 = (bf16[1,4096,128]{2,1,0:T(8,128)(2,1)S(1)}, bf16[1,4096,128]{2,1,0:T(8,128)(2,1)}, u32[]{:S(2)}) copy-start(bf16[1,4096,128]{2,1,0:T(8,128)(2,1)} %param.12) | copy-start | bytes 3145732
  188.3 94.4 %copy-start.2 = (f32[64,8]{0,1:T(8,128)S(1)}, f32[64,8]{0,1:T(8,128)}, u32[]{:S(2)}) copy-start(f32[64,8]{0,1:T(8,128)} %param.10) | copy-start | bytes 6148
  264.6 46.6 %all-to-all-start.3 = ((bf16[1,64,2,4096]{3,2,0,1:T(2,128)(2,1)}), bf16[1,64,2,4096]{3,2,0,1:T(2,128)(2,1)S(1)}, u32[]{:S(2)}, u32[]{:S(2)}) async-start(bf16[1,64,2,4096]{3,2,0,1:T(2,128)(2,1)} %all_to_all.27), calls=%async_computation.3 | async-start | bytes 2097152 | tf_op jit(solution)/shard_map/all_to_all | solution.py:69
Sparse Core Ops, SparseCore 0:
  78.3 87.8 all-gather.5
  188.4 44.3 all-gather.3

commit v2 on v1

--- a/solution.py
+++ b/solution.py
@@ -52,15 +52,17 @@
         "rec,rd->ecd", chosen.astype(jnp.bfloat16), restored, preferred_element_type=jnp.float32
     ).astype(jnp.bfloat16)
     recv = lax.all_to_all(send, "expert", split_axis=0, concat_axis=0, tiled=True)
-    rows = lax.all_gather(recv, "tensor", axis=0, tiled=False)
-    slot_total = tensor_count * expert_count * capacity
-    rows = rows.reshape(slot_total, feature_width)
+    rows = lax.all_gather(
+        recv.reshape(expert_count * capacity, feature_width), "tensor", axis=0, tiled=True
+    )
     gate_act = jnp.dot(rows, gate_matrix, preferred_element_type=jnp.float32)
     up_act = jnp.dot(rows, up_matrix, preferred_element_type=jnp.float32)
     hidden = (jax.nn.silu(gate_act) * up_act).astype(jnp.bfloat16)
-    expert_sum = jnp.dot(
-        lax.all_gather(hidden, "tensor", axis=1, tiled=True),
-        down_matrix,
+    hidden_all = lax.all_gather(hidden, "tensor", axis=0, tiled=False)
+    expert_sum = jnp.einsum(
+        "tsh,thc->sc",
+        hidden_all,
+        down_matrix.reshape(tensor_count, -1, column_share),
         preferred_element_type=jnp.float32,
     )
     expert_rows = expert_sum.astype(jnp.bfloat16).reshape(

time: 321 us -> 303 us (0.944)
  local copies, waits for them, and re-layouts: 18.6 us -> 6.67 us
  waiting for transfers between devices: 175 us -> 169 us
    reshape x1, local copies, waits for them, and re-layouts: 13.1 us -> 1.27 us  [on_device(): recv.reshape(expert_count * capacity, feature_width)]
    all_gather x2, waiting for transfers between devices: 132 us -> 126 us  [the longest x1 87.9 us: on_device(): lax.all_gather(recv.reshape(expert_count * capacity, feature_width), 'ten...]
where the time goes in v2:
time: 303 us; the launch traced here: 302 us
  waiting for transfers between devices  169 us (56%)
  blocking collectives  71.7 us (24%)
  starting transfers between devices  24.9 us (8%)
  matrix products  15.2 us (5%)
  between operations  13.5 us (4%)
  local copies, waits for them, and re-layouts  6.67 us (2%)
    all_gather x1, waiting for transfers between devices, on_device(): lax.all_gather(recv.reshape(expert_count * capacity, feature_width), 'ten...  87.9 us
    all_to_all x1, blocking collectives, on_device(): lax.all_to_all(send, 'expert', split_axis=0, concat_axis=0, tiled=True)  45.2 us
    all_gather x1, waiting for transfers between devices, on_device(): hidden_all = lax.all_gather(hidden, 'tensor', axis=0, tiled=False)  38.6 us
    all_to_all x1, waiting for transfers between devices, on_device(): lax.all_to_all(lax.all_to_all(expert_rows, 'tensor', split_axis=0, concat...  28.3 us
    all_to_all x1, blocking collectives, on_device(): lax.all_to_all(expert_rows, 'tensor', split_axis=0, concat_axis=3, tiled=...  26.6 us
    all_to_all x1, starting transfers between devices, on_device(): lax.all_to_all(lax.all_to_all(expert_rows, 'tensor', split_axis=0, concat...  17 us
    all_to_all x1, waiting for transfers between devices, on_device(): lax.all_to_all(attn_partial[0].reshape(tensor_count, row_count, feature_w...  13.9 us
    all_to_all x1, starting transfers between devices, on_device(): lax.all_to_all(attn_partial[0].reshape(tensor_count, row_count, feature_w...  7.77 us
  transfers between devices with their start and end apart: 4, of which 4 were waited for; matrix products, arithmetic and copies ran while one was open for 0% of the time, Pallas kernels for 0%

profile of v2, /device:TPU:1, one launch (start us, length us, event | category | flops | bytes accessed | tf_op | source)
XLA Modules:
  0.0 302.0 jit_solution(6091969412281994335)
XLA Ops:
  6.5 7.8 %all-to-all-start = ((bf16[8,8,4096]{2,1,0:T(8,128)(2,1)}), bf16[8,8,4096]{2,1,0:T(8,128)(2,1)S(1)}, u32[]{:S(2)}, u32[]{:S(2)}) async-start(bf16[8,8,4096]{2,1,0:T(8,128)(2,1)} %bitcast.54), calls=%async_computation | async-start | bytes 1048576 | tf_op jit(solution)/shard_map/all_to_all | solution.py:38
  14.3 0.0 all-gather.4.cloned.1.call-start
  14.4 0.8 constant_dynamic-slice_fusion.1
  15.1 0.1 copy.31
  15.2 0.1 convert_reduce_fusion.1
  15.3 13.9 %all-to-all-done = bf16[8,8,4096]{2,1,0:T(8,128)(2,1)S(1)} async-done(((bf16[8,8,4096]{2,1,0:T(8,128)(2,1)}), bf16[8,8,4096]{2,1,0:T(8,128)(2,1)S(1)}, u32[]{:S(2)}, u32[]{:S(2)}) %all-to-all-start) | async-done | bytes 524320 | tf_op jit(solution)/shard_map/all_to_all | solution.py:38
  29.3 0.1 convert_reduce_fusion
  29.3 0.1 multiply_reduce_fusion
  29.5 0.9 fusion.11
  30.4 0.1 copy.33
  30.5 0.1 copy.34
  30.6 1.2 convolution_convert_fusion
  31.8 1.1 copy.35
  32.9 45.2 %all_to_all.33 = bf16[64,2,4096]{2,1,0:T(2,128)(2,1)S(1)} all-to-all(bf16[64,2,4096]{2,1,0:T(2,128)(2,1)S(1)} %copy.35), channel_id=1, replica_groups=mesh['tensor'=8,'expert'=64] {'expert'}, dimensions={0} | all-to-all | bytes 2097152 | tf_op jit(solution)/shard_map/all_to_all | solution.py:54
  78.0 1.3 reshape.59
  79.3 0.0 all-gather.4.cloned.1.call-update
  79.3 0.0 all-gather.6.cloned.1.call-start
  79.4 87.9 %all-gather.4.cloned.1.call-done = bf16[1024,4096]{1,0:T(8,128)(2,1)} async-done(((bf16[128,4096]{1,0:T(8,128)(2,1)}), bf16[1024,4096]{1,0:T(8,128)(2,1)}) %all-gather.4.cloned.1.call-update) | async-done | bytes 8388624 | tf_op jit(solution)/shard_map/all_gather | solution.py:55
  167.3 5.9 %fusion.4 = f32[1024,128]{1,0:T(8,128)S(1)} fusion(bf16[1024,4096]{1,0:T(8,128)(2,1)} %all-gather.4.cloned.1.call-done, bf16[1,4096,128]{2,1,0:T(8,128)(2,1)S(1)} %copy-done.3), kind=kOutput, calls=%fused_computation.8 | convolution fusion | flops 1073741824 | bytes 9961472 | tf_op jit(solution)/shard_map/dot_general | solution.py:58
  173.2 3.1 %fusion.1 = bf16[1024,128]{1,0:T(8,128)(2,1)} fusion(bf16[1024,4096]{1,0:T(8,128)(2,1)S(1)} %copy-done.2, bf16[1,4096,128]{2,1,0:T(8,128)(2,1)S(1)} %copy-done.4, f32[1024,128]{1,0:T(8,128)S(1)} %fusion.4), kind=kOutput, calls=%fused_computation.5 | convolution fusion | flops 1074528256 | bytes 10223616 | tf_op jit(solution)/shard_map/dot_general | solution.py:59
  176.3 38.6 %all-gather.6.cloned.1.call-done = bf16[8192,128]{1,0:T(8,128)(2,1)} async-done(((bf16[1024,128]{1,0:T(8,128)(2,1)}), bf16[8192,128]{1,0:T(8,128)(2,1)}) %all-gather.6.cloned.1.call-update) | async-done | bytes 2097168 | tf_op jit(solution)/shard_map/all_gather | solution.py:61
  214.9 2.8 bitcast_convert_fusion
  217.7 0.4 reshape.60
  218.1 26.6 %all_to_all.34 = bf16[8,64,2,512]{3,2,1,0:T(2,128)(2,1)S(1)} all-to-all(bf16[8,64,2,512]{3,2,1,0:T(2,128)(2,1)S(1)} %reshape.60), channel_id=1, replica_groups=mesh['tensor'=8,'expert'=64] {'tensor'}, dimensions={0} | all-to-all | bytes 2097152 | tf_op jit(solution)/shard_map/all_to_all | solution.py:72
  244.7 1.1 copy.36
  245.8 1.6 all_to_all.27
  247.4 17.0 %all-to-all-start.3 = ((bf16[1,64,2,4096]{3,2,0,1:T(2,128)(2,1)}), bf16[1,64,2,4096]{3,2,0,1:T(2,128)(2,1)S(1)}, u32[]{:S(2)}, u32[]{:S(2)}) async-start(bf16[1,64,2,4096]{3,2,0,1:T(2,128)(2,1)} %all_to_all.27), calls=%async_computation.3 | async-start | bytes 2097152 | tf_op jit(solution)/shard_map/all_to_all | solution.py:71
  264.5 0.1 constant_dynamic-slice_fusion
  264.5 0.1 copy.32
  264.6 0.1 select_reduce_fusion
  264.7 28.3 %all-to-all-done.3 = bf16[1,64,2,4096]{3,2,0,1:T(2,128)(2,1)S(1)} async-done(((bf16[1,64,2,4096]{3,2,0,1:T(2,128)(2,1)}), bf16[1,64,2,4096]{3,2,0,1:T(2,128)(2,1)S(1)}, u32[]{:S(2)}, u32[]{:S(2)}) %all-to-all-start.3) | async-done | bytes 1048608 | tf_op jit(solution)/shard_map/all_to_all | solution.py:71
  293.0 2.2 fusion
  (16 shorter events, 0.1 us)
Async XLA Ops:
  6.5 208.3 %copy-start = (bf16[1,1024,512]{2,1,0:T(8,128)(2,1)S(1)}, bf16[1,1024,512]{2,1,0:T(8,128)(2,1)}, u32[]{:S(2)}) copy-start(bf16[1,1024,512]{2,1,0:T(8,128)(2,1)} %param.13) | copy-start | bytes 3145732
  6.5 160.8 %copy-start.3 = (bf16[1,4096,128]{2,1,0:T(8,128)(2,1)S(1)}, bf16[1,4096,128]{2,1,0:T(8,128)(2,1)}, u32[]{:S(2)}) copy-start(bf16[1,4096,128]{2,1,0:T(8,128)(2,1)} %param.11) | copy-start | bytes 3145732
  6.5 22.7 %all-to-all-start = ((bf16[8,8,4096]{2,1,0:T(8,128)(2,1)}), bf16[8,8,4096]{2,1,0:T(8,128)(2,1)S(1)}, u32[]{:S(2)}, u32[]{:S(2)}) async-start(bf16[8,8,4096]{2,1,0:T(8,128)(2,1)} %bitcast.54), calls=%async_computation | async-start | bytes 1048576 | tf_op jit(solution)/shard_map/all_to_all | solution.py:38
  14.3 153.0 %all-gather.4.cloned.1.call-start = ((), (), s32[]{:S(2)}) async-start(), calls=%async_computation.4 | async-start | bytes 9437184 | tf_op jit(solution)/shard_map/all_gather | solution.py:55
  79.3 93.9 %copy-start.4 = (bf16[1,4096,128]{2,1,0:T(8,128)(2,1)S(1)}, bf16[1,4096,128]{2,1,0:T(8,128)(2,1)}, u32[]{:S(2)}) copy-start(bf16[1,4096,128]{2,1,0:T(8,128)(2,1)} %param.12) | copy-start | bytes 3145732
  79.3 135.5 %all-gather.6.cloned.1.call-start = ((), (), s32[]{:S(2)}) async-start(), calls=%async_computation.5 | async-start | bytes 2359296 | tf_op jit(solution)/shard_map/all_gather | solution.py:61
  167.3 5.9 %copy-start.2 = (bf16[1024,4096]{1,0:T(8,128)(2,1)S(1)}, bf16[1024,4096]{1,0:T(8,128)(2,1)}, u32[]{:S(2)}) copy-start(bf16[1024,4096]{1,0:T(8,128)(2,1)} %all-gather.4.cloned.1.call-done) | copy-start | bytes 25165828
  214.8 49.6 %copy-start.1 = (f32[64,8]{0,1:T(8,128)S(1)}, f32[64,8]{0,1:T(8,128)}, u32[]{:S(2)}) copy-start(f32[64,8]{0,1:T(8,128)} %param.10) | copy-start | bytes 6148
  247.4 45.6 %all-to-all-start.3 = ((bf16[1,64,2,4096]{3,2,0,1:T(2,128)(2,1)}), bf16[1,64,2,4096]{3,2,0,1:T(2,128)(2,1)S(1)}, u32[]{:S(2)}, u32[]{:S(2)}) async-start(bf16[1,64,2,4096]{3,2,0,1:T(2,128)(2,1)} %all_to_all.27), calls=%async_computation.3 | async-start | bytes 2097152 | tf_op jit(solution)/shard_map/all_to_all | solution.py:71
Sparse Core Ops, SparseCore 0:
  79.5 87.8 all-gather.3
  176.4 38.3 all-gather.5

commit v3 on v2

--- a/solution.py
+++ b/solution.py
@@ -30,7 +30,6 @@
     gate_matrix = gate_proj[0]
     up_matrix = up_proj[0]
     down_matrix = down_proj[0]
-    column_share = down_matrix.shape[1]
     own_start = tensor_index * row_count
     own_ids = lax.dynamic_slice_in_dim(expert_ids, own_start, row_count, 0)
     own_weights = lax.dynamic_slice_in_dim(route_weights, own_start, row_count, 0)
@@ -52,29 +51,23 @@
         "rec,rd->ecd", chosen.astype(jnp.bfloat16), restored, preferred_element_type=jnp.float32
     ).astype(jnp.bfloat16)
     recv = lax.all_to_all(send, "expert", split_axis=0, concat_axis=0, tiled=True)
+    down_all = lax.all_gather(down_matrix, "tensor", axis=0, tiled=False)
+    down_all, recv = lax.optimization_barrier((down_all, recv))
     rows = lax.all_gather(
         recv.reshape(expert_count * capacity, feature_width), "tensor", axis=0, tiled=True
     )
     gate_act = jnp.dot(rows, gate_matrix, preferred_element_type=jnp.float32)
     up_act = jnp.dot(rows, up_matrix, preferred_element_type=jnp.float32)
     hidden = (jax.nn.silu(gate_act) * up_act).astype(jnp.bfloat16)
-    hidden_all = lax.all_gather(hidden, "tensor", axis=0, tiled=False)
+    hidden_own = lax.all_to_all(
+        hidden.reshape(tensor_count, expert_count * capacity, -1),
+        "tensor", split_axis=0, concat_axis=2, tiled=True,
+    )[0]
     expert_sum = jnp.einsum(
-        "tsh,thc->sc",
-        hidden_all,
-        down_matrix.reshape(tensor_count, -1, column_share),
-        preferred_element_type=jnp.float32,
+        "sh,thc->stc", hidden_own, down_all, preferred_element_type=jnp.float32
     )
-    expert_rows = expert_sum.astype(jnp.bfloat16).reshape(
-        tensor_count, expert_count, capacity, column_share
-    )
-    returned = lax.all_to_all(
-        lax.all_to_all(expert_rows, "tensor", split_axis=0, concat_axis=3, tiled=True),
-        "expert",
-        split_axis=1,
-        concat_axis=1,
-        tiled=True,
-    )
+    expert_rows = expert_sum.astype(jnp.bfloat16).reshape(expert_count, capacity, feature_width)
+    returned = lax.all_to_all(expert_rows, "expert", split_axis=0, concat_axis=0, tiled=True)
     returned = returned.reshape(expert_count, capacity, feature_width)
     pair_weight = jnp.sum(jnp.where(hit, own_weights[..., None], 0.0), axis=1)
     mixing = jnp.where(chosen, pair_weight[..., None], 0.0)

time: 303 us -> 290 us (0.957)
  blocking collectives: 71.7 us -> 60.9 us
  starting transfers between devices: 24.9 us -> 20.5 us
    all_to_all x1, blocking collectives: 26.6 us -> 14.3 us  [on_device(): lax.all_to_all(hidden.reshape(tensor_count, expert_count * capacity, -1),...]
    all_gather x1, waiting for transfers between devices: 87.9 us -> 97.1 us  [on_device(): lax.all_gather(recv.reshape(expert_count * capacity, feature_width), 'ten...]
    all_gather x1, waiting for transfers between devices: 38.6 us -> 31.3 us  [on_device(): down_all = lax.all_gather(down_matrix, 'tensor', axis=0, tiled=False)]
    all_to_all x1, starting transfers between devices: 17 us -> 12.8 us  [on_device(): lax.all_to_all(expert_rows, 'expert', split_axis=0, concat_axis=0, tiled=...]
  transfers between devices with their start and end apart: 4 -> 4, of which waited for: 4 -> 4; matrix products, arithmetic and copies ran while one was open for 0% -> 2% of each run, Pallas kernels for 0% -> 0%
where the time goes in v3:
time: 290 us
  waiting for transfers between devices  171 us (59%)
  blocking collectives  60.9 us (21%)
  starting transfers between devices  20.5 us (7%)
  matrix products  16.2 us (6%)
  between operations  13.5 us (5%)
  local copies, waits for them, and re-layouts  5.92 us (2%)
    all_gather x1, waiting for transfers between devices, on_device(): lax.all_gather(recv.reshape(expert_count * capacity, feature_width), 'ten...  97.1 us
    all_to_all x1, blocking collectives, on_device(): lax.all_to_all(send, 'expert', split_axis=0, concat_axis=0, tiled=True)  46.5 us
    all_gather x1, waiting for transfers between devices, on_device(): down_all = lax.all_gather(down_matrix, 'tensor', axis=0, tiled=False)  31.3 us
    all_to_all x1, waiting for transfers between devices, on_device(): lax.all_to_all(expert_rows, 'expert', split_axis=0, concat_axis=0, tiled=...  28.3 us
    all_to_all x1, blocking collectives, on_device(): lax.all_to_all(hidden.reshape(tensor_count, expert_count * capacity, -1),...  14.3 us
    all_to_all x1, waiting for transfers between devices, on_device(): lax.all_to_all(attn_partial[0].reshape(tensor_count, row_count, feature_w...  13.9 us
    all_to_all x1, starting transfers between devices, on_device(): lax.all_to_all(expert_rows, 'expert', split_axis=0, concat_axis=0, tiled=...  12.8 us
    all_to_all x1, starting transfers between devices, on_device(): lax.all_to_all(attn_partial[0].reshape(tensor_count, row_count, feature_w...  7.65 us
  transfers between devices with their start and end apart: 4, of which 4 were waited for; matrix products, arithmetic and copies ran while one was open for 2% of the time, Pallas kernels for 0%

profile of v3, /device:TPU:1, one launch (start us, length us, event | category | flops | bytes accessed | tf_op | source)
XLA Modules:
  0.0 289.7 jit_solution(14666531974471024455)
XLA Ops:
  6.5 0.7 all-gather.3.cloned.1.call-update
  7.3 7.7 %all-to-all-start = ((bf16[8,8,4096]{2,1,0:T(8,128)(2,1)}), bf16[8,8,4096]{2,1,0:T(8,128)(2,1)S(1)}, u32[]{:S(2)}, u32[]{:S(2)}) async-start(bf16[8,8,4096]{2,1,0:T(8,128)(2,1)} %bitcast.47), calls=%async_computation | async-start | bytes 1048576 | tf_op jit(solution)/shard_map/all_to_all | solution.py:37
  14.9 0.0 all-gather.5.cloned.1.call-start
  15.0 0.8 constant_dynamic-slice_fusion.1
  15.7 0.1 copy.36
  15.8 0.1 convert_reduce_fusion.1
  15.9 13.9 %all-to-all-done = bf16[8,8,4096]{2,1,0:T(8,128)(2,1)S(1)} async-done(((bf16[8,8,4096]{2,1,0:T(8,128)(2,1)}), bf16[8,8,4096]{2,1,0:T(8,128)(2,1)S(1)}, u32[]{:S(2)}, u32[]{:S(2)}) %all-to-all-start) | async-done | bytes 524320 | tf_op jit(solution)/shard_map/all_to_all | solution.py:37
  29.9 0.1 convert_reduce_fusion
  29.9 0.1 multiply_reduce_fusion
  30.1 0.9 fusion.10
  31.0 0.1 copy.38
  31.1 0.1 copy.39
  31.2 1.2 convolution_convert_fusion
  32.4 1.1 copy.40
  33.5 46.5 %all_to_all.30 = bf16[64,2,4096]{2,1,0:T(2,128)(2,1)S(1)} all-to-all(bf16[64,2,4096]{2,1,0:T(2,128)(2,1)S(1)} %copy.40), channel_id=1, replica_groups=mesh['tensor'=8,'expert'=64] {'expert'}, dimensions={0} | all-to-all | bytes 2097152 | tf_op jit(solution)/shard_map/all_to_all | solution.py:53
  80.0 31.3 %all-gather.3.cloned.1.call-done = bf16[8,1024,512]{2,1,0:T(8,128)(2,1)} async-done(((bf16[1,1024,512]{2,1,0:T(8,128)(2,1)}), bf16[8,1024,512]{2,1,0:T(8,128)(2,1)}) %all-gather.3.cloned.1.call-update) | async-done | bytes 8388624 | tf_op jit(solution)/shard_map/all_gather | solution.py:54
  111.3 1.2 reshape.60
  112.6 97.1 %all-gather.5.cloned.1.call-done = bf16[1024,4096]{1,0:T(8,128)(2,1)} async-done(((bf16[128,4096]{1,0:T(8,128)(2,1)}), bf16[1024,4096]{1,0:T(8,128)(2,1)}) %all-gather.5.cloned.1.call-update) | async-done | bytes 8388624 | tf_op jit(solution)/shard_map/all_gather | solution.py:56
  209.7 5.8 %fusion.3 = f32[1024,128]{1,0:T(8,128)S(1)} fusion(bf16[1024,4096]{1,0:T(8,128)(2,1)} %all-gather.5.cloned.1.call-done, bf16[1,4096,128]{2,1,0:T(8,128)(2,1)S(1)} %copy-done), kind=kOutput, calls=%fused_computation.7 | convolution fusion | flops 1073741824 | bytes 9961472 | tf_op jit(solution)/shard_map/dot_general | solution.py:59
  215.5 2.3 fusion.1
  217.9 14.3 %all_to_all.31 = bf16[8,128,128]{2,1,0:T(8,128)(2,1)S(1)} all-to-all(bf16[8,128,128]{2,1,0:T(8,128)(2,1)S(1)} %bitcast.48), channel_id=1, replica_groups=mesh['tensor'=8,'expert'=64] {'tensor'}, dimensions={0} | all-to-all | bytes 524288 | tf_op jit(solution)/shard_map/all_to_all | solution.py:62
  232.2 0.2 copy.41
  232.4 0.1 reshape.64
  232.5 4.7 %convolution_convert_fusion.1 = bf16[128,8,512]{2,0,1:T(8,128)(2,1)S(1)} fusion(bf16[128,1024,1]{1,0,2:T(8,128)(2,1)S(1)} %reshape.64, bf16[8,1024,512]{2,1,0:T(8,128)(2,1)} %all-gather.3.cloned.1.call-done), kind=kOutput, calls=%fused_computation.3 | convolution fusion | flops 1074266112 | bytes 9699328 | tf_op jit(solution)/shard_map/sh,thc->stc/dot_general | solution.py:66
  237.2 0.6 copy.42
  237.8 1.6 reshape.62
  239.4 12.8 %all-to-all-start.3 = ((bf16[64,2,4096]{2,1,0:T(2,128)(2,1)}), bf16[64,2,4096]{2,1,0:T(2,128)(2,1)S(1)}, u32[]{:S(2)}, u32[]{:S(2)}) async-start(bf16[64,2,4096]{2,1,0:T(2,128)(2,1)} %reshape.62), calls=%async_computation.3 | async-start | bytes 2097152 | tf_op jit(solution)/shard_map/all_to_all | solution.py:70
  252.2 0.1 constant_dynamic-slice_fusion
  252.3 0.1 copy.37
  252.4 0.1 select_reduce_fusion
  252.5 28.3 %all-to-all-done.3 = bf16[64,2,4096]{2,1,0:T(2,128)(2,1)S(1)} async-done(((bf16[64,2,4096]{2,1,0:T(2,128)(2,1)}), bf16[64,2,4096]{2,1,0:T(2,128)(2,1)S(1)}, u32[]{:S(2)}, u32[]{:S(2)}) %all-to-all-start.3) | async-done | bytes 1048608 | tf_op jit(solution)/shard_map/all_to_all | solution.py:70
  280.7 2.2 fusion
  (15 shorter events, 0.1 us)
Async XLA Ops:
  6.5 203.1 %copy-start = (bf16[1,4096,128]{2,1,0:T(8,128)(2,1)S(1)}, bf16[1,4096,128]{2,1,0:T(8,128)(2,1)}, u32[]{:S(2)}) copy-start(bf16[1,4096,128]{2,1,0:T(8,128)(2,1)} %param.11) | copy-start | bytes 3145732
  6.5 104.8 %all-gather.3.cloned.1.call-start = ((), (), s32[]{:S(2)}) async-start(), calls=%async_computation.4 | async-start | bytes 9437184 | tf_op jit(solution)/shard_map/all_gather | solution.py:54
  7.3 22.6 %all-to-all-start = ((bf16[8,8,4096]{2,1,0:T(8,128)(2,1)}), bf16[8,8,4096]{2,1,0:T(8,128)(2,1)S(1)}, u32[]{:S(2)}, u32[]{:S(2)}) async-start(bf16[8,8,4096]{2,1,0:T(8,128)(2,1)} %bitcast.47), calls=%async_computation | async-start | bytes 1048576 | tf_op jit(solution)/shard_map/all_to_all | solution.py:37
  14.9 194.7 %all-gather.5.cloned.1.call-start = ((), (), s32[]{:S(2)}) async-start(), calls=%async_computation.5 | async-start | bytes 9437184 | tf_op jit(solution)/shard_map/all_gather | solution.py:56
  33.5 182.0 %copy-start.3 = (bf16[1,4096,128]{2,1,0:T(8,128)(2,1)S(1)}, bf16[1,4096,128]{2,1,0:T(8,128)(2,1)}, u32[]{:S(2)}) copy-start(bf16[1,4096,128]{2,1,0:T(8,128)(2,1)} %param.12) | copy-start | bytes 3145732
  209.7 5.9 %copy-start.2 = (bf16[1024,4096]{1,0:T(8,128)(2,1)S(1)}, bf16[1024,4096]{1,0:T(8,128)(2,1)}, u32[]{:S(2)}) copy-start(bf16[1024,4096]{1,0:T(8,128)(2,1)} %all-gather.5.cloned.1.call-done) | copy-start | bytes 25165828
  232.4 19.8 %copy-start.1 = (f32[64,8]{0,1:T(8,128)S(1)}, f32[64,8]{0,1:T(8,128)}, u32[]{:S(2)}) copy-start(f32[64,8]{0,1:T(8,128)} %param.10) | copy-start | bytes 6148
  239.4 41.4 %all-to-all-start.3 = ((bf16[64,2,4096]{2,1,0:T(2,128)(2,1)}), bf16[64,2,4096]{2,1,0:T(2,128)(2,1)S(1)}, u32[]{:S(2)}, u32[]{:S(2)}) async-start(bf16[64,2,4096]{2,1,0:T(2,128)(2,1)} %reshape.62), calls=%async_computation.3 | async-start | bytes 2097152 | tf_op jit(solution)/shard_map/all_to_all | solution.py:70
Sparse Core Ops, SparseCore 0:
  9.4 101.8 all-gather.2
  113.4 96.2 all-gather.4

commit v4 on v3

--- a/solution.py
+++ b/solution.py
@@ -51,8 +51,17 @@
         "rec,rd->ecd", chosen.astype(jnp.bfloat16), restored, preferred_element_type=jnp.float32
     ).astype(jnp.bfloat16)
     recv = lax.all_to_all(send, "expert", split_axis=0, concat_axis=0, tiled=True)
-    down_all = lax.all_gather(down_matrix, "tensor", axis=0, tiled=False)
-    down_all, recv = lax.optimization_barrier((down_all, recv))
+    pieces = [down_matrix] + [None] * (tensor_count - 1)
+    ahead = down_matrix
+    behind = down_matrix
+    for step in range(1, tensor_count // 2 + 1):
+        ahead = lax.ppermute(ahead, "tensor", [(i, (i + 1) % tensor_count) for i in range(tensor_count)])
+        pieces[tensor_count - step] = ahead
+        if step < tensor_count - step:
+            behind = lax.ppermute(behind, "tensor", [(i, (i - 1) % tensor_count) for i in range(tensor_count)])
+            pieces[step] = behind
+    pieces, recv = lax.optimization_barrier((pieces, recv))
+    down_ring = jnp.stack(pieces)
     rows = lax.all_gather(
         recv.reshape(expert_count * capacity, feature_width), "tensor", axis=0, tiled=True
     )
@@ -64,9 +73,10 @@
         "tensor", split_axis=0, concat_axis=2, tiled=True,
     )[0]
     expert_sum = jnp.einsum(
-        "sh,thc->stc", hidden_own, down_all, preferred_element_type=jnp.float32
-    )
-    expert_rows = expert_sum.astype(jnp.bfloat16).reshape(expert_count, capacity, feature_width)
+        "sh,mhc->smc", hidden_own, down_ring, preferred_element_type=jnp.float32
+    ).astype(jnp.bfloat16)
+    expert_sum = jnp.roll(expert_sum, tensor_index, axis=1)
+    expert_rows = expert_sum.reshape(expert_count, capacity, feature_width)
     returned = lax.all_to_all(expert_rows, "expert", split_axis=0, concat_axis=0, tiled=True)
     returned = returned.reshape(expert_count, capacity, feature_width)
     pair_weight = jnp.sum(jnp.where(hit, own_weights[..., None], 0.0), axis=1)

time: 290 us -> 308 us (1.062)
  blocking collectives: 60.9 us -> 0 us
  starting transfers between devices: 20.5 us -> 67.5 us
  local copies, waits for them, and re-layouts: 5.92 us -> 24 us
  waiting for transfers between devices: 171 us -> 183 us
    all_to_all x2 -> x0, blocking collectives: 60.9 us -> none  [the longest x1 46.5 us: on_device(): lax.all_to_all(send, 'expert', split_axis=0, concat_axis=0, tiled=True)]
    all_gather x1 -> x0, waiting for transfers between devices: 31.3 us -> none  [on_device(): down_all = lax.all_gather(down_matrix, 'tensor', axis=0, tiled=False)]
    ppermute x0 -> x7, starting transfers between devices: none -> 28.7 us  [the longest x4 15.3 us: on_device(): lax.ppermute(ahead, 'tensor', [(i, (i + 1) % tensor_count) for i in range...]
    ppermute x0 -> x7, waiting for transfers between devices: none -> 27.9 us  [the longest x4 23.5 us: on_device(): lax.ppermute(ahead, 'tensor', [(i, (i + 1) % tensor_count) for i in range...]
    all_to_all x0 -> x2, waiting for transfers between devices: none -> 27.5 us  [the longest x1 21.7 us: on_device(): lax.all_to_all(send, 'expert', split_axis=0, concat_axis=0, tiled=True)]
    all_to_all x0 -> x2, starting transfers between devices: none -> 20.1 us  [the longest x1 15.9 us: on_device(): lax.all_to_all(send, 'expert', split_axis=0, concat_axis=0, tiled=True)]
    unnamed x8 -> x17, local copies, waits for them, and re-layouts: 0.02 us -> 14.9 us
    all_to_all x1, waiting for transfers between devices: 13.9 us -> 7.16 us  [on_device(): lax.all_to_all(attn_partial[0].reshape(tensor_count, row_count, feature_w...]
  transfers between devices with their start and end apart: 4 -> 12, of which waited for: 4 -> 9; matrix products, arithmetic and copies ran while one was open for 2% -> 7% of each run, Pallas kernels for 0% -> 0%
where the time goes in v4:
time: 308 us; the launch traced here: 307 us
  waiting for transfers between devices  183 us (59%)
  starting transfers between devices  67.5 us (22%)
  local copies, waits for them, and re-layouts  24 us (8%)
  matrix products  16.9 us (5%)
  between operations  13.6 us (4%)
    all_gather x1, waiting for transfers between devices, on_device(): lax.all_gather(recv.reshape(expert_count * capacity, feature_width), 'ten...  92.6 us
    all_to_all x1, waiting for transfers between devices, on_device(): lax.all_to_all(expert_rows, 'expert', split_axis=0, concat_axis=0, tiled=...  28.3 us
    ppermute x4, waiting for transfers between devices, on_device(): lax.ppermute(ahead, 'tensor', [(i, (i + 1) % tensor_count) for i in range...  23.5 us
    all_to_all x1, waiting for transfers between devices, on_device(): lax.all_to_all(send, 'expert', split_axis=0, concat_axis=0, tiled=True)  21.7 us
    all_to_all x1, starting transfers between devices, on_device(): lax.all_to_all(send, 'expert', split_axis=0, concat_axis=0, tiled=True)  15.9 us
    ppermute x4, starting transfers between devices, on_device(): lax.ppermute(ahead, 'tensor', [(i, (i + 1) % tensor_count) for i in range...  15.3 us
    unnamed x17, local copies, waits for them, and re-layouts  14.9 us
    ppermute x3, starting transfers between devices, on_device(): lax.ppermute(behind, 'tensor', [(i, (i - 1) % tensor_count) for i in rang...  13.3 us
  transfers between devices with their start and end apart: 12, of which 9 were waited for; matrix products, arithmetic and copies ran while one was open for 7% of the time, Pallas kernels for 0%

profile of v4, /device:TPU:1, one launch (start us, length us, event | category | flops | bytes accessed | tf_op | source)
XLA Modules:
  0.0 307.2 jit_solution(2763109174775245242)
XLA Ops:
  6.5 4.1 %collective-permute-start.3 = (bf16[1024,512]{1,0:T(8,128)(2,1)}, bf16[1024,512]{1,0:T(8,128)(2,1)}, u32[]{:S(2)}, u32[]{:S(2)}) collective-permute-start(bf16[1024,512]{1,0:T(8,128)(2,1)} %bitcast.63), channel_id=1, source_target_pairs={{0,64},{64,128},{128,192},{192,256},{256,320},{320,384},{384,448},... | collective-permute-start | bytes 3145736 | tf_op jit(solution)/shard_map/ppermute | solution.py:58
  10.7 5.9 %all-to-all-start = ((bf16[8,8,4096]{2,1,0:T(8,128)(2,1)}), bf16[8,8,4096]{2,1,0:T(8,128)(2,1)S(1)}, u32[]{:S(2)}, u32[]{:S(2)}) async-start(bf16[8,8,4096]{2,1,0:T(8,128)(2,1)} %bitcast.67), calls=%async_computation | async-start | bytes 1048576 | tf_op jit(solution)/shard_map/all_to_all | solution.py:37
  16.6 4.6 %collective-permute-start = (bf16[1024,512]{1,0:T(8,128)(2,1)}, bf16[1024,512]{1,0:T(8,128)(2,1)}, u32[]{:S(2)}, u32[]{:S(2)}) collective-permute-start(bf16[1024,512]{1,0:T(8,128)(2,1)} %bitcast.64), channel_id=1, source_target_pairs={{0,448},{64,0},{128,64},{192,128},{256,192},{320,256},{384,320},{4... | collective-permute-start | bytes 3145736 | tf_op jit(solution)/shard_map/ppermute | solution.py:61
  22.0 8.6 %collective-permute-done.3 = bf16[1024,512]{1,0:T(8,128)(2,1)} collective-permute-done((bf16[1024,512]{1,0:T(8,128)(2,1)}, bf16[1024,512]{1,0:T(8,128)(2,1)}, u32[]{:S(2)}, u32[]{:S(2)}) %collective-permute-start.3) | collective-permute-done | bytes 1048608 | tf_op jit(solution)/shard_map/ppermute | solution.py:58
  30.6 7.4 %collective-permute-start.4 = (bf16[1024,512]{1,0:T(8,128)(2,1)}, bf16[1024,512]{1,0:T(8,128)(2,1)}, u32[]{:S(2)}, u32[]{:S(2)}) collective-permute-start(bf16[1024,512]{1,0:T(8,128)(2,1)} %collective-permute-done.3), channel_id=1, source_target_pairs={{0,64},{64,128},{128,192},{192,256},{256,320},{320,384},{384,448},... | collective-permute-start | bytes 3145736 | tf_op jit(solution)/shard_map/ppermute | solution.py:58
  38.2 7.2 %all-to-all-done = bf16[8,8,4096]{2,1,0:T(8,128)(2,1)S(1)} async-done(((bf16[8,8,4096]{2,1,0:T(8,128)(2,1)}), bf16[8,8,4096]{2,1,0:T(8,128)(2,1)S(1)}, u32[]{:S(2)}, u32[]{:S(2)}) %all-to-all-start) | async-done | bytes 524320 | tf_op jit(solution)/shard_map/all_to_all | solution.py:37
  46.6 4.3 %collective-permute-done = bf16[1024,512]{1,0:T(8,128)(2,1)} collective-permute-done((bf16[1024,512]{1,0:T(8,128)(2,1)}, bf16[1024,512]{1,0:T(8,128)(2,1)}, u32[]{:S(2)}, u32[]{:S(2)}) %collective-permute-start) | collective-permute-done | bytes 1048608 | tf_op jit(solution)/shard_map/ppermute | solution.py:61
  50.9 3.9 %collective-permute-start.1 = (bf16[1024,512]{1,0:T(8,128)(2,1)}, bf16[1024,512]{1,0:T(8,128)(2,1)}, u32[]{:S(2)}, u32[]{:S(2)}) collective-permute-start(bf16[1024,512]{1,0:T(8,128)(2,1)} %collective-permute-done), channel_id=1, source_target_pairs={{0,448},{64,0},{128,64},{192,128},{256,192},{320,256},{384,320},{4... | collective-permute-start | bytes 3145736 | tf_op jit(solution)/shard_map/ppermute | solution.py:61
  54.8 13.3 %collective-permute-done.4 = bf16[1024,512]{1,0:T(8,128)(2,1)} collective-permute-done((bf16[1024,512]{1,0:T(8,128)(2,1)}, bf16[1024,512]{1,0:T(8,128)(2,1)}, u32[]{:S(2)}, u32[]{:S(2)}) %collective-permute-start.4) | collective-permute-done | bytes 1048608 | tf_op jit(solution)/shard_map/ppermute | solution.py:58
  68.2 1.9 collective-permute-start.5
  71.3 2.1 copy.40
  73.4 15.9 %all-to-all-start.1 = ((bf16[64,2,4096]{2,1,0:T(2,128)(2,1)}), bf16[64,2,4096]{2,1,0:T(2,128)(2,1)S(1)}, u32[]{:S(2)}, u32[]{:S(2)}) async-start(bf16[64,2,4096]{2,1,0:T(2,128)(2,1)} %copy.40), calls=%async_computation.1 | async-start | bytes 2097152 | tf_op jit(solution)/shard_map/all_to_all | solution.py:53
  89.3 4.9 %collective-permute-start.2 = (bf16[1024,512]{1,0:T(8,128)(2,1)}, bf16[1024,512]{1,0:T(8,128)(2,1)}, u32[]{:S(2)}, u32[]{:S(2)}) collective-permute-start(bf16[1024,512]{1,0:T(8,128)(2,1)} %collective-permute-done.1), channel_id=1, source_target_pairs={{0,448},{64,0},{128,64},{192,128},{256,192},{320,256},{384,320},{4... | collective-permute-start | bytes 3145736 | tf_op jit(solution)/shard_map/ppermute | solution.py:61
  94.2 1.9 collective-permute-start.6
  96.1 21.7 %all-to-all-done.1 = bf16[64,2,4096]{2,1,0:T(2,128)(2,1)S(1)} async-done(((bf16[64,2,4096]{2,1,0:T(2,128)(2,1)}), bf16[64,2,4096]{2,1,0:T(2,128)(2,1)S(1)}, u32[]{:S(2)}, u32[]{:S(2)}) %all-to-all-start.1) | async-done | bytes 1048608 | tf_op jit(solution)/shard_map/all_to_all | solution.py:53
  117.8 1.6 collective-permute-done.6
  121.8 2.3 bitcast_dynamic-update-slice_fusion.6
  124.0 2.3 bitcast_dynamic-update-slice_fusion.5
  126.3 2.4 bitcast_dynamic-update-slice_fusion.4
  128.7 2.3 bitcast_dynamic-update-slice_fusion.3
  131.0 2.3 bitcast_dynamic-update-slice_fusion.2
  133.2 92.6 %all-gather.2.cloned.1.call-done = bf16[1024,4096]{1,0:T(8,128)(2,1)} async-done(((bf16[128,4096]{1,0:T(8,128)(2,1)}), bf16[1024,4096]{1,0:T(8,128)(2,1)}) %all-gather.2.cloned.1.call-update) | async-done | bytes 8388624 | tf_op jit(solution)/shard_map/all_gather | solution.py:65
  225.8 5.8 %fusion.4 = f32[1024,128]{1,0:T(8,128)S(1)} fusion(bf16[1024,4096]{1,0:T(8,128)(2,1)} %all-gather.2.cloned.1.call-done, bf16[1,4096,128]{2,1,0:T(8,128)(2,1)S(1)} %copy-done), kind=kOutput, calls=%fused_computation.18 | convolution fusion | flops 1073741824 | bytes 9961472 | tf_op jit(solution)/shard_map/dot_general | solution.py:68
  231.7 3.0 fusion.1
  234.7 4.2 %all-to-all-start.2 = ((bf16[8,128,128]{2,1,0:T(8,128)(2,1)}), bf16[8,128,128]{2,1,0:T(8,128)(2,1)S(1)}, u32[]{:S(2)}, u32[]{:S(2)}) async-start(bf16[8,128,128]{2,1,0:T(8,128)(2,1)} %bitcast.8), calls=%async_computation.2 | async-start | bytes 524288 | tf_op jit(solution)/shard_map/all_to_all | solution.py:71
  238.9 2.3 bitcast_dynamic-update-slice_fusion.1
  241.2 2.3 bitcast_dynamic-update-slice_fusion
  243.5 5.8 %all-to-all-done.2 = bf16[8,128,128]{2,1,0:T(8,128)(2,1)S(1)} async-done(((bf16[8,128,128]{2,1,0:T(8,128)(2,1)}), bf16[8,128,128]{2,1,0:T(8,128)(2,1)S(1)}, u32[]{:S(2)}, u32[]{:S(2)}) %all-to-all-start.2) | async-done | bytes 262176 | tf_op jit(solution)/shard_map/all_to_all | solution.py:71
  249.6 4.7 %convolution_convert_fusion.1 = bf16[128,8,512]{2,0,1:T(8,128)(2,1)S(1)} fusion(bf16[128,1024,1]{1,0,2:T(8,128)(2,1)S(1)} %reshape.64, bf16[8,1024,512]{2,1,0:T(8,128)(2,1)} %bitcast_dynamic-update-slice_fusion), kind=kOutput, calls=%fused_computation.5 | convolution fusion | flops 1074266112 | bytes 9699328 | tf_op jit(solution)/shard_map/sh,mhc->smc/dot_general | solution.py:75
  256.8 12.8 %all-to-all-start.3 = ((bf16[64,2,4096]{2,1,0:T(2,128)(2,1)}), bf16[64,2,4096]{2,1,0:T(2,128)(2,1)S(1)}, u32[]{:S(2)}, u32[]{:S(2)}) async-start(bf16[64,2,4096]{2,1,0:T(2,128)(2,1)} %reshape.62), calls=%async_computation.3 | async-start | bytes 2097152 | tf_op jit(solution)/shard_map/all_to_all | solution.py:80
  269.9 28.3 %all-to-all-done.3 = bf16[64,2,4096]{2,1,0:T(2,128)(2,1)S(1)} async-done(((bf16[64,2,4096]{2,1,0:T(2,128)(2,1)}), bf16[64,2,4096]{2,1,0:T(2,128)(2,1)S(1)}, u32[]{:S(2)}, u32[]{:S(2)}) %all-to-all-start.3) | async-done | bytes 1048608 | tf_op jit(solution)/shard_map/all_to_all | solution.py:80
  298.2 2.2 fusion
  (39 shorter events, 8.9 us)
Async XLA Ops:
  6.5 219.3 %copy-start = (bf16[1,4096,128]{2,1,0:T(8,128)(2,1)S(1)}, bf16[1,4096,128]{2,1,0:T(8,128)(2,1)}, u32[]{:S(2)}) copy-start(bf16[1,4096,128]{2,1,0:T(8,128)(2,1)} %param.11) | copy-start | bytes 3145732
  6.5 114.1 %copy-start.1 = (bf16[1,1024,512]{2,1,0:T(8,128)(2,1)S(1)}, bf16[1,1024,512]{2,1,0:T(8,128)(2,1)}, u32[]{:S(2)}) copy-start(bf16[1,1024,512]{2,1,0:T(8,128)(2,1)} %param.13) | copy-start | bytes 3145732
  6.5 24.1 %collective-permute-start.3 = (bf16[1024,512]{1,0:T(8,128)(2,1)}, bf16[1024,512]{1,0:T(8,128)(2,1)}, u32[]{:S(2)}, u32[]{:S(2)}) collective-permute-start(bf16[1024,512]{1,0:T(8,128)(2,1)} %bitcast.63), channel_id=1, source_target_pairs={{0,64},{64,128},{128,192},{192,256},{256,320},{320,384},{384,448},... | collective-permute-start | bytes 3145736 | tf_op jit(solution)/shard_map/ppermute | solution.py:58
  10.7 34.6 %all-to-all-start = ((bf16[8,8,4096]{2,1,0:T(8,128)(2,1)}), bf16[8,8,4096]{2,1,0:T(8,128)(2,1)S(1)}, u32[]{:S(2)}, u32[]{:S(2)}) async-start(bf16[8,8,4096]{2,1,0:T(8,128)(2,1)} %bitcast.67), calls=%async_computation | async-start | bytes 1048576 | tf_op jit(solution)/shard_map/all_to_all | solution.py:37
  16.6 34.3 %collective-permute-start = (bf16[1024,512]{1,0:T(8,128)(2,1)}, bf16[1024,512]{1,0:T(8,128)(2,1)}, u32[]{:S(2)}, u32[]{:S(2)}) collective-permute-start(bf16[1024,512]{1,0:T(8,128)(2,1)} %bitcast.64), channel_id=1, source_target_pairs={{0,448},{64,0},{128,64},{192,128},{256,192},{320,256},{384,320},{4... | collective-permute-start | bytes 3145736 | tf_op jit(solution)/shard_map/ppermute | solution.py:61
  30.6 37.5 %collective-permute-start.4 = (bf16[1024,512]{1,0:T(8,128)(2,1)}, bf16[1024,512]{1,0:T(8,128)(2,1)}, u32[]{:S(2)}, u32[]{:S(2)}) collective-permute-start(bf16[1024,512]{1,0:T(8,128)(2,1)} %collective-permute-done.3), channel_id=1, source_target_pairs={{0,64},{64,128},{128,192},{192,256},{256,320},{320,384},{384,448},... | collective-permute-start | bytes 3145736 | tf_op jit(solution)/shard_map/ppermute | solution.py:58
  50.9 38.4 %collective-permute-start.1 = (bf16[1024,512]{1,0:T(8,128)(2,1)}, bf16[1024,512]{1,0:T(8,128)(2,1)}, u32[]{:S(2)}, u32[]{:S(2)}) collective-permute-start(bf16[1024,512]{1,0:T(8,128)(2,1)} %collective-permute-done), channel_id=1, source_target_pairs={{0,448},{64,0},{128,64},{192,128},{256,192},{320,256},{384,320},{4... | collective-permute-start | bytes 3145736 | tf_op jit(solution)/shard_map/ppermute | solution.py:61
  68.2 26.0 %collective-permute-start.5 = (bf16[1024,512]{1,0:T(8,128)(2,1)}, bf16[1024,512]{1,0:T(8,128)(2,1)}, u32[]{:S(2)}, u32[]{:S(2)}) collective-permute-start(bf16[1024,512]{1,0:T(8,128)(2,1)} %collective-permute-done.4), channel_id=1, source_target_pairs={{0,64},{64,128},{128,192},{192,256},{256,320},{320,384},{384,448},... | collective-permute-start | bytes 3145736 | tf_op jit(solution)/shard_map/ppermute | solution.py:58
  73.4 44.4 %all-to-all-start.1 = ((bf16[64,2,4096]{2,1,0:T(2,128)(2,1)}), bf16[64,2,4096]{2,1,0:T(2,128)(2,1)S(1)}, u32[]{:S(2)}, u32[]{:S(2)}) async-start(bf16[64,2,4096]{2,1,0:T(2,128)(2,1)} %copy.40), calls=%async_computation.1 | async-start | bytes 2097152 | tf_op jit(solution)/shard_map/all_to_all | solution.py:53
  89.3 136.5 %all-gather.2.cloned.1.call-start = ((), (), s32[]{:S(2)}) async-start(), calls=%async_computation.4 | async-start | bytes 9437184 | tf_op jit(solution)/shard_map/all_gather | solution.py:65
  89.3 28.5 %collective-permute-start.2 = (bf16[1024,512]{1,0:T(8,128)(2,1)}, bf16[1024,512]{1,0:T(8,128)(2,1)}, u32[]{:S(2)}, u32[]{:S(2)}) collective-permute-start(bf16[1024,512]{1,0:T(8,128)(2,1)} %collective-permute-done.1), channel_id=1, source_target_pairs={{0,448},{64,0},{128,64},{192,128},{256,192},{320,256},{384,320},{4... | collective-permute-start | bytes 3145736 | tf_op jit(solution)/shard_map/ppermute | solution.py:61
  94.2 25.2 %collective-permute-start.6 = (bf16[1024,512]{1,0:T(8,128)(2,1)}, bf16[1024,512]{1,0:T(8,128)(2,1)}, u32[]{:S(2)}, u32[]{:S(2)}) collective-permute-start(bf16[1024,512]{1,0:T(8,128)(2,1)} %collective-permute-done.5), channel_id=1, source_target_pairs={{0,64},{64,128},{128,192},{192,256},{256,320},{320,384},{384,448},... | collective-permute-start | bytes 3145736 | tf_op jit(solution)/shard_map/ppermute | solution.py:58
  126.3 105.4 %copy-start.4 = (bf16[1,4096,128]{2,1,0:T(8,128)(2,1)S(1)}, bf16[1,4096,128]{2,1,0:T(8,128)(2,1)}, u32[]{:S(2)}) copy-start(bf16[1,4096,128]{2,1,0:T(8,128)(2,1)} %param.12) | copy-start | bytes 3145732
  225.8 5.9 %copy-start.3 = (bf16[1024,4096]{1,0:T(8,128)(2,1)S(1)}, bf16[1024,4096]{1,0:T(8,128)(2,1)}, u32[]{:S(2)}) copy-start(bf16[1024,4096]{1,0:T(8,128)(2,1)} %all-gather.2.cloned.1.call-done) | copy-start | bytes 25165828
  234.7 14.5 %all-to-all-start.2 = ((bf16[8,128,128]{2,1,0:T(8,128)(2,1)}), bf16[8,128,128]{2,1,0:T(8,128)(2,1)S(1)}, u32[]{:S(2)}, u32[]{:S(2)}) async-start(bf16[8,128,128]{2,1,0:T(8,128)(2,1)} %bitcast.8), calls=%async_computation.2 | async-start | bytes 524288 | tf_op jit(solution)/shard_map/all_to_all | solution.py:71
  249.6 20.1 %copy-start.2 = (f32[64,8]{0,1:T(8,128)S(1)}, f32[64,8]{0,1:T(8,128)}, u32[]{:S(2)}) copy-start(f32[64,8]{0,1:T(8,128)} %param.10) | copy-start | bytes 6148
  256.8 41.4 %all-to-all-start.3 = ((bf16[64,2,4096]{2,1,0:T(2,128)(2,1)}), bf16[64,2,4096]{2,1,0:T(2,128)(2,1)S(1)}, u32[]{:S(2)}, u32[]{:S(2)}) async-start(bf16[64,2,4096]{2,1,0:T(2,128)(2,1)} %reshape.62), calls=%async_computation.3 | async-start | bytes 2097152 | tf_op jit(solution)/shard_map/all_to_all | solution.py:80
Sparse Core Ops, SparseCore 0:
  120.7 105.0 all-gather.1

commit v5 on v3

--- a/solution.py
+++ b/solution.py
@@ -52,13 +52,22 @@
     ).astype(jnp.bfloat16)
     recv = lax.all_to_all(send, "expert", split_axis=0, concat_axis=0, tiled=True)
     down_all = lax.all_gather(down_matrix, "tensor", axis=0, tiled=False)
-    down_all, recv = lax.optimization_barrier((down_all, recv))
-    rows = lax.all_gather(
-        recv.reshape(expert_count * capacity, feature_width), "tensor", axis=0, tiled=True
-    )
-    gate_act = jnp.dot(rows, gate_matrix, preferred_element_type=jnp.float32)
-    up_act = jnp.dot(rows, up_matrix, preferred_element_type=jnp.float32)
-    hidden = (jax.nn.silu(gate_act) * up_act).astype(jnp.bfloat16)
+    def front(piece):
+        gate_act = jnp.dot(piece, gate_matrix, preferred_element_type=jnp.float32)
+        up_act = jnp.dot(piece, up_matrix, preferred_element_type=jnp.float32)
+        return (jax.nn.silu(gate_act) * up_act).astype(jnp.bfloat16)
+
+    own_rows = recv.reshape(expert_count * capacity, feature_width)
+    hidden_parts = [front(own_rows)] + [None] * (tensor_count - 1)
+    ahead = own_rows
+    behind = own_rows
+    for step in range(1, tensor_count // 2 + 1):
+        ahead = lax.ppermute(ahead, "tensor", [(i, (i + 1) % tensor_count) for i in range(tensor_count)])
+        hidden_parts[tensor_count - step] = front(ahead)
+        if step < tensor_count - step:
+            behind = lax.ppermute(behind, "tensor", [(i, (i - 1) % tensor_count) for i in range(tensor_count)])
+            hidden_parts[step] = front(behind)
+    hidden = jnp.roll(jnp.stack(hidden_parts), tensor_index, axis=0)
     hidden_own = lax.all_to_all(
         hidden.reshape(tensor_count, expert_count * capacity, -1),
         "tensor", split_axis=0, concat_axis=2, tiled=True,

time: 290 us -> 288 us (level)
  waiting for transfers between devices: 171 us -> 142 us
  starting transfers between devices: 20.5 us -> 43.8 us
  matrix products: 16.2 us -> 22.5 us
    ppermute x0 -> x7, waiting for transfers between devices: none -> 98.6 us  [the longest x4 98.6 us: on_device(): lax.ppermute(ahead, 'tensor', [(i, (i + 1) % tensor_count) for i in range...]
    all_gather x1 -> x0, waiting for transfers between devices: 97.1 us -> none  [on_device(): lax.all_gather(recv.reshape(expert_count * capacity, feature_width), 'ten...]
    all_gather x1, waiting for transfers between devices: 31.3 us -> 0.02 us  [on_device(): down_all = lax.all_gather(down_matrix, 'tensor', axis=0, tiled=False)]
    ppermute x0 -> x7, starting transfers between devices: none -> 21.4 us  [the longest x3 13.1 us: on_device(): lax.ppermute(behind, 'tensor', [(i, (i - 1) % tensor_count) for i in rang...]
    dot_general x2 -> x16, matrix products: 8.18 us -> 14.4 us  [the longest x8 7.27 us: front(): up_act = jnp.dot(piece, up_matrix, preferred_element_type=jnp.float32)]
  transfers between devices with their start and end apart: 4 -> 10, of which waited for: 4 -> 6; matrix products, arithmetic and copies ran while one was open for 2% -> 7% of each run, Pallas kernels for 0% -> 0%
where the time goes in v5:
time: 288 us; the launch traced here: 287 us
  waiting for transfers between devices  142 us (49%)
  blocking collectives  58.3 us (20%)
  starting transfers between devices  43.8 us (15%)
  matrix products  22.5 us (8%)
  between operations  13.7 us (5%)
  local copies, waits for them, and re-layouts  6.13 us (2%)
    ppermute x4, waiting for transfers between devices, on_device(): lax.ppermute(ahead, 'tensor', [(i, (i + 1) % tensor_count) for i in range...  98.6 us
    all_to_all x1, blocking collectives, on_device(): lax.all_to_all(send, 'expert', split_axis=0, concat_axis=0, tiled=True)  46.5 us
    all_to_all x1, waiting for transfers between devices, on_device(): lax.all_to_all(expert_rows, 'expert', split_axis=0, concat_axis=0, tiled=...  28.3 us
    all_to_all x1, starting transfers between devices, on_device(): lax.all_to_all(expert_rows, 'expert', split_axis=0, concat_axis=0, tiled=...  14.8 us
    all_to_all x1, waiting for transfers between devices, on_device(): lax.all_to_all(attn_partial[0].reshape(tensor_count, row_count, feature_w...  14 us
    ppermute x3, starting transfers between devices, on_device(): lax.ppermute(behind, 'tensor', [(i, (i - 1) % tensor_count) for i in rang...  13.1 us
    all_to_all x1, blocking collectives, on_device(): lax.all_to_all(hidden.reshape(tensor_count, expert_count * capacity, -1),...  11.8 us
    ppermute x4, starting transfers between devices, on_device(): lax.ppermute(ahead, 'tensor', [(i, (i + 1) % tensor_count) for i in range...  8.26 us
  transfers between devices with their start and end apart: 10, of which 6 were waited for; matrix products, arithmetic and copies ran while one was open for 7% of the time, Pallas kernels for 0%

profile of v5, /device:TPU:1, one launch (start us, length us, event | category | flops | bytes accessed | tf_op | source)
XLA Modules:
  0.0 287.4 jit_solution(4507087296770239593)
XLA Ops:
  6.5 0.7 all-gather.2.cloned.1.call-update
  7.3 7.7 %all-to-all-start = ((bf16[8,8,4096]{2,1,0:T(8,128)(2,1)}), bf16[8,8,4096]{2,1,0:T(8,128)(2,1)S(1)}, u32[]{:S(2)}, u32[]{:S(2)}) async-start(bf16[8,8,4096]{2,1,0:T(8,128)(2,1)} %bitcast.129), calls=%async_computation | async-start | bytes 1048576 | tf_op jit(solution)/shard_map/all_to_all | solution.py:37
  14.9 0.8 constant_dynamic-slice_fusion.2
  15.9 14.0 %all-to-all-done = bf16[8,8,4096]{2,1,0:T(8,128)(2,1)S(1)} async-done(((bf16[8,8,4096]{2,1,0:T(8,128)(2,1)}), bf16[8,8,4096]{2,1,0:T(8,128)(2,1)S(1)}, u32[]{:S(2)}, u32[]{:S(2)}) %all-to-all-start) | async-done | bytes 524320 | tf_op jit(solution)/shard_map/all_to_all | solution.py:37
  30.1 0.9 fusion.39
  31.2 1.2 convolution_convert_fusion
  32.4 1.1 copy.43
  33.5 46.5 %all_to_all.30 = bf16[64,2,4096]{2,1,0:T(2,128)(2,1)} all-to-all(bf16[64,2,4096]{2,1,0:T(2,128)(2,1)S(1)} %copy.43), channel_id=1, replica_groups=mesh['tensor'=8,'expert'=64] {'expert'}, dimensions={0} | all-to-all | bytes 2097152 | tf_op jit(solution)/shard_map/all_to_all | solution.py:53
  80.0 1.5 reshape.57
  81.5 2.5 collective-permute-start.3
  84.0 4.0 %collective-permute-start = (bf16[128,4096]{1,0:T(8,128)(2,1)S(1)}, bf16[128,4096]{1,0:T(8,128)(2,1)}, u32[]{:S(2)}, u32[]{:S(2)}) collective-permute-start(bf16[128,4096]{1,0:T(8,128)(2,1)S(1)} %reshape.57), channel_id=1, source_target_pairs={{0,448},{64,0},{128,64},{192,128},{256,192},{320,256},{384,320},{4... | collective-permute-start | bytes 3145736 | tf_op jit(solution)/shard_map/ppermute | solution.py:68
  88.0 44.3 %collective-permute-done.3 = bf16[128,4096]{1,0:T(8,128)(2,1)} collective-permute-done((bf16[128,4096]{1,0:T(8,128)(2,1)S(1)}, bf16[128,4096]{1,0:T(8,128)(2,1)}, u32[]{:S(2)}, u32[]{:S(2)}) %collective-permute-start.3) | collective-permute-done | bytes 1048608 | tf_op jit(solution)/shard_map/ppermute | solution.py:65
  132.3 1.9 collective-permute-start.4
  134.7 4.6 %collective-permute-start.1 = (bf16[128,4096]{1,0:T(8,128)(2,1)}, bf16[128,4096]{1,0:T(8,128)(2,1)S(1)}, u32[]{:S(2)}, u32[]{:S(2)}) collective-permute-start(bf16[128,4096]{1,0:T(8,128)(2,1)} %collective-permute-done), channel_id=1, source_target_pairs={{0,448},{64,0},{128,64},{192,128},{256,192},{320,256},{384,320},{4... | collective-permute-start | bytes 3145736 | tf_op jit(solution)/shard_map/ppermute | solution.py:68
  139.7 1.6 fusion.30
  141.4 18.3 %collective-permute-done.4 = bf16[128,4096]{1,0:T(8,128)(2,1)} collective-permute-done((bf16[128,4096]{1,0:T(8,128)(2,1)}, bf16[128,4096]{1,0:T(8,128)(2,1)}, u32[]{:S(2)}, u32[]{:S(2)}) %collective-permute-start.4) | collective-permute-done | bytes 1048608 | tf_op jit(solution)/shard_map/ppermute | solution.py:65
  159.6 1.9 collective-permute-start.5
  161.6 1.6 fusion.18
  163.2 1.7 constant_dynamic-update-slice_fusion.14
  164.9 4.6 %collective-permute-start.2 = (bf16[128,4096]{1,0:T(8,128)(2,1)S(1)}, bf16[128,4096]{1,0:T(8,128)(2,1)S(1)}, u32[]{:S(2)}, u32[]{:S(2)}) collective-permute-start(bf16[128,4096]{1,0:T(8,128)(2,1)S(1)} %collective-permute-done.1), channel_id=1, source_target_pairs={{0,448},{64,0},{128,64},{192,128},{256,192},{320,256},{384,320},{4... | collective-permute-start | bytes 3145736 | tf_op jit(solution)/shard_map/ppermute | solution.py:68
  170.4 15.6 %collective-permute-done.5 = bf16[128,4096]{1,0:T(8,128)(2,1)S(1)} collective-permute-done((bf16[128,4096]{1,0:T(8,128)(2,1)}, bf16[128,4096]{1,0:T(8,128)(2,1)S(1)}, u32[]{:S(2)}, u32[]{:S(2)}) %collective-permute-start.5) | collective-permute-done | bytes 1048608 | tf_op jit(solution)/shard_map/ppermute | solution.py:65
  186.0 1.9 collective-permute-start.6
  187.9 1.6 fusion.20
  190.9 20.4 %collective-permute-done.6 = bf16[128,4096]{1,0:T(8,128)(2,1)S(1)} collective-permute-done((bf16[128,4096]{1,0:T(8,128)(2,1)S(1)}, bf16[128,4096]{1,0:T(8,128)(2,1)S(1)}, u32[]{:S(2)}, u32[]{:S(2)}) %collective-permute-start.6) | collective-permute-done | bytes 1048608 | tf_op jit(solution)/shard_map/ppermute | solution.py:65
  212.7 1.7 constant_dynamic-update-slice_fusion.9
  214.3 1.7 constant_dynamic-update-slice_fusion.8
  216.2 11.8 %all_to_all.31 = bf16[8,128,128]{2,1,0:T(8,128)(2,1)S(1)} all-to-all(bf16[8,128,128]{2,1,0:T(8,128)(2,1)S(1)} %constant_dynamic-slice_fusion), channel_id=1, replica_groups=mesh['tensor'=8,'expert'=64] {'tensor'}, dimensions={0} | all-to-all | bytes 524288 | tf_op jit(solution)/shard_map/all_to_all | solution.py:71
  228.2 4.7 %convolution_convert_fusion.1 = bf16[128,8,512]{2,0,1:T(8,128)(2,1)S(1)} fusion(bf16[128,1024,1]{0,1,2:T(8,128)(2,1)S(1)} %bitcast.127, bf16[8,1024,512]{2,1,0:T(8,128)(2,1)} %all-gather.2.cloned.1.call-done), kind=kOutput, calls=%fused_computation.3 | convolution fusion | flops 1074266112 | bytes 9699328 | tf_op jit(solution)/shard_map/sh,thc->stc/dot_general | solution.py:75
  233.5 1.6 reshape.58
  235.0 14.8 %all-to-all-start.3 = ((bf16[64,2,4096]{2,1,0:T(2,128)(2,1)}), bf16[64,2,4096]{2,1,0:T(2,128)(2,1)S(1)}, u32[]{:S(2)}, u32[]{:S(2)}) async-start(bf16[64,2,4096]{2,1,0:T(2,128)(2,1)} %reshape.58), calls=%async_computation.3 | async-start | bytes 2097152 | tf_op jit(solution)/shard_map/all_to_all | solution.py:79
  250.1 28.3 %all-to-all-done.3 = bf16[64,2,4096]{2,1,0:T(2,128)(2,1)S(1)} async-done(((bf16[64,2,4096]{2,1,0:T(2,128)(2,1)}), bf16[64,2,4096]{2,1,0:T(2,128)(2,1)S(1)}, u32[]{:S(2)}, u32[]{:S(2)}) %all-to-all-start.3) | async-done | bytes 1048608 | tf_op jit(solution)/shard_map/all_to_all | solution.py:79
  278.3 2.2 fusion
  (46 shorter events, 6.2 us)
Async XLA Ops:
  6.5 132.7 %copy-start = (bf16[1,4096,128]{2,1,0:T(8,128)(2,1)S(1)}, bf16[1,4096,128]{2,1,0:T(8,128)(2,1)}, u32[]{:S(2)}) copy-start(bf16[1,4096,128]{2,1,0:T(8,128)(2,1)} %param.12) | copy-start | bytes 3145732
  6.5 127.7 %copy-start.1 = (bf16[1,4096,128]{2,1,0:T(8,128)(2,1)S(1)}, bf16[1,4096,128]{2,1,0:T(8,128)(2,1)}, u32[]{:S(2)}) copy-start(bf16[1,4096,128]{2,1,0:T(8,128)(2,1)} %param.11) | copy-start | bytes 3145732
  6.5 221.7 %all-gather.2.cloned.1.call-start = ((), (), s32[]{:S(2)}) async-start(), calls=%async_computation.4 | async-start | bytes 9437184 | tf_op jit(solution)/shard_map/all_gather | solution.py:54
  7.3 22.6 %all-to-all-start = ((bf16[8,8,4096]{2,1,0:T(8,128)(2,1)}), bf16[8,8,4096]{2,1,0:T(8,128)(2,1)S(1)}, u32[]{:S(2)}, u32[]{:S(2)}) async-start(bf16[8,8,4096]{2,1,0:T(8,128)(2,1)} %bitcast.129), calls=%async_computation | async-start | bytes 1048576 | tf_op jit(solution)/shard_map/all_to_all | solution.py:37
  81.5 50.8 %collective-permute-start.3 = (bf16[128,4096]{1,0:T(8,128)(2,1)S(1)}, bf16[128,4096]{1,0:T(8,128)(2,1)}, u32[]{:S(2)}, u32[]{:S(2)}) collective-permute-start(bf16[128,4096]{1,0:T(8,128)(2,1)S(1)} %reshape.57), channel_id=1, source_target_pairs={{0,64},{64,128},{128,192},{192,256},{256,320},{320,384},{384,448},... | collective-permute-start | bytes 3145736 | tf_op jit(solution)/shard_map/ppermute | solution.py:65
  84.0 50.7 %collective-permute-start = (bf16[128,4096]{1,0:T(8,128)(2,1)S(1)}, bf16[128,4096]{1,0:T(8,128)(2,1)}, u32[]{:S(2)}, u32[]{:S(2)}) collective-permute-start(bf16[128,4096]{1,0:T(8,128)(2,1)S(1)} %reshape.57), channel_id=1, source_target_pairs={{0,448},{64,0},{128,64},{192,128},{256,192},{320,256},{384,320},{4... | collective-permute-start | bytes 3145736 | tf_op jit(solution)/shard_map/ppermute | solution.py:68
  132.3 27.3 %collective-permute-start.4 = (bf16[128,4096]{1,0:T(8,128)(2,1)}, bf16[128,4096]{1,0:T(8,128)(2,1)}, u32[]{:S(2)}, u32[]{:S(2)}) collective-permute-start(bf16[128,4096]{1,0:T(8,128)(2,1)} %collective-permute-done.3), channel_id=1, source_target_pairs={{0,64},{64,128},{128,192},{192,256},{256,320},{320,384},{384,448},... | collective-permute-start | bytes 3145736 | tf_op jit(solution)/shard_map/ppermute | solution.py:65
  134.7 30.2 %collective-permute-start.1 = (bf16[128,4096]{1,0:T(8,128)(2,1)}, bf16[128,4096]{1,0:T(8,128)(2,1)S(1)}, u32[]{:S(2)}, u32[]{:S(2)}) collective-permute-start(bf16[128,4096]{1,0:T(8,128)(2,1)} %collective-permute-done), channel_id=1, source_target_pairs={{0,448},{64,0},{128,64},{192,128},{256,192},{320,256},{384,320},{4... | collective-permute-start | bytes 3145736 | tf_op jit(solution)/shard_map/ppermute | solution.py:68
  159.6 26.4 %collective-permute-start.5 = (bf16[128,4096]{1,0:T(8,128)(2,1)}, bf16[128,4096]{1,0:T(8,128)(2,1)S(1)}, u32[]{:S(2)}, u32[]{:S(2)}) collective-permute-start(bf16[128,4096]{1,0:T(8,128)(2,1)} %collective-permute-done.4), channel_id=1, source_target_pairs={{0,64},{64,128},{128,192},{192,256},{256,320},{320,384},{384,448},... | collective-permute-start | bytes 3145736 | tf_op jit(solution)/shard_map/ppermute | solution.py:65
  164.9 25.1 %collective-permute-start.2 = (bf16[128,4096]{1,0:T(8,128)(2,1)S(1)}, bf16[128,4096]{1,0:T(8,128)(2,1)S(1)}, u32[]{:S(2)}, u32[]{:S(2)}) collective-permute-start(bf16[128,4096]{1,0:T(8,128)(2,1)S(1)} %collective-permute-done.1), channel_id=1, source_target_pairs={{0,448},{64,0},{128,64},{192,128},{256,192},{320,256},{384,320},{4... | collective-permute-start | bytes 3145736 | tf_op jit(solution)/shard_map/ppermute | solution.py:68
  186.0 25.3 %collective-permute-start.6 = (bf16[128,4096]{1,0:T(8,128)(2,1)S(1)}, bf16[128,4096]{1,0:T(8,128)(2,1)S(1)}, u32[]{:S(2)}, u32[]{:S(2)}) collective-permute-start(bf16[128,4096]{1,0:T(8,128)(2,1)S(1)} %collective-permute-done.5), channel_id=1, source_target_pairs={{0,64},{64,128},{128,192},{192,256},{256,320},{320,384},{384,448},... | collective-permute-start | bytes 3145736 | tf_op jit(solution)/shard_map/ppermute | solution.py:65
  228.0 21.8 %copy-start.2 = (f32[64,8]{0,1:T(8,128)S(1)}, f32[64,8]{0,1:T(8,128)}, u32[]{:S(2)}) copy-start(f32[64,8]{0,1:T(8,128)} %param.10) | copy-start | bytes 6148
  235.0 43.3 %all-to-all-start.3 = ((bf16[64,2,4096]{2,1,0:T(2,128)(2,1)}), bf16[64,2,4096]{2,1,0:T(2,128)(2,1)S(1)}, u32[]{:S(2)}, u32[]{:S(2)}) async-start(bf16[64,2,4096]{2,1,0:T(2,128)(2,1)} %reshape.58), calls=%async_computation.3 | async-start | bytes 2097152 | tf_op jit(solution)/shard_map/all_to_all | solution.py:79
Sparse Core Ops, SparseCore 0:
  9.4 124.3 all-gather.1

commit v6 on v5

--- a/solution.py
+++ b/solution.py
@@ -57,16 +57,24 @@
         up_act = jnp.dot(piece, up_matrix, preferred_element_type=jnp.float32)
         return (jax.nn.silu(gate_act) * up_act).astype(jnp.bfloat16)
 
+    down_all, recv = lax.optimization_barrier((down_all, recv))
     own_rows = recv.reshape(expert_count * capacity, feature_width)
     hidden_parts = [front(own_rows)] + [None] * (tensor_count - 1)
     ahead = own_rows
     behind = own_rows
+    forward = [(i, (i + 1) % tensor_count) for i in range(tensor_count)]
+    backward = [(i, (i - 1) % tensor_count) for i in range(tensor_count)]
+    half = own_rows.shape[0] // 2
     for step in range(1, tensor_count // 2 + 1):
-        ahead = lax.ppermute(ahead, "tensor", [(i, (i + 1) % tensor_count) for i in range(tensor_count)])
-        hidden_parts[tensor_count - step] = front(ahead)
         if step < tensor_count - step:
-            behind = lax.ppermute(behind, "tensor", [(i, (i - 1) % tensor_count) for i in range(tensor_count)])
+            ahead = lax.ppermute(ahead, "tensor", forward)
+            hidden_parts[tensor_count - step] = front(ahead)
+            behind = lax.ppermute(behind, "tensor", backward)
             hidden_parts[step] = front(behind)
+        else:
+            first = lax.ppermute(ahead[:half], "tensor", forward)
+            second = lax.ppermute(behind[half:], "tensor", backward)
+            hidden_parts[step] = jnp.concatenate([front(first), front(second)], axis=0)
     hidden = jnp.roll(jnp.stack(hidden_parts), tensor_index, axis=0)
     hidden_own = lax.all_to_all(
         hidden.reshape(tensor_count, expert_count * capacity, -1),

time: 288 us -> 289 us (level)
  starting transfers between devices: 43.8 us -> 52.3 us
  waiting for transfers between devices: 142 us -> 134 us
    ppermute x7 -> x8, waiting for transfers between devices: 98.6 us -> 59.5 us  [the longest x3 50.5 us: on_device(): behind = lax.ppermute(behind, 'tensor', backward)]
    all_gather x1, waiting for transfers between devices: 0.02 us -> 31.3 us  [on_device(): down_all = lax.all_gather(down_matrix, 'tensor', axis=0, tiled=False)]
    ppermute x7 -> x8, starting transfers between devices: 21.4 us -> 25.7 us  [the longest x3 12.2 us: on_device(): behind = lax.ppermute(behind, 'tensor', backward)]
    all_to_all x1, starting transfers between devices: 14.8 us -> 19 us  [on_device(): lax.all_to_all(expert_rows, 'expert', split_axis=0, concat_axis=0, tiled=...]
    dot_general x8 -> x9, matrix products: 7.14 us -> 6.13 us  [front(): gate_act = jnp.dot(piece, gate_matrix, preferred_element_type=jnp.float32)]
    dot_general x8 -> x9, matrix products: 7.27 us -> 6.27 us  [front(): up_act = jnp.dot(piece, up_matrix, preferred_element_type=jnp.float32)]
  transfers between devices with their start and end apart: 10 -> 11, of which waited for: 6 -> 8; matrix products, arithmetic and copies ran while one was open for 7% -> 5% of each run, Pallas kernels for 0% -> 0%
where the time goes in v6:
time: 289 us
  waiting for transfers between devices  134 us (46%)
  blocking collectives  60.7 us (21%)
  starting transfers between devices  52.3 us (18%)
  matrix products  20.5 us (7%)
  between operations  13.7 us (5%)
  local copies, waits for them, and re-layouts  6.19 us (2%)
    ppermute x3, waiting for transfers between devices, on_device(): behind = lax.ppermute(behind, 'tensor', backward)  50.5 us
    all_to_all x1, blocking collectives, on_device(): lax.all_to_all(send, 'expert', split_axis=0, concat_axis=0, tiled=True)  46.5 us
    all_gather x1, waiting for transfers between devices, on_device(): down_all = lax.all_gather(down_matrix, 'tensor', axis=0, tiled=False)  31.3 us
    all_to_all x1, waiting for transfers between devices, on_device(): lax.all_to_all(expert_rows, 'expert', split_axis=0, concat_axis=0, tiled=...  28.3 us
    all_to_all x1, starting transfers between devices, on_device(): lax.all_to_all(expert_rows, 'expert', split_axis=0, concat_axis=0, tiled=...  19 us
    all_to_all x1, blocking collectives, on_device(): lax.all_to_all(hidden.reshape(tensor_count, expert_count * capacity, -1),...  14.2 us
    all_to_all x1, waiting for transfers between devices, on_device(): lax.all_to_all(attn_partial[0].reshape(tensor_count, row_count, feature_w...  14 us
    ppermute x3, starting transfers between devices, on_device(): behind = lax.ppermute(behind, 'tensor', backward)  12.2 us
  transfers between devices with their start and end apart: 11, of which 8 were waited for; matrix products, arithmetic and copies ran while one was open for 5% of the time, Pallas kernels for 0%

profile of v6, /device:TPU:1, one launch (start us, length us, event | category | flops | bytes accessed | tf_op | source)
XLA Modules:
  0.0 288.5 jit_solution(2763907558451994514)
XLA Ops:
  7.3 7.7 %all-to-all-start = ((bf16[8,8,4096]{2,1,0:T(8,128)(2,1)}), bf16[8,8,4096]{2,1,0:T(8,128)(2,1)S(1)}, u32[]{:S(2)}, u32[]{:S(2)}) async-start(bf16[8,8,4096]{2,1,0:T(8,128)(2,1)} %bitcast.140), calls=%async_computation | async-start | bytes 1048576 | tf_op jit(solution)/shard_map/all_to_all | solution.py:37
  14.9 0.8 constant_dynamic-slice_fusion.2
  15.9 14.0 %all-to-all-done = bf16[8,8,4096]{2,1,0:T(8,128)(2,1)S(1)} async-done(((bf16[8,8,4096]{2,1,0:T(8,128)(2,1)}), bf16[8,8,4096]{2,1,0:T(8,128)(2,1)S(1)}, u32[]{:S(2)}, u32[]{:S(2)}) %all-to-all-start) | async-done | bytes 524320 | tf_op jit(solution)/shard_map/all_to_all | solution.py:37
  30.1 0.9 fusion.43
  31.2 1.2 convolution_convert_fusion
  32.4 1.1 copy.43
  33.5 46.5 %all_to_all.30 = bf16[64,2,4096]{2,1,0:T(2,128)(2,1)} all-to-all(bf16[64,2,4096]{2,1,0:T(2,128)(2,1)S(1)} %copy.43), channel_id=1, replica_groups=mesh['tensor'=8,'expert'=64] {'expert'}, dimensions={0} | all-to-all | bytes 2097152 | tf_op jit(solution)/shard_map/all_to_all | solution.py:53
  80.0 31.3 %all-gather.2.cloned.1.call-done = bf16[8,1024,512]{2,1,0:T(8,128)(2,1)} async-done(((bf16[1,1024,512]{2,1,0:T(8,128)(2,1)}), bf16[8,1024,512]{2,1,0:T(8,128)(2,1)}) %all-gather.2.cloned.1.call-update) | async-done | bytes 8388624 | tf_op jit(solution)/shard_map/all_gather | solution.py:54
  111.3 1.5 reshape.57
  112.8 2.9 %collective-permute-start = (bf16[128,4096]{1,0:T(8,128)(2,1)S(1)}, bf16[128,4096]{1,0:T(8,128)(2,1)}, u32[]{:S(2)}, u32[]{:S(2)}) collective-permute-start(bf16[128,4096]{1,0:T(8,128)(2,1)S(1)} %reshape.57), channel_id=1, source_target_pairs={{0,448},{64,0},{128,64},{192,128},{256,192},{320,256},{384,320},{4... | collective-permute-start | bytes 3145736 | tf_op jit(solution)/shard_map/ppermute | solution.py:72
  115.7 2.4 collective-permute-start.3
  118.1 20.6 %collective-permute-done = bf16[128,4096]{1,0:T(8,128)(2,1)} collective-permute-done((bf16[128,4096]{1,0:T(8,128)(2,1)S(1)}, bf16[128,4096]{1,0:T(8,128)(2,1)}, u32[]{:S(2)}, u32[]{:S(2)}) %collective-permute-start) | collective-permute-done | bytes 1048608 | tf_op jit(solution)/shard_map/ppermute | solution.py:72
  138.7 4.1 %collective-permute-start.1 = (bf16[128,4096]{1,0:T(8,128)(2,1)}, bf16[128,4096]{1,0:T(8,128)(2,1)S(1)}, u32[]{:S(2)}, u32[]{:S(2)}) collective-permute-start(bf16[128,4096]{1,0:T(8,128)(2,1)} %collective-permute-done), channel_id=1, source_target_pairs={{0,448},{64,0},{128,64},{192,128},{256,192},{320,256},{384,320},{4... | collective-permute-start | bytes 3145736 | tf_op jit(solution)/shard_map/ppermute | solution.py:72
  142.8 1.9 collective-permute-start.4
  145.6 1.6 fusion.34
  147.2 1.7 constant_dynamic-update-slice_fusion.14
  148.9 15.0 %collective-permute-done.1 = bf16[128,4096]{1,0:T(8,128)(2,1)S(1)} collective-permute-done((bf16[128,4096]{1,0:T(8,128)(2,1)}, bf16[128,4096]{1,0:T(8,128)(2,1)S(1)}, u32[]{:S(2)}, u32[]{:S(2)}) %collective-permute-start.1) | collective-permute-done | bytes 1048608 | tf_op jit(solution)/shard_map/ppermute | solution.py:72
  163.9 5.2 %collective-permute-start.2 = (bf16[128,4096]{1,0:T(8,128)(2,1)S(1)}, bf16[128,4096]{1,0:T(8,128)(2,1)S(1)}, u32[]{:S(2)}, u32[]{:S(2)}) collective-permute-start(bf16[128,4096]{1,0:T(8,128)(2,1)S(1)} %collective-permute-done.1), channel_id=1, source_target_pairs={{0,448},{64,0},{128,64},{192,128},{256,192},{320,256},{384,320},{4... | collective-permute-start | bytes 3145736 | tf_op jit(solution)/shard_map/ppermute | solution.py:72
  169.1 1.9 collective-permute-start.5
  171.0 1.6 fusion.20
  174.1 15.0 %collective-permute-done.2 = bf16[128,4096]{1,0:T(8,128)(2,1)S(1)} collective-permute-done((bf16[128,4096]{1,0:T(8,128)(2,1)S(1)}, bf16[128,4096]{1,0:T(8,128)(2,1)S(1)}, u32[]{:S(2)}, u32[]{:S(2)}) %collective-permute-start.2) | collective-permute-done | bytes 1048608 | tf_op jit(solution)/shard_map/ppermute | solution.py:72
  189.1 5.3 %collective-permute-start.7 = (bf16[64,4096]{1,0:T(8,128)(2,1)S(1)}, bf16[64,4096]{1,0:T(8,128)(2,1)S(1)}, u32[]{:S(2)}, u32[]{:S(2)}) collective-permute-start(bf16[64,4096]{1,0:T(8,128)(2,1)S(1)} %slice.9), channel_id=1, source_target_pairs={{0,448},{64,0},{128,64},{192,128},{256,192},{320,256},{384,320},{4... | collective-permute-start | bytes 1572872 | tf_op jit(solution)/shard_map/ppermute | solution.py:76
  194.5 1.9 collective-permute-start.6
  197.8 4.5 %collective-permute-done.7 = bf16[64,4096]{1,0:T(8,128)(2,1)S(1)} collective-permute-done((bf16[64,4096]{1,0:T(8,128)(2,1)S(1)}, bf16[64,4096]{1,0:T(8,128)(2,1)S(1)}, u32[]{:S(2)}, u32[]{:S(2)}) %collective-permute-start.7) | collective-permute-done | bytes 524320 | tf_op jit(solution)/shard_map/ppermute | solution.py:76
  202.9 4.4 %collective-permute-done.6 = bf16[64,4096]{1,0:T(8,128)(2,1)S(1)} collective-permute-done((bf16[64,4096]{1,0:T(8,128)(2,1)S(1)}, bf16[64,4096]{1,0:T(8,128)(2,1)S(1)}, u32[]{:S(2)}, u32[]{:S(2)}) %collective-permute-start.6) | collective-permute-done | bytes 524320 | tf_op jit(solution)/shard_map/ppermute | solution.py:75
  209.0 1.7 constant_dynamic-update-slice_fusion.8
  210.8 14.2 %all_to_all.31 = bf16[8,128,128]{2,1,0:T(8,128)(2,1)S(1)} all-to-all(bf16[8,128,128]{2,1,0:T(8,128)(2,1)S(1)} %constant_dynamic-slice_fusion), channel_id=1, replica_groups=mesh['tensor'=8,'expert'=64] {'tensor'}, dimensions={0} | all-to-all | bytes 524288 | tf_op jit(solution)/shard_map/all_to_all | solution.py:79
  225.1 4.7 %convolution_convert_fusion.1 = bf16[128,8,512]{2,0,1:T(8,128)(2,1)S(1)} fusion(bf16[128,1024,1]{0,1,2:T(8,128)(2,1)S(1)} %bitcast.138, bf16[8,1024,512]{2,1,0:T(8,128)(2,1)} %all-gather.2.cloned.1.call-done), kind=kOutput, calls=%fused_computation.3 | convolution fusion | flops 1074266112 | bytes 9699328 | tf_op jit(solution)/shard_map/sh,thc->stc/dot_general | solution.py:83
  230.4 1.6 reshape.58
  232.0 19.0 %all-to-all-start.3 = ((bf16[64,2,4096]{2,1,0:T(2,128)(2,1)}), bf16[64,2,4096]{2,1,0:T(2,128)(2,1)S(1)}, u32[]{:S(2)}, u32[]{:S(2)}) async-start(bf16[64,2,4096]{2,1,0:T(2,128)(2,1)} %reshape.58), calls=%async_computation.3 | async-start | bytes 2097152 | tf_op jit(solution)/shard_map/all_to_all | solution.py:87
  251.2 28.3 %all-to-all-done.3 = bf16[64,2,4096]{2,1,0:T(2,128)(2,1)S(1)} async-done(((bf16[64,2,4096]{2,1,0:T(2,128)(2,1)}), bf16[64,2,4096]{2,1,0:T(2,128)(2,1)S(1)}, u32[]{:S(2)}, u32[]{:S(2)}) %all-to-all-start.3) | async-done | bytes 1048608 | tf_op jit(solution)/shard_map/all_to_all | solution.py:87
  279.5 2.2 fusion
  (53 shorter events, 8.3 us)
Async XLA Ops:
  6.5 138.6 %copy-start = (bf16[1,4096,128]{2,1,0:T(8,128)(2,1)S(1)}, bf16[1,4096,128]{2,1,0:T(8,128)(2,1)}, u32[]{:S(2)}) copy-start(bf16[1,4096,128]{2,1,0:T(8,128)(2,1)} %param.12) | copy-start | bytes 3145732
  6.5 138.2 %copy-start.1 = (bf16[1,4096,128]{2,1,0:T(8,128)(2,1)S(1)}, bf16[1,4096,128]{2,1,0:T(8,128)(2,1)}, u32[]{:S(2)}) copy-start(bf16[1,4096,128]{2,1,0:T(8,128)(2,1)} %param.11) | copy-start | bytes 3145732
  6.5 104.8 %all-gather.2.cloned.1.call-start = ((), (), s32[]{:S(2)}) async-start(), calls=%async_computation.4 | async-start | bytes 9437184 | tf_op jit(solution)/shard_map/all_gather | solution.py:54
  7.3 22.6 %all-to-all-start = ((bf16[8,8,4096]{2,1,0:T(8,128)(2,1)}), bf16[8,8,4096]{2,1,0:T(8,128)(2,1)S(1)}, u32[]{:S(2)}, u32[]{:S(2)}) async-start(bf16[8,8,4096]{2,1,0:T(8,128)(2,1)} %bitcast.140), calls=%async_computation | async-start | bytes 1048576 | tf_op jit(solution)/shard_map/all_to_all | solution.py:37
  112.8 25.9 %collective-permute-start = (bf16[128,4096]{1,0:T(8,128)(2,1)S(1)}, bf16[128,4096]{1,0:T(8,128)(2,1)}, u32[]{:S(2)}, u32[]{:S(2)}) collective-permute-start(bf16[128,4096]{1,0:T(8,128)(2,1)S(1)} %reshape.57), channel_id=1, source_target_pairs={{0,448},{64,0},{128,64},{192,128},{256,192},{320,256},{384,320},{4... | collective-permute-start | bytes 3145736 | tf_op jit(solution)/shard_map/ppermute | solution.py:72
  115.7 27.1 %collective-permute-start.3 = (bf16[128,4096]{1,0:T(8,128)(2,1)S(1)}, bf16[128,4096]{1,0:T(8,128)(2,1)}, u32[]{:S(2)}, u32[]{:S(2)}) collective-permute-start(bf16[128,4096]{1,0:T(8,128)(2,1)S(1)} %reshape.57), channel_id=1, source_target_pairs={{0,64},{64,128},{128,192},{192,256},{256,320},{320,384},{384,448},... | collective-permute-start | bytes 3145736 | tf_op jit(solution)/shard_map/ppermute | solution.py:70
  138.7 25.2 %collective-permute-start.1 = (bf16[128,4096]{1,0:T(8,128)(2,1)}, bf16[128,4096]{1,0:T(8,128)(2,1)S(1)}, u32[]{:S(2)}, u32[]{:S(2)}) collective-permute-start(bf16[128,4096]{1,0:T(8,128)(2,1)} %collective-permute-done), channel_id=1, source_target_pairs={{0,448},{64,0},{128,64},{192,128},{256,192},{320,256},{384,320},{4... | collective-permute-start | bytes 3145736 | tf_op jit(solution)/shard_map/ppermute | solution.py:72
  142.8 26.3 %collective-permute-start.4 = (bf16[128,4096]{1,0:T(8,128)(2,1)}, bf16[128,4096]{1,0:T(8,128)(2,1)S(1)}, u32[]{:S(2)}, u32[]{:S(2)}) collective-permute-start(bf16[128,4096]{1,0:T(8,128)(2,1)} %collective-permute-done.3), channel_id=1, source_target_pairs={{0,64},{64,128},{128,192},{192,256},{256,320},{320,384},{384,448},... | collective-permute-start | bytes 3145736 | tf_op jit(solution)/shard_map/ppermute | solution.py:70
  163.9 25.2 %collective-permute-start.2 = (bf16[128,4096]{1,0:T(8,128)(2,1)S(1)}, bf16[128,4096]{1,0:T(8,128)(2,1)S(1)}, u32[]{:S(2)}, u32[]{:S(2)}) collective-permute-start(bf16[128,4096]{1,0:T(8,128)(2,1)S(1)} %collective-permute-done.1), channel_id=1, source_target_pairs={{0,448},{64,0},{128,64},{192,128},{256,192},{320,256},{384,320},{4... | collective-permute-start | bytes 3145736 | tf_op jit(solution)/shard_map/ppermute | solution.py:72
  169.1 25.3 %collective-permute-start.5 = (bf16[128,4096]{1,0:T(8,128)(2,1)S(1)}, bf16[128,4096]{1,0:T(8,128)(2,1)S(1)}, u32[]{:S(2)}, u32[]{:S(2)}) collective-permute-start(bf16[128,4096]{1,0:T(8,128)(2,1)S(1)} %collective-permute-done.4), channel_id=1, source_target_pairs={{0,64},{64,128},{128,192},{192,256},{256,320},{320,384},{384,448},... | collective-permute-start | bytes 3145736 | tf_op jit(solution)/shard_map/ppermute | solution.py:70
  189.1 13.2 %collective-permute-start.7 = (bf16[64,4096]{1,0:T(8,128)(2,1)S(1)}, bf16[64,4096]{1,0:T(8,128)(2,1)S(1)}, u32[]{:S(2)}, u32[]{:S(2)}) collective-permute-start(bf16[64,4096]{1,0:T(8,128)(2,1)S(1)} %slice.9), channel_id=1, source_target_pairs={{0,448},{64,0},{128,64},{192,128},{256,192},{320,256},{384,320},{4... | collective-permute-start | bytes 1572872 | tf_op jit(solution)/shard_map/ppermute | solution.py:76
  194.5 12.9 %collective-permute-start.6 = (bf16[64,4096]{1,0:T(8,128)(2,1)S(1)}, bf16[64,4096]{1,0:T(8,128)(2,1)S(1)}, u32[]{:S(2)}, u32[]{:S(2)}) collective-permute-start(bf16[64,4096]{1,0:T(8,128)(2,1)S(1)} %slice.8), channel_id=1, source_target_pairs={{0,64},{64,128},{128,192},{192,256},{256,320},{320,384},{384,448},... | collective-permute-start | bytes 1572872 | tf_op jit(solution)/shard_map/ppermute | solution.py:75
  225.0 26.0 %copy-start.2 = (f32[64,8]{0,1:T(8,128)S(1)}, f32[64,8]{0,1:T(8,128)}, u32[]{:S(2)}) copy-start(f32[64,8]{0,1:T(8,128)} %param.10) | copy-start | bytes 6148
  232.0 47.5 %all-to-all-start.3 = ((bf16[64,2,4096]{2,1,0:T(2,128)(2,1)}), bf16[64,2,4096]{2,1,0:T(2,128)(2,1)S(1)}, u32[]{:S(2)}, u32[]{:S(2)}) async-start(bf16[64,2,4096]{2,1,0:T(2,128)(2,1)} %reshape.58), calls=%async_computation.3 | async-start | bytes 2097152 | tf_op jit(solution)/shard_map/all_to_all | solution.py:87
Sparse Core Ops, SparseCore 0:
  9.4 101.8 all-gather.1

commit v7 on v6

--- a/solution.py
+++ b/solution.py
@@ -51,7 +51,18 @@
         "rec,rd->ecd", chosen.astype(jnp.bfloat16), restored, preferred_element_type=jnp.float32
     ).astype(jnp.bfloat16)
     recv = lax.all_to_all(send, "expert", split_axis=0, concat_axis=0, tiled=True)
-    down_all = lax.all_gather(down_matrix, "tensor", axis=0, tiled=False)
+    forward = [(i, (i + 1) % tensor_count) for i in range(tensor_count)]
+    backward = [(i, (i - 1) % tensor_count) for i in range(tensor_count)]
+    weight_parts = [down_matrix] + [None] * (tensor_count - 1)
+    ahead = down_matrix
+    behind = down_matrix
+    for step in range(1, tensor_count // 2 + 1):
+        ahead = lax.ppermute(ahead, "tensor", forward)
+        weight_parts[tensor_count - step] = ahead
+        if step < tensor_count - step:
+            behind = lax.ppermute(behind, "tensor", backward)
+            weight_parts[step] = behind
+    down_all = weight_parts
     def front(piece):
         gate_act = jnp.dot(piece, gate_matrix, preferred_element_type=jnp.float32)
         up_act = jnp.dot(piece, up_matrix, preferred_element_type=jnp.float32)
@@ -62,8 +73,6 @@
     hidden_parts = [front(own_rows)] + [None] * (tensor_count - 1)
     ahead = own_rows
     behind = own_rows
-    forward = [(i, (i + 1) % tensor_count) for i in range(tensor_count)]
-    backward = [(i, (i - 1) % tensor_count) for i in range(tensor_count)]
     half = own_rows.shape[0] // 2
     for step in range(1, tensor_count // 2 + 1):
         if step < tensor_count - step:
@@ -81,9 +90,10 @@
         "tensor", split_axis=0, concat_axis=2, tiled=True,
     )[0]
     expert_sum = jnp.einsum(
-        "sh,thc->stc", hidden_own, down_all, preferred_element_type=jnp.float32
-    )
-    expert_rows = expert_sum.astype(jnp.bfloat16).reshape(expert_count, capacity, feature_width)
+        "sh,mhc->smc", hidden_own, jnp.stack(down_all), preferred_element_type=jnp.float32
+    ).astype(jnp.bfloat16)
+    expert_sum = jnp.roll(expert_sum, tensor_index, axis=1)
+    expert_rows = expert_sum.reshape(expert_count, capacity, feature_width)
     returned = lax.all_to_all(expert_rows, "expert", split_axis=0, concat_axis=0, tiled=True)
     returned = returned.reshape(expert_count, capacity, feature_width)
     pair_weight = jnp.sum(jnp.where(hit, own_weights[..., None], 0.0), axis=1)

time: 289 us -> 281 us (0.972)
  blocking collectives: 60.7 us -> 0 us
  starting transfers between devices: 52.3 us -> 103 us
  local copies, waits for them, and re-layouts: 6.19 us -> 20.1 us
  between operations: 13.7 us -> 0.5 us
  matrix products: 20.5 us -> 15.4 us
  waiting for transfers between devices: 134 us -> 139 us
    ppermute x3 -> x7, waiting for transfers between devices: 0.01 us -> 61.6 us  [on_device(): ahead = lax.ppermute(ahead, 'tensor', forward)]
    all_to_all x2 -> x0, blocking collectives: 60.7 us -> none  [the longest x1 46.5 us: on_device(): lax.all_to_all(send, 'expert', split_axis=0, concat_axis=0, tiled=True)]
    ppermute x3 -> x6, waiting for transfers between devices: 50.5 us -> 8.15 us  [on_device(): behind = lax.ppermute(behind, 'tensor', backward)]
    all_gather x1 -> x0, waiting for transfers between devices: 31.3 us -> none  [on_device(): down_all = lax.all_gather(down_matrix, 'tensor', axis=0, tiled=False)]
    all_to_all x0 -> x2, waiting for transfers between devices: none -> 27.6 us  [the longest x1 21.7 us: on_device(): lax.all_to_all(send, 'expert', split_axis=0, concat_axis=0, tiled=True)]
    all_to_all x0 -> x2, starting transfers between devices: none -> 22.3 us  [the longest x1 16 us: on_device(): lax.all_to_all(send, 'expert', split_axis=0, concat_axis=0, tiled=True)]
    ppermute x3 -> x7, starting transfers between devices: 6.23 us -> 23.4 us  [on_device(): ahead = lax.ppermute(ahead, 'tensor', forward)]
    ppermute x3 -> x6, starting transfers between devices: 12.2 us -> 24 us  [on_device(): behind = lax.ppermute(behind, 'tensor', backward)]
  transfers between devices with their start and end apart: 11 -> 19, of which waited for: 8 -> 15; matrix products, arithmetic and copies ran while one was open for 5% -> 8% of each run, Pallas kernels for 0% -> 0%
where the time goes in v7:
time: 281 us; the launch traced here: 280 us
  waiting for transfers between devices  139 us (49%)
  starting transfers between devices  103 us (37%)
  local copies, waits for them, and re-layouts  20.1 us (7%)
  matrix products  15.4 us (5%)
    ppermute x7, waiting for transfers between devices, on_device(): ahead = lax.ppermute(ahead, 'tensor', forward)  61.6 us
    all_to_all x1, waiting for transfers between devices, on_device(): lax.all_to_all(expert_rows, 'expert', split_axis=0, concat_axis=0, tiled=...  28.3 us
    ppermute x6, starting transfers between devices, on_device(): behind = lax.ppermute(behind, 'tensor', backward)  24 us
    ppermute x7, starting transfers between devices, on_device(): ahead = lax.ppermute(ahead, 'tensor', forward)  23.4 us
    all_to_all x1, starting transfers between devices, on_device(): lax.all_to_all(expert_rows, 'expert', split_axis=0, concat_axis=0, tiled=...  22 us
    all_to_all x1, waiting for transfers between devices, on_device(): lax.all_to_all(send, 'expert', split_axis=0, concat_axis=0, tiled=True)  21.7 us
    all_to_all x1, starting transfers between devices, on_device(): lax.all_to_all(send, 'expert', split_axis=0, concat_axis=0, tiled=True)  16 us
    unnamed x27, local copies, waits for them, and re-layouts  11.1 us
  transfers between devices with their start and end apart: 19, of which 15 were waited for; matrix products, arithmetic and copies ran while one was open for 8% of the time, Pallas kernels for 0%

profile of v7, /device:TPU:1, one launch (start us, length us, event | category | flops | bytes accessed | tf_op | source)
XLA Modules:
  0.0 279.7 jit_solution(11885599860619819126)
XLA Ops:
  0.0 4.1 %collective-permute-start.3 = (bf16[1024,512]{1,0:T(8,128)(2,1)}, bf16[1024,512]{1,0:T(8,128)(2,1)S(1)}, u32[]{:S(2)}, u32[]{:S(2)}) collective-permute-start(bf16[1024,512]{1,0:T(8,128)(2,1)} %bitcast.156), channel_id=1, source_target_pairs={{0,64},{64,128},{128,192},{192,256},{256,320},{320,384},{384,448},... | collective-permute-start | bytes 3145736 | tf_op jit(solution)/shard_map/ppermute | solution.py:60
  4.2 5.9 %all-to-all-start = ((bf16[8,8,4096]{2,1,0:T(8,128)(2,1)}), bf16[8,8,4096]{2,1,0:T(8,128)(2,1)S(1)}, u32[]{:S(2)}, u32[]{:S(2)}) async-start(bf16[8,8,4096]{2,1,0:T(8,128)(2,1)} %bitcast.160), calls=%async_computation | async-start | bytes 1048576 | tf_op jit(solution)/shard_map/all_to_all | solution.py:37
  10.1 4.6 %collective-permute-start = (bf16[1024,512]{1,0:T(8,128)(2,1)}, bf16[1024,512]{1,0:T(8,128)(2,1)}, u32[]{:S(2)}, u32[]{:S(2)}) collective-permute-start(bf16[1024,512]{1,0:T(8,128)(2,1)} %bitcast.157), channel_id=1, source_target_pairs={{0,448},{64,0},{128,64},{192,128},{256,192},{320,256},{384,320},{4... | collective-permute-start | bytes 3145736 | tf_op jit(solution)/shard_map/ppermute | solution.py:63
  15.5 8.5 %collective-permute-done.3 = bf16[1024,512]{1,0:T(8,128)(2,1)S(1)} collective-permute-done((bf16[1024,512]{1,0:T(8,128)(2,1)}, bf16[1024,512]{1,0:T(8,128)(2,1)S(1)}, u32[]{:S(2)}, u32[]{:S(2)}) %collective-permute-start.3) | collective-permute-done | bytes 1048608 | tf_op jit(solution)/shard_map/ppermute | solution.py:60
  24.0 7.9 %collective-permute-start.4 = (bf16[1024,512]{1,0:T(8,128)(2,1)S(1)}, bf16[1024,512]{1,0:T(8,128)(2,1)}, u32[]{:S(2)}, u32[]{:S(2)}) collective-permute-start(bf16[1024,512]{1,0:T(8,128)(2,1)S(1)} %collective-permute-done.3), channel_id=1, source_target_pairs={{0,64},{64,128},{128,192},{192,256},{256,320},{320,384},{384,448},... | collective-permute-start | bytes 3145736 | tf_op jit(solution)/shard_map/ppermute | solution.py:60
  32.0 6.8 %all-to-all-done = bf16[8,8,4096]{2,1,0:T(8,128)(2,1)S(1)} async-done(((bf16[8,8,4096]{2,1,0:T(8,128)(2,1)}), bf16[8,8,4096]{2,1,0:T(8,128)(2,1)S(1)}, u32[]{:S(2)}, u32[]{:S(2)}) %all-to-all-start) | async-done | bytes 524320 | tf_op jit(solution)/shard_map/all_to_all | solution.py:37
  40.1 4.3 %collective-permute-done = bf16[1024,512]{1,0:T(8,128)(2,1)} collective-permute-done((bf16[1024,512]{1,0:T(8,128)(2,1)}, bf16[1024,512]{1,0:T(8,128)(2,1)}, u32[]{:S(2)}, u32[]{:S(2)}) %collective-permute-start) | collective-permute-done | bytes 1048608 | tf_op jit(solution)/shard_map/ppermute | solution.py:63
  44.4 3.9 %collective-permute-start.1 = (bf16[1024,512]{1,0:T(8,128)(2,1)}, bf16[1024,512]{1,0:T(8,128)(2,1)}, u32[]{:S(2)}, u32[]{:S(2)}) collective-permute-start(bf16[1024,512]{1,0:T(8,128)(2,1)} %collective-permute-done), channel_id=1, source_target_pairs={{0,448},{64,0},{128,64},{192,128},{256,192},{320,256},{384,320},{4... | collective-permute-start | bytes 3145736 | tf_op jit(solution)/shard_map/ppermute | solution.py:63
  48.3 13.2 %collective-permute-done.4 = bf16[1024,512]{1,0:T(8,128)(2,1)} collective-permute-done((bf16[1024,512]{1,0:T(8,128)(2,1)S(1)}, bf16[1024,512]{1,0:T(8,128)(2,1)}, u32[]{:S(2)}, u32[]{:S(2)}) %collective-permute-start.4) | collective-permute-done | bytes 1048608 | tf_op jit(solution)/shard_map/ppermute | solution.py:60
  64.6 2.1 copy.43
  66.8 16.0 %all-to-all-start.1 = ((bf16[64,2,4096]{2,1,0:T(2,128)(2,1)}), bf16[64,2,4096]{2,1,0:T(2,128)(2,1)S(1)}, u32[]{:S(2)}, u32[]{:S(2)}) async-start(bf16[64,2,4096]{2,1,0:T(2,128)(2,1)} %copy.43), calls=%async_computation.1 | async-start | bytes 2097152 | tf_op jit(solution)/shard_map/all_to_all | solution.py:53
  82.8 4.9 %collective-permute-start.2 = (bf16[1024,512]{1,0:T(8,128)(2,1)}, bf16[1024,512]{1,0:T(8,128)(2,1)}, u32[]{:S(2)}, u32[]{:S(2)}) collective-permute-start(bf16[1024,512]{1,0:T(8,128)(2,1)} %collective-permute-done.1), channel_id=1, source_target_pairs={{0,448},{64,0},{128,64},{192,128},{256,192},{320,256},{384,320},{4... | collective-permute-start | bytes 3145736 | tf_op jit(solution)/shard_map/ppermute | solution.py:63
  89.6 21.7 %all-to-all-done.1 = bf16[64,2,4096]{2,1,0:T(2,128)(2,1)S(1)} async-done(((bf16[64,2,4096]{2,1,0:T(2,128)(2,1)}), bf16[64,2,4096]{2,1,0:T(2,128)(2,1)S(1)}, u32[]{:S(2)}, u32[]{:S(2)}) %all-to-all-start.1) | async-done | bytes 1048608 | tf_op jit(solution)/shard_map/all_to_all | solution.py:53
  114.5 2.3 collective-permute-start.10
  116.8 4.2 %collective-permute-start.7 = (bf16[128,4096]{1,0:T(8,128)(2,1)S(1)}, bf16[128,4096]{1,0:T(8,128)(2,1)S(1)}, u32[]{:S(2)}, u32[]{:S(2)}) collective-permute-start(bf16[128,4096]{1,0:T(8,128)(2,1)S(1)} %reshape.57), channel_id=1, source_target_pairs={{0,448},{64,0},{128,64},{192,128},{256,192},{320,256},{384,320},{4... | collective-permute-start | bytes 3145736 | tf_op jit(solution)/shard_map/ppermute | solution.py:81
  127.9 10.8 %collective-permute-done.10 = bf16[128,4096]{1,0:T(8,128)(2,1)S(1)} collective-permute-done((bf16[128,4096]{1,0:T(8,128)(2,1)S(1)}, bf16[128,4096]{1,0:T(8,128)(2,1)S(1)}, u32[]{:S(2)}, u32[]{:S(2)}) %collective-permute-start.10) | collective-permute-done | bytes 1048608 | tf_op jit(solution)/shard_map/ppermute | solution.py:79
  140.6 4.6 %collective-permute-start.8 = (bf16[128,4096]{1,0:T(8,128)(2,1)S(1)}, bf16[128,4096]{1,0:T(8,128)(2,1)S(1)}, u32[]{:S(2)}, u32[]{:S(2)}) collective-permute-start(bf16[128,4096]{1,0:T(8,128)(2,1)S(1)} %collective-permute-done.7), channel_id=1, source_target_pairs={{0,448},{64,0},{128,64},{192,128},{256,192},{320,256},{384,320},{4... | collective-permute-start | bytes 3145736 | tf_op jit(solution)/shard_map/ppermute | solution.py:81
  147.8 14.2 %collective-permute-done.11 = bf16[128,4096]{1,0:T(8,128)(2,1)S(1)} collective-permute-done((bf16[128,4096]{1,0:T(8,128)(2,1)S(1)}, bf16[128,4096]{1,0:T(8,128)(2,1)S(1)}, u32[]{:S(2)}, u32[]{:S(2)}) %collective-permute-start.11) | collective-permute-done | bytes 1048608 | tf_op jit(solution)/shard_map/ppermute | solution.py:79
  162.0 3.4 %collective-permute-start.12 = (bf16[128,4096]{1,0:T(8,128)(2,1)S(1)}, bf16[128,4096]{1,0:T(8,128)(2,1)S(1)}, u32[]{:S(2)}, u32[]{:S(2)}) collective-permute-start(bf16[128,4096]{1,0:T(8,128)(2,1)S(1)} %collective-permute-done.11), channel_id=1, source_target_pairs={{0,64},{64,128},{128,192},{192,256},{256,320},{320,384},{384,448},... | collective-permute-start | bytes 3145736 | tf_op jit(solution)/shard_map/ppermute | solution.py:79
  170.8 14.3 %collective-permute-done.12 = bf16[128,4096]{1,0:T(8,128)(2,1)S(1)} collective-permute-done((bf16[128,4096]{1,0:T(8,128)(2,1)S(1)}, bf16[128,4096]{1,0:T(8,128)(2,1)S(1)}, u32[]{:S(2)}, u32[]{:S(2)}) %collective-permute-start.12) | collective-permute-done | bytes 1048608 | tf_op jit(solution)/shard_map/ppermute | solution.py:79
  185.2 2.9 %collective-permute-start.13 = (bf16[64,4096]{1,0:T(8,128)(2,1)S(1)}, bf16[64,4096]{1,0:T(8,128)(2,1)S(1)}, u32[]{:S(2)}, u32[]{:S(2)}) collective-permute-start(bf16[64,4096]{1,0:T(8,128)(2,1)S(1)} %slice.8), channel_id=1, source_target_pairs={{0,64},{64,128},{128,192},{192,256},{256,320},{320,384},{384,448},... | collective-permute-start | bytes 1572872 | tf_op jit(solution)/shard_map/ppermute | solution.py:84
  188.1 2.0 collective-permute-done.9
  190.2 2.1 collective-permute-start.14
  193.6 2.7 collective-permute-done.13
  197.0 4.1 %collective-permute-done.14 = bf16[64,4096]{1,0:T(8,128)(2,1)S(1)} collective-permute-done((bf16[64,4096]{1,0:T(8,128)(2,1)S(1)}, bf16[64,4096]{1,0:T(8,128)(2,1)S(1)}, u32[]{:S(2)}, u32[]{:S(2)}) %collective-permute-start.14) | collective-permute-done | bytes 524320 | tf_op jit(solution)/shard_map/ppermute | solution.py:85
  203.9 6.3 %all-to-all-start.2 = ((bf16[8,128,128]{2,1,0:T(8,128)(2,1)}), bf16[8,128,128]{2,1,0:T(8,128)(2,1)S(1)}, u32[]{:S(2)}, u32[]{:S(2)}) async-start(bf16[8,128,128]{2,1,0:T(8,128)(2,1)} %constant_dynamic-slice_fusion), calls=%async_computation.2 | async-start | bytes 524288 | tf_op jit(solution)/shard_map/all_to_all | solution.py:88
  210.2 2.3 bitcast_dynamic-update-slice_fusion.1
  213.6 5.9 %all-to-all-done.2 = bf16[8,128,128]{2,1,0:T(8,128)(2,1)S(1)} async-done(((bf16[8,128,128]{2,1,0:T(8,128)(2,1)}), bf16[8,128,128]{2,1,0:T(8,128)(2,1)S(1)}, u32[]{:S(2)}, u32[]{:S(2)}) %all-to-all-start.2) | async-done | bytes 262176 | tf_op jit(solution)/shard_map/all_to_all | solution.py:88
  219.8 4.7 %convolution_convert_fusion.1 = bf16[128,8,512]{2,0,1:T(8,128)(2,1)S(1)} fusion(bf16[128,1024,1]{0,1,2:T(8,128)(2,1)S(1)} %bitcast.155, bf16[8,1024,512]{2,1,0:T(8,128)(2,1)} %bitcast_dynamic-update-slice_fusion), kind=kOutput, calls=%fused_computation.5 | convolution fusion | flops 1074266112 | bytes 9699328 | tf_op jit(solution)/shard_map/sh,mhc->smc/dot_general | solution.py:92
  227.0 22.0 %all-to-all-start.3 = ((bf16[64,2,4096]{2,1,0:T(2,128)(2,1)}), bf16[64,2,4096]{2,1,0:T(2,128)(2,1)S(1)}, u32[]{:S(2)}, u32[]{:S(2)}) async-start(bf16[64,2,4096]{2,1,0:T(2,128)(2,1)} %reshape.58), calls=%async_computation.3 | async-start | bytes 2097152 | tf_op jit(solution)/shard_map/all_to_all | solution.py:97
  249.2 28.3 %all-to-all-done.3 = bf16[64,2,4096]{2,1,0:T(2,128)(2,1)S(1)} async-done(((bf16[64,2,4096]{2,1,0:T(2,128)(2,1)}), bf16[64,2,4096]{2,1,0:T(2,128)(2,1)S(1)}, u32[]{:S(2)}, u32[]{:S(2)}) %all-to-all-start.3) | async-done | bytes 1048608 | tf_op jit(solution)/shard_map/all_to_all | solution.py:97
  277.5 2.2 fusion
  (83 shorter events, 36.3 us)
Async XLA Ops:
  0.0 146.5 %copy-start = (bf16[1,4096,128]{2,1,0:T(8,128)(2,1)S(1)}, bf16[1,4096,128]{2,1,0:T(8,128)(2,1)}, u32[]{:S(2)}) copy-start(bf16[1,4096,128]{2,1,0:T(8,128)(2,1)} %param.12) | copy-start | bytes 3145732
  0.0 24.0 %collective-permute-start.3 = (bf16[1024,512]{1,0:T(8,128)(2,1)}, bf16[1024,512]{1,0:T(8,128)(2,1)S(1)}, u32[]{:S(2)}, u32[]{:S(2)}) collective-permute-start(bf16[1024,512]{1,0:T(8,128)(2,1)} %bitcast.156), channel_id=1, source_target_pairs={{0,64},{64,128},{128,192},{192,256},{256,320},{320,384},{384,448},... | collective-permute-start | bytes 3145736 | tf_op jit(solution)/shard_map/ppermute | solution.py:60
  4.2 34.6 %all-to-all-start = ((bf16[8,8,4096]{2,1,0:T(8,128)(2,1)}), bf16[8,8,4096]{2,1,0:T(8,128)(2,1)S(1)}, u32[]{:S(2)}, u32[]{:S(2)}) async-start(bf16[8,8,4096]{2,1,0:T(8,128)(2,1)} %bitcast.160), calls=%async_computation | async-start | bytes 1048576 | tf_op jit(solution)/shard_map/all_to_all | solution.py:37
  10.1 34.3 %collective-permute-start = (bf16[1024,512]{1,0:T(8,128)(2,1)}, bf16[1024,512]{1,0:T(8,128)(2,1)}, u32[]{:S(2)}, u32[]{:S(2)}) collective-permute-start(bf16[1024,512]{1,0:T(8,128)(2,1)} %bitcast.157), channel_id=1, source_target_pairs={{0,448},{64,0},{128,64},{192,128},{256,192},{320,256},{384,320},{4... | collective-permute-start | bytes 3145736 | tf_op jit(solution)/shard_map/ppermute | solution.py:63
  24.0 39.4 %copy-start.4 = (bf16[1024,512]{1,0:T(8,128)(2,1)}, bf16[1024,512]{1,0:T(8,128)(2,1)S(1)}, u32[]{:S(2)}) copy-start(bf16[1024,512]{1,0:T(8,128)(2,1)S(1)} %collective-permute-done.3) | copy-start | bytes 3145732
  24.0 37.5 %collective-permute-start.4 = (bf16[1024,512]{1,0:T(8,128)(2,1)S(1)}, bf16[1024,512]{1,0:T(8,128)(2,1)}, u32[]{:S(2)}, u32[]{:S(2)}) collective-permute-start(bf16[1024,512]{1,0:T(8,128)(2,1)S(1)} %collective-permute-done.3), channel_id=1, source_target_pairs={{0,64},{64,128},{128,192},{192,256},{256,320},{320,384},{384,448},... | collective-permute-start | bytes 3145736 | tf_op jit(solution)/shard_map/ppermute | solution.py:60
  44.4 38.4 %collective-permute-start.1 = (bf16[1024,512]{1,0:T(8,128)(2,1)}, bf16[1024,512]{1,0:T(8,128)(2,1)}, u32[]{:S(2)}, u32[]{:S(2)}) collective-permute-start(bf16[1024,512]{1,0:T(8,128)(2,1)} %collective-permute-done), channel_id=1, source_target_pairs={{0,448},{64,0},{128,64},{192,128},{256,192},{320,256},{384,320},{4... | collective-permute-start | bytes 3145736 | tf_op jit(solution)/shard_map/ppermute | solution.py:63
  61.5 26.2 %collective-permute-start.5 = (bf16[1024,512]{1,0:T(8,128)(2,1)}, bf16[1024,512]{1,0:T(8,128)(2,1)}, u32[]{:S(2)}, u32[]{:S(2)}) collective-permute-start(bf16[1024,512]{1,0:T(8,128)(2,1)} %collective-permute-done.4), channel_id=1, source_target_pairs={{0,64},{64,128},{128,192},{192,256},{256,320},{320,384},{384,448},... | collective-permute-start | bytes 3145736 | tf_op jit(solution)/shard_map/ppermute | solution.py:60
  64.6 62.9 %copy-start.1 = (bf16[1,4096,128]{2,1,0:T(8,128)(2,1)S(1)}, bf16[1,4096,128]{2,1,0:T(8,128)(2,1)}, u32[]{:S(2)}) copy-start(bf16[1,4096,128]{2,1,0:T(8,128)(2,1)} %param.11) | copy-start | bytes 3145732
  66.8 44.6 %all-to-all-start.1 = ((bf16[64,2,4096]{2,1,0:T(2,128)(2,1)}), bf16[64,2,4096]{2,1,0:T(2,128)(2,1)S(1)}, u32[]{:S(2)}, u32[]{:S(2)}) async-start(bf16[64,2,4096]{2,1,0:T(2,128)(2,1)} %copy.43), calls=%async_computation.1 | async-start | bytes 2097152 | tf_op jit(solution)/shard_map/all_to_all | solution.py:53
  82.8 28.5 %collective-permute-start.2 = (bf16[1024,512]{1,0:T(8,128)(2,1)}, bf16[1024,512]{1,0:T(8,128)(2,1)}, u32[]{:S(2)}, u32[]{:S(2)}) collective-permute-start(bf16[1024,512]{1,0:T(8,128)(2,1)} %collective-permute-done.1), channel_id=1, source_target_pairs={{0,448},{64,0},{128,64},{192,128},{256,192},{320,256},{384,320},{4... | collective-permute-start | bytes 3145736 | tf_op jit(solution)/shard_map/ppermute | solution.py:63
  87.7 25.4 %collective-permute-start.6 = (bf16[1024,512]{1,0:T(8,128)(2,1)}, bf16[1024,512]{1,0:T(8,128)(2,1)}, u32[]{:S(2)}, u32[]{:S(2)}) collective-permute-start(bf16[1024,512]{1,0:T(8,128)(2,1)} %collective-permute-done.5), channel_id=1, source_target_pairs={{0,64},{64,128},{128,192},{192,256},{256,320},{320,384},{384,448},... | collective-permute-start | bytes 3145736 | tf_op jit(solution)/shard_map/ppermute | solution.py:60
  111.3 1.0 copy-start.3
  114.5 24.2 %collective-permute-start.10 = (bf16[128,4096]{1,0:T(8,128)(2,1)S(1)}, bf16[128,4096]{1,0:T(8,128)(2,1)S(1)}, u32[]{:S(2)}, u32[]{:S(2)}) collective-permute-start(bf16[128,4096]{1,0:T(8,128)(2,1)S(1)} %reshape.57), channel_id=1, source_target_pairs={{0,64},{64,128},{128,192},{192,256},{256,320},{320,384},{384,448},... | collective-permute-start | bytes 3145736 | tf_op jit(solution)/shard_map/ppermute | solution.py:79
  116.8 23.8 %collective-permute-start.7 = (bf16[128,4096]{1,0:T(8,128)(2,1)S(1)}, bf16[128,4096]{1,0:T(8,128)(2,1)S(1)}, u32[]{:S(2)}, u32[]{:S(2)}) collective-permute-start(bf16[128,4096]{1,0:T(8,128)(2,1)S(1)} %reshape.57), channel_id=1, source_target_pairs={{0,448},{64,0},{128,64},{192,128},{256,192},{320,256},{384,320},{4... | collective-permute-start | bytes 3145736 | tf_op jit(solution)/shard_map/ppermute | solution.py:81
  138.7 23.3 %collective-permute-start.11 = (bf16[128,4096]{1,0:T(8,128)(2,1)S(1)}, bf16[128,4096]{1,0:T(8,128)(2,1)S(1)}, u32[]{:S(2)}, u32[]{:S(2)}) collective-permute-start(bf16[128,4096]{1,0:T(8,128)(2,1)S(1)} %collective-permute-done.10), channel_id=1, source_target_pairs={{0,64},{64,128},{128,192},{192,256},{256,320},{320,384},{384,448},... | collective-permute-start | bytes 3145736 | tf_op jit(solution)/shard_map/ppermute | solution.py:79
  140.6 26.6 %collective-permute-start.8 = (bf16[128,4096]{1,0:T(8,128)(2,1)S(1)}, bf16[128,4096]{1,0:T(8,128)(2,1)S(1)}, u32[]{:S(2)}, u32[]{:S(2)}) collective-permute-start(bf16[128,4096]{1,0:T(8,128)(2,1)S(1)} %collective-permute-done.7), channel_id=1, source_target_pairs={{0,448},{64,0},{128,64},{192,128},{256,192},{320,256},{384,320},{4... | collective-permute-start | bytes 3145736 | tf_op jit(solution)/shard_map/ppermute | solution.py:81
  146.5 43.7 %copy-start.2 = (bf16[8,1024,512]{2,1,0:T(8,128)(2,1)}, bf16[8,1024,512]{2,1,0:T(8,128)(2,1)S(1)}, u32[]{:S(2)}) copy-start(bf16[8,1024,512]{2,1,0:T(8,128)(2,1)S(1)} %bitcast_dynamic-update-slice_fusion.2) | copy-start | bytes 25165828
  162.0 23.1 %collective-permute-start.12 = (bf16[128,4096]{1,0:T(8,128)(2,1)S(1)}, bf16[128,4096]{1,0:T(8,128)(2,1)S(1)}, u32[]{:S(2)}, u32[]{:S(2)}) collective-permute-start(bf16[128,4096]{1,0:T(8,128)(2,1)S(1)} %collective-permute-done.11), channel_id=1, source_target_pairs={{0,64},{64,128},{128,192},{192,256},{256,320},{320,384},{384,448},... | collective-permute-start | bytes 3145736 | tf_op jit(solution)/shard_map/ppermute | solution.py:79
  167.2 23.0 %collective-permute-start.9 = (bf16[128,4096]{1,0:T(8,128)(2,1)S(1)}, bf16[128,4096]{1,0:T(8,128)(2,1)S(1)}, u32[]{:S(2)}, u32[]{:S(2)}) collective-permute-start(bf16[128,4096]{1,0:T(8,128)(2,1)S(1)} %collective-permute-done.8), channel_id=1, source_target_pairs={{0,448},{64,0},{128,64},{192,128},{256,192},{320,256},{384,320},{4... | collective-permute-start | bytes 3145736 | tf_op jit(solution)/shard_map/ppermute | solution.py:81
  185.2 11.2 %collective-permute-start.13 = (bf16[64,4096]{1,0:T(8,128)(2,1)S(1)}, bf16[64,4096]{1,0:T(8,128)(2,1)S(1)}, u32[]{:S(2)}, u32[]{:S(2)}) collective-permute-start(bf16[64,4096]{1,0:T(8,128)(2,1)S(1)} %slice.8), channel_id=1, source_target_pairs={{0,64},{64,128},{128,192},{192,256},{256,320},{320,384},{384,448},... | collective-permute-start | bytes 1572872 | tf_op jit(solution)/shard_map/ppermute | solution.py:84
  190.2 10.9 %collective-permute-start.14 = (bf16[64,4096]{1,0:T(8,128)(2,1)S(1)}, bf16[64,4096]{1,0:T(8,128)(2,1)S(1)}, u32[]{:S(2)}, u32[]{:S(2)}) collective-permute-start(bf16[64,4096]{1,0:T(8,128)(2,1)S(1)} %slice.9), channel_id=1, source_target_pairs={{0,448},{64,0},{128,64},{192,128},{256,192},{320,256},{384,320},{4... | collective-permute-start | bytes 1572872 | tf_op jit(solution)/shard_map/ppermute | solution.py:85
  193.6 18.9 %copy-start.5 = (bf16[1024,512]{1,0:T(8,128)(2,1)S(1)}, bf16[1024,512]{1,0:T(8,128)(2,1)}, u32[]{:S(2)}) copy-start(bf16[1024,512]{1,0:T(8,128)(2,1)} %copy-done.4) | copy-start | bytes 3145732
  203.9 15.6 %all-to-all-start.2 = ((bf16[8,128,128]{2,1,0:T(8,128)(2,1)}), bf16[8,128,128]{2,1,0:T(8,128)(2,1)S(1)}, u32[]{:S(2)}, u32[]{:S(2)}) async-start(bf16[8,128,128]{2,1,0:T(8,128)(2,1)} %constant_dynamic-slice_fusion), calls=%async_computation.2 | async-start | bytes 524288 | tf_op jit(solution)/shard_map/all_to_all | solution.py:88
  219.7 29.2 %copy-start.6 = (f32[64,8]{0,1:T(8,128)S(1)}, f32[64,8]{0,1:T(8,128)}, u32[]{:S(2)}) copy-start(f32[64,8]{0,1:T(8,128)} %param.10) | copy-start | bytes 6148
  227.0 50.5 %all-to-all-start.3 = ((bf16[64,2,4096]{2,1,0:T(2,128)(2,1)}), bf16[64,2,4096]{2,1,0:T(2,128)(2,1)S(1)}, u32[]{:S(2)}, u32[]{:S(2)}) async-start(bf16[64,2,4096]{2,1,0:T(2,128)(2,1)} %reshape.58), calls=%async_computation.3 | async-start | bytes 2097152 | tf_op jit(solution)/shard_map/all_to_all | solution.py:97

commit v8 on v7

--- a/solution.py
+++ b/solution.py
@@ -70,25 +70,26 @@
 
     down_all, recv = lax.optimization_barrier((down_all, recv))
     own_rows = recv.reshape(expert_count * capacity, feature_width)
-    hidden_parts = [front(own_rows)] + [None] * (tensor_count - 1)
+    def toward(shift):
+        return [(i, (i + shift) % tensor_count) for i in range(tensor_count)]
+
+    received = [front(own_rows)] + [None] * (tensor_count - 1)
     ahead = own_rows
     behind = own_rows
     half = own_rows.shape[0] // 2
     for step in range(1, tensor_count // 2 + 1):
         if step < tensor_count - step:
             ahead = lax.ppermute(ahead, "tensor", forward)
-            hidden_parts[tensor_count - step] = front(ahead)
+            received[step] = lax.ppermute(front(ahead), "tensor", toward(-step))
             behind = lax.ppermute(behind, "tensor", backward)
-            hidden_parts[step] = front(behind)
+            received[tensor_count - step] = lax.ppermute(front(behind), "tensor", toward(step))
         else:
             first = lax.ppermute(ahead[:half], "tensor", forward)
             second = lax.ppermute(behind[half:], "tensor", backward)
-            hidden_parts[step] = jnp.concatenate([front(first), front(second)], axis=0)
-    hidden = jnp.roll(jnp.stack(hidden_parts), tensor_index, axis=0)
-    hidden_own = lax.all_to_all(
-        hidden.reshape(tensor_count, expert_count * capacity, -1),
-        "tensor", split_axis=0, concat_axis=2, tiled=True,
-    )[0]
+            opposite = jnp.concatenate([front(first), front(second)], axis=0)
+            received[step] = lax.ppermute(opposite, "tensor", toward(step))
+    hidden_own = jnp.roll(jnp.stack(received), tensor_index, axis=0)
+    hidden_own = hidden_own.transpose(1, 0, 2).reshape(own_rows.shape[0], -1)
     expert_sum = jnp.einsum(
         "sh,mhc->smc", hidden_own, jnp.stack(down_all), preferred_element_type=jnp.float32
     ).astype(jnp.bfloat16)

time: 281 us -> 296 us (1.053)
  starting transfers between devices: 103 us -> 124 us
  local copies, waits for them, and re-layouts: 20.1 us -> 16.4 us
  waiting for transfers between devices: 139 us -> 136 us
    ppermute x0 -> x7, waiting for transfers between devices: none -> 26.7 us  [the longest x3 22.4 us: on_device(): received[step] = lax.ppermute(front(ahead), 'tensor', toward(-step))]
    ppermute x7, waiting for transfers between devices: 61.6 us -> 35.9 us  [on_device(): ahead = lax.ppermute(ahead, 'tensor', forward)]
    ppermute x0 -> x7, starting transfers between devices: none -> 21.7 us  [the longest x3 11.6 us: on_device(): lax.ppermute(front(behind), 'tensor', toward(step))]
    all_to_all x1 -> x0, starting transfers between devices: 6.28 us -> none  [on_device(): lax.all_to_all(hidden.reshape(tensor_count, expert_count * capacity, -1),...]
    ppermute x1, waiting for transfers between devices: 2.71 us -> 8.99 us  [on_device(): first = lax.ppermute(ahead[:half], 'tensor', forward)]
    all_to_all x1 -> x0, waiting for transfers between devices: 5.95 us -> none  [on_device(): lax.all_to_all(hidden.reshape(tensor_count, expert_count * capacity, -1),...]
    ppermute x6, waiting for transfers between devices: 8.15 us -> 4.35 us  [on_device(): behind = lax.ppermute(behind, 'tensor', backward)]
    ppermute x6, starting transfers between devices: 24 us -> 27.5 us  [on_device(): behind = lax.ppermute(behind, 'tensor', backward)]
  transfers between devices with their start and end apart: 19 -> 25, of which waited for: 15 -> 13; matrix products, arithmetic and copies ran while one was open for 8% -> 8% of each run, Pallas kernels for 0% -> 0%
where the time goes in v8:
time: 296 us; the launch traced here: 294 us
  waiting for transfers between devices  136 us (46%)
  starting transfers between devices  124 us (42%)
  local copies, waits for them, and re-layouts  16.4 us (6%)
  matrix products  15.4 us (5%)
    ppermute x7, waiting for transfers between devices, on_device(): ahead = lax.ppermute(ahead, 'tensor', forward)  35.9 us
    all_to_all x1, waiting for transfers between devices, on_device(): lax.all_to_all(expert_rows, 'expert', split_axis=0, concat_axis=0, tiled=...  28.3 us
    ppermute x6, starting transfers between devices, on_device(): behind = lax.ppermute(behind, 'tensor', backward)  27.5 us
    all_to_all x1, starting transfers between devices, on_device(): lax.all_to_all(expert_rows, 'expert', split_axis=0, concat_axis=0, tiled=...  22.9 us
    ppermute x7, starting transfers between devices, on_device(): ahead = lax.ppermute(ahead, 'tensor', forward)  22.7 us
    ppermute x3, waiting for transfers between devices, on_device(): received[step] = lax.ppermute(front(ahead), 'tensor', toward(-step))  22.4 us
    all_to_all x1, waiting for transfers between devices, on_device(): lax.all_to_all(send, 'expert', split_axis=0, concat_axis=0, tiled=True)  21.7 us
    all_to_all x1, starting transfers between devices, on_device(): lax.all_to_all(send, 'expert', split_axis=0, concat_axis=0, tiled=True)  16 us
  transfers between devices with their start and end apart: 25, of which 13 were waited for; matrix products, arithmetic and copies ran while one was open for 8% of the time, Pallas kernels for 0%

profile of v8, /device:TPU:1, one launch (start us, length us, event | category | flops | bytes accessed | tf_op | source)
XLA Modules:
  0.0 294.2 jit_solution(14481180930707458700)
XLA Ops:
  0.0 4.1 %collective-permute-start.3 = (bf16[1024,512]{1,0:T(8,128)(2,1)}, bf16[1024,512]{1,0:T(8,128)(2,1)S(1)}, u32[]{:S(2)}, u32[]{:S(2)}) collective-permute-start(bf16[1024,512]{1,0:T(8,128)(2,1)} %bitcast.152), channel_id=1, source_target_pairs={{0,64},{64,128},{128,192},{192,256},{256,320},{320,384},{384,448},... | collective-permute-start | bytes 3145736 | tf_op jit(solution)/shard_map/ppermute | solution.py:60
  4.2 5.9 %all-to-all-start = ((bf16[8,8,4096]{2,1,0:T(8,128)(2,1)}), bf16[8,8,4096]{2,1,0:T(8,128)(2,1)S(1)}, u32[]{:S(2)}, u32[]{:S(2)}) async-start(bf16[8,8,4096]{2,1,0:T(8,128)(2,1)} %bitcast.155), calls=%async_computation | async-start | bytes 1048576 | tf_op jit(solution)/shard_map/all_to_all | solution.py:37
  10.1 4.6 %collective-permute-start = (bf16[1024,512]{1,0:T(8,128)(2,1)}, bf16[1024,512]{1,0:T(8,128)(2,1)}, u32[]{:S(2)}, u32[]{:S(2)}) collective-permute-start(bf16[1024,512]{1,0:T(8,128)(2,1)} %bitcast.153), channel_id=1, source_target_pairs={{0,448},{64,0},{128,64},{192,128},{256,192},{320,256},{384,320},{4... | collective-permute-start | bytes 3145736 | tf_op jit(solution)/shard_map/ppermute | solution.py:63
  15.5 8.5 %collective-permute-done.3 = bf16[1024,512]{1,0:T(8,128)(2,1)S(1)} collective-permute-done((bf16[1024,512]{1,0:T(8,128)(2,1)}, bf16[1024,512]{1,0:T(8,128)(2,1)S(1)}, u32[]{:S(2)}, u32[]{:S(2)}) %collective-permute-start.3) | collective-permute-done | bytes 1048608 | tf_op jit(solution)/shard_map/ppermute | solution.py:60
  24.0 7.9 %collective-permute-start.4 = (bf16[1024,512]{1,0:T(8,128)(2,1)S(1)}, bf16[1024,512]{1,0:T(8,128)(2,1)}, u32[]{:S(2)}, u32[]{:S(2)}) collective-permute-start(bf16[1024,512]{1,0:T(8,128)(2,1)S(1)} %collective-permute-done.3), channel_id=1, source_target_pairs={{0,64},{64,128},{128,192},{192,256},{256,320},{320,384},{384,448},... | collective-permute-start | bytes 3145736 | tf_op jit(solution)/shard_map/ppermute | solution.py:60
  32.0 6.8 %all-to-all-done = bf16[8,8,4096]{2,1,0:T(8,128)(2,1)S(1)} async-done(((bf16[8,8,4096]{2,1,0:T(8,128)(2,1)}), bf16[8,8,4096]{2,1,0:T(8,128)(2,1)S(1)}, u32[]{:S(2)}, u32[]{:S(2)}) %all-to-all-start) | async-done | bytes 524320 | tf_op jit(solution)/shard_map/all_to_all | solution.py:37
  40.1 4.3 %collective-permute-done = bf16[1024,512]{1,0:T(8,128)(2,1)} collective-permute-done((bf16[1024,512]{1,0:T(8,128)(2,1)}, bf16[1024,512]{1,0:T(8,128)(2,1)}, u32[]{:S(2)}, u32[]{:S(2)}) %collective-permute-start) | collective-permute-done | bytes 1048608 | tf_op jit(solution)/shard_map/ppermute | solution.py:63
  44.4 3.9 %collective-permute-start.1 = (bf16[1024,512]{1,0:T(8,128)(2,1)}, bf16[1024,512]{1,0:T(8,128)(2,1)}, u32[]{:S(2)}, u32[]{:S(2)}) collective-permute-start(bf16[1024,512]{1,0:T(8,128)(2,1)} %collective-permute-done), channel_id=1, source_target_pairs={{0,448},{64,0},{128,64},{192,128},{256,192},{320,256},{384,320},{4... | collective-permute-start | bytes 3145736 | tf_op jit(solution)/shard_map/ppermute | solution.py:63
  48.3 13.2 %collective-permute-done.4 = bf16[1024,512]{1,0:T(8,128)(2,1)} collective-permute-done((bf16[1024,512]{1,0:T(8,128)(2,1)S(1)}, bf16[1024,512]{1,0:T(8,128)(2,1)}, u32[]{:S(2)}, u32[]{:S(2)}) %collective-permute-start.4) | collective-permute-done | bytes 1048608 | tf_op jit(solution)/shard_map/ppermute | solution.py:60
  64.6 2.1 copy.149
  66.7 16.0 %all-to-all-start.1 = ((bf16[64,2,4096]{2,1,0:T(2,128)(2,1)}), bf16[64,2,4096]{2,1,0:T(2,128)(2,1)S(1)}, u32[]{:S(2)}, u32[]{:S(2)}) async-start(bf16[64,2,4096]{2,1,0:T(2,128)(2,1)} %copy.149), calls=%async_computation.1 | async-start | bytes 2097152 | tf_op jit(solution)/shard_map/all_to_all | solution.py:53
  82.8 4.9 %collective-permute-start.2 = (bf16[1024,512]{1,0:T(8,128)(2,1)}, bf16[1024,512]{1,0:T(8,128)(2,1)S(1)}, u32[]{:S(2)}, u32[]{:S(2)}) collective-permute-start(bf16[1024,512]{1,0:T(8,128)(2,1)} %collective-permute-done.1), channel_id=1, source_target_pairs={{0,448},{64,0},{128,64},{192,128},{256,192},{320,256},{384,320},{4... | collective-permute-start | bytes 3145736 | tf_op jit(solution)/shard_map/ppermute | solution.py:63
  89.6 21.7 %all-to-all-done.1 = bf16[64,2,4096]{2,1,0:T(2,128)(2,1)S(1)} async-done(((bf16[64,2,4096]{2,1,0:T(2,128)(2,1)}), bf16[64,2,4096]{2,1,0:T(2,128)(2,1)S(1)}, u32[]{:S(2)}, u32[]{:S(2)}) %all-to-all-start.1) | async-done | bytes 1048608 | tf_op jit(solution)/shard_map/all_to_all | solution.py:53
  113.4 4.3 %collective-permute-start.14 = (bf16[128,4096]{1,0:T(8,128)(2,1)S(1)}, bf16[128,4096]{1,0:T(8,128)(2,1)S(1)}, u32[]{:S(2)}, u32[]{:S(2)}) collective-permute-start(bf16[128,4096]{1,0:T(8,128)(2,1)S(1)} %reshape.59), channel_id=1, source_target_pairs={{0,448},{64,0},{128,64},{192,128},{256,192},{320,256},{384,320},{4... | collective-permute-start | bytes 3145736 | tf_op jit(solution)/shard_map/ppermute | solution.py:84
  129.7 13.5 %collective-permute-done.7 = bf16[128,4096]{1,0:T(8,128)(2,1)S(1)} collective-permute-done((bf16[128,4096]{1,0:T(8,128)(2,1)S(1)}, bf16[128,4096]{1,0:T(8,128)(2,1)S(1)}, u32[]{:S(2)}, u32[]{:S(2)}) %collective-permute-start.7) | collective-permute-done | bytes 1048608 | tf_op jit(solution)/shard_map/ppermute | solution.py:82
  145.5 4.6 %collective-permute-start.15 = (bf16[128,4096]{1,0:T(8,128)(2,1)S(1)}, bf16[128,4096]{1,0:T(8,128)(2,1)S(1)}, u32[]{:S(2)}, u32[]{:S(2)}) collective-permute-start(bf16[128,4096]{1,0:T(8,128)(2,1)S(1)} %collective-permute-done.14), channel_id=1, source_target_pairs={{0,448},{64,0},{128,64},{192,128},{256,192},{320,256},{384,320},{4... | collective-permute-start | bytes 3145736 | tf_op jit(solution)/shard_map/ppermute | solution.py:84
  153.3 3.4 %collective-permute-start.21 = (bf16[128,128]{1,0:T(8,128)(2,1)S(1)}, bf16[128,128]{1,0:T(8,128)(2,1)S(1)}, u32[]{:S(2)}, u32[]{:S(2)}) collective-permute-start(bf16[128,128]{1,0:T(8,128)(2,1)S(1)} %multiply_convert_fusion), channel_id=1, source_target_pairs={{0,64},{64,128},{128,192},{192,256},{256,320},{320,384},{384,448},... | collective-permute-start | bytes 98312 | tf_op jit(solution)/shard_map/ppermute | solution.py:85
  156.7 13.1 %collective-permute-done.8 = bf16[128,128]{1,0:T(8,128)(2,1)S(1)} collective-permute-done((bf16[128,128]{1,0:T(8,128)(2,1)S(1)}, bf16[128,128]{1,0:T(8,128)(2,1)S(1)}, u32[]{:S(2)}, u32[]{:S(2)}) %collective-permute-start.8) | collective-permute-done | bytes 32800 | tf_op jit(solution)/shard_map/ppermute | solution.py:83
  169.9 5.3 %collective-permute-start.16 = (bf16[128,4096]{1,0:T(8,128)(2,1)S(1)}, bf16[128,4096]{1,0:T(8,128)(2,1)S(1)}, u32[]{:S(2)}, u32[]{:S(2)}) collective-permute-start(bf16[128,4096]{1,0:T(8,128)(2,1)S(1)} %collective-permute-done.15), channel_id=1, source_target_pairs={{0,448},{64,0},{128,64},{192,128},{256,192},{320,256},{384,320},{4... | collective-permute-start | bytes 3145736 | tf_op jit(solution)/shard_map/ppermute | solution.py:84
  178.0 3.1 %collective-permute-start.11 = (bf16[128,4096]{1,0:T(8,128)(2,1)S(1)}, bf16[128,4096]{1,0:T(8,128)(2,1)S(1)}, u32[]{:S(2)}, u32[]{:S(2)}) collective-permute-start(bf16[128,4096]{1,0:T(8,128)(2,1)S(1)} %collective-permute-done.9), channel_id=1, source_target_pairs={{0,64},{64,128},{128,192},{192,256},{256,320},{320,384},{384,448},... | collective-permute-start | bytes 3145736 | tf_op jit(solution)/shard_map/ppermute | solution.py:82
  182.0 3.1 %collective-permute-start.20 = (bf16[128,128]{1,0:T(8,128)(2,1)S(1)}, bf16[128,128]{1,0:T(8,128)(2,1)S(1)}, u32[]{:S(2)}, u32[]{:S(2)}) collective-permute-start(bf16[128,128]{1,0:T(8,128)(2,1)S(1)} %multiply_convert_fusion.1), channel_id=1, source_target_pairs={{0,128},{64,192},{128,256},{192,320},{256,384},{320,448},{384,0},{... | collective-permute-start | bytes 98312 | tf_op jit(solution)/shard_map/ppermute | solution.py:85
  185.1 9.3 %collective-permute-done.10 = bf16[128,128]{1,0:T(8,128)(2,1)S(1)} collective-permute-done((bf16[128,128]{1,0:T(8,128)(2,1)S(1)}, bf16[128,128]{1,0:T(8,128)(2,1)S(1)}, u32[]{:S(2)}, u32[]{:S(2)}) %collective-permute-start.10) | collective-permute-done | bytes 32800 | tf_op jit(solution)/shard_map/ppermute | solution.py:83
  195.3 5.2 %collective-permute-start.19 = (bf16[128,128]{1,0:T(8,128)(2,1)S(1)}, bf16[128,128]{1,0:T(8,128)(2,1)S(1)}, u32[]{:S(2)}, u32[]{:S(2)}) collective-permute-start(bf16[128,128]{1,0:T(8,128)(2,1)S(1)} %multiply_convert_fusion.2), channel_id=1, source_target_pairs={{0,192},{64,256},{128,320},{192,384},{256,448},{320,0},{384,64},{4... | collective-permute-start | bytes 98312 | tf_op jit(solution)/shard_map/ppermute | solution.py:85
  200.5 4.9 %collective-permute-start.17 = (bf16[64,4096]{1,0:T(8,128)(2,1)S(1)}, bf16[64,4096]{1,0:T(8,128)(2,1)S(1)}, u32[]{:S(2)}, u32[]{:S(2)}) collective-permute-start(bf16[64,4096]{1,0:T(8,128)(2,1)S(1)} %slice.9), channel_id=1, source_target_pairs={{0,448},{64,0},{128,64},{192,128},{256,192},{320,256},{384,320},{4... | collective-permute-start | bytes 1572872 | tf_op jit(solution)/shard_map/ppermute | solution.py:88
  208.3 3.7 %collective-permute-done.17 = bf16[64,4096]{1,0:T(8,128)(2,1)S(1)} collective-permute-done((bf16[64,4096]{1,0:T(8,128)(2,1)S(1)}, bf16[64,4096]{1,0:T(8,128)(2,1)S(1)}, u32[]{:S(2)}, u32[]{:S(2)}) %collective-permute-start.17) | collective-permute-done | bytes 524320 | tf_op jit(solution)/shard_map/ppermute | solution.py:88
  214.6 9.0 %collective-permute-done.13 = bf16[64,4096]{1,0:T(8,128)(2,1)S(1)} collective-permute-done((bf16[64,4096]{1,0:T(8,128)(2,1)S(1)}, bf16[64,4096]{1,0:T(8,128)(2,1)S(1)}, u32[]{:S(2)}, u32[]{:S(2)}) %collective-permute-start.13) | collective-permute-done | bytes 524320 | tf_op jit(solution)/shard_map/ppermute | solution.py:87
  224.3 4.3 %collective-permute-start.18 = (bf16[128,128]{1,0:T(8,128)(2,1)S(1)}, bf16[128,128]{1,0:T(8,128)(2,1)S(1)}, u32[]{:S(2)}, u32[]{:S(2)}) collective-permute-start(bf16[128,128]{1,0:T(8,128)(2,1)S(1)} %pad_maximum_fusion), channel_id=1, source_target_pairs={{0,256},{64,320},{128,384},{192,448},{256,0},{320,64},{384,128},{4... | collective-permute-start | bytes 98312 | tf_op jit(solution)/shard_map/ppermute | solution.py:90
  228.7 4.3 %collective-permute-done.18 = bf16[128,128]{1,0:T(8,128)(2,1)S(1)} collective-permute-done((bf16[128,128]{1,0:T(8,128)(2,1)S(1)}, bf16[128,128]{1,0:T(8,128)(2,1)S(1)}, u32[]{:S(2)}, u32[]{:S(2)}) %collective-permute-start.18) | collective-permute-done | bytes 32800 | tf_op jit(solution)/shard_map/ppermute | solution.py:90
  233.4 4.7 %convolution_convert_fusion.1 = bf16[128,8,512]{2,0,1:T(8,128)(2,1)S(1)} fusion(bf16[128,1024,1]{0,1,2:T(8,128)(2,1)S(1)} %bitcast.151, bf16[8,1024,512]{2,1,0:T(8,128)(2,1)} %copy-done.2), kind=kOutput, calls=%fused_computation.5 | convolution fusion | flops 1074266112 | bytes 9699328 | tf_op jit(solution)/shard_map/sh,mhc->smc/dot_general | solution.py:93
  240.7 22.9 %all-to-all-start.2 = ((bf16[64,2,4096]{2,1,0:T(2,128)(2,1)}), bf16[64,2,4096]{2,1,0:T(2,128)(2,1)S(1)}, u32[]{:S(2)}, u32[]{:S(2)}) async-start(bf16[64,2,4096]{2,1,0:T(2,128)(2,1)} %reshape.61), calls=%async_computation.2 | async-start | bytes 2097152 | tf_op jit(solution)/shard_map/all_to_all | solution.py:98
  263.8 28.3 %all-to-all-done.2 = bf16[64,2,4096]{2,1,0:T(2,128)(2,1)S(1)} async-done(((bf16[64,2,4096]{2,1,0:T(2,128)(2,1)}), bf16[64,2,4096]{2,1,0:T(2,128)(2,1)S(1)}, u32[]{:S(2)}, u32[]{:S(2)}) %all-to-all-start.2) | async-done | bytes 1048608 | tf_op jit(solution)/shard_map/all_to_all | solution.py:98
  292.1 2.2 fusion
  (102 shorter events, 40.7 us)
Async XLA Ops:
  0.0 129.2 %copy-start = (bf16[1,4096,128]{2,1,0:T(8,128)(2,1)S(1)}, bf16[1,4096,128]{2,1,0:T(8,128)(2,1)}, u32[]{:S(2)}) copy-start(bf16[1,4096,128]{2,1,0:T(8,128)(2,1)} %param.12) | copy-start | bytes 3145732
  0.0 24.0 %collective-permute-start.3 = (bf16[1024,512]{1,0:T(8,128)(2,1)}, bf16[1024,512]{1,0:T(8,128)(2,1)S(1)}, u32[]{:S(2)}, u32[]{:S(2)}) collective-permute-start(bf16[1024,512]{1,0:T(8,128)(2,1)} %bitcast.152), channel_id=1, source_target_pairs={{0,64},{64,128},{128,192},{192,256},{256,320},{320,384},{384,448},... | collective-permute-start | bytes 3145736 | tf_op jit(solution)/shard_map/ppermute | solution.py:60
  4.2 34.6 %all-to-all-start = ((bf16[8,8,4096]{2,1,0:T(8,128)(2,1)}), bf16[8,8,4096]{2,1,0:T(8,128)(2,1)S(1)}, u32[]{:S(2)}, u32[]{:S(2)}) async-start(bf16[8,8,4096]{2,1,0:T(8,128)(2,1)} %bitcast.155), calls=%async_computation | async-start | bytes 1048576 | tf_op jit(solution)/shard_map/all_to_all | solution.py:37
  10.1 34.3 %collective-permute-start = (bf16[1024,512]{1,0:T(8,128)(2,1)}, bf16[1024,512]{1,0:T(8,128)(2,1)}, u32[]{:S(2)}, u32[]{:S(2)}) collective-permute-start(bf16[1024,512]{1,0:T(8,128)(2,1)} %bitcast.153), channel_id=1, source_target_pairs={{0,448},{64,0},{128,64},{192,128},{256,192},{320,256},{384,320},{4... | collective-permute-start | bytes 3145736 | tf_op jit(solution)/shard_map/ppermute | solution.py:63
  24.0 42.7 %copy-start.3 = (bf16[1024,512]{1,0:T(8,128)(2,1)}, bf16[1024,512]{1,0:T(8,128)(2,1)S(1)}, u32[]{:S(2)}) copy-start(bf16[1024,512]{1,0:T(8,128)(2,1)S(1)} %collective-permute-done.3) | copy-start | bytes 3145732
  24.0 37.5 %collective-permute-start.4 = (bf16[1024,512]{1,0:T(8,128)(2,1)S(1)}, bf16[1024,512]{1,0:T(8,128)(2,1)}, u32[]{:S(2)}, u32[]{:S(2)}) collective-permute-start(bf16[1024,512]{1,0:T(8,128)(2,1)S(1)} %collective-permute-done.3), channel_id=1, source_target_pairs={{0,64},{64,128},{128,192},{192,256},{256,320},{320,384},{384,448},... | collective-permute-start | bytes 3145736 | tf_op jit(solution)/shard_map/ppermute | solution.py:60
  44.4 38.3 %collective-permute-start.1 = (bf16[1024,512]{1,0:T(8,128)(2,1)}, bf16[1024,512]{1,0:T(8,128)(2,1)}, u32[]{:S(2)}, u32[]{:S(2)}) collective-permute-start(bf16[1024,512]{1,0:T(8,128)(2,1)} %collective-permute-done), channel_id=1, source_target_pairs={{0,448},{64,0},{128,64},{192,128},{256,192},{320,256},{384,320},{4... | collective-permute-start | bytes 3145736 | tf_op jit(solution)/shard_map/ppermute | solution.py:63
  61.5 26.1 %collective-permute-start.5 = (bf16[1024,512]{1,0:T(8,128)(2,1)}, bf16[1024,512]{1,0:T(8,128)(2,1)}, u32[]{:S(2)}, u32[]{:S(2)}) collective-permute-start(bf16[1024,512]{1,0:T(8,128)(2,1)} %collective-permute-done.4), channel_id=1, source_target_pairs={{0,64},{64,128},{128,192},{192,256},{256,320},{320,384},{384,448},... | collective-permute-start | bytes 3145736 | tf_op jit(solution)/shard_map/ppermute | solution.py:60
  66.7 44.6 %all-to-all-start.1 = ((bf16[64,2,4096]{2,1,0:T(2,128)(2,1)}), bf16[64,2,4096]{2,1,0:T(2,128)(2,1)S(1)}, u32[]{:S(2)}, u32[]{:S(2)}) async-start(bf16[64,2,4096]{2,1,0:T(2,128)(2,1)} %copy.149), calls=%async_computation.1 | async-start | bytes 2097152 | tf_op jit(solution)/shard_map/all_to_all | solution.py:53
  82.8 28.5 %collective-permute-start.2 = (bf16[1024,512]{1,0:T(8,128)(2,1)}, bf16[1024,512]{1,0:T(8,128)(2,1)S(1)}, u32[]{:S(2)}, u32[]{:S(2)}) collective-permute-start(bf16[1024,512]{1,0:T(8,128)(2,1)} %collective-permute-done.1), channel_id=1, source_target_pairs={{0,448},{64,0},{128,64},{192,128},{256,192},{320,256},{384,320},{4... | collective-permute-start | bytes 3145736 | tf_op jit(solution)/shard_map/ppermute | solution.py:63
  87.6 25.3 %collective-permute-start.6 = (bf16[1024,512]{1,0:T(8,128)(2,1)}, bf16[1024,512]{1,0:T(8,128)(2,1)}, u32[]{:S(2)}, u32[]{:S(2)}) collective-permute-start(bf16[1024,512]{1,0:T(8,128)(2,1)} %collective-permute-done.5), channel_id=1, source_target_pairs={{0,64},{64,128},{128,192},{192,256},{256,320},{320,384},{384,448},... | collective-permute-start | bytes 3145736 | tf_op jit(solution)/shard_map/ppermute | solution.py:60
  111.3 1.0 copy-start.5
  113.4 15.3 %copy-start.4 = (bf16[1024,512]{1,0:T(8,128)(2,1)S(1)}, bf16[1024,512]{1,0:T(8,128)(2,1)}, u32[]{:S(2)}) copy-start(bf16[1024,512]{1,0:T(8,128)(2,1)} %copy-done.3) | copy-start | bytes 3145732
  113.4 15.4 %copy-start.1 = (bf16[1,4096,128]{2,1,0:T(8,128)(2,1)S(1)}, bf16[1,4096,128]{2,1,0:T(8,128)(2,1)}, u32[]{:S(2)}) copy-start(bf16[1,4096,128]{2,1,0:T(8,128)(2,1)} %param.11) | copy-start | bytes 3145732
  113.4 32.2 %collective-permute-start.14 = (bf16[128,4096]{1,0:T(8,128)(2,1)S(1)}, bf16[128,4096]{1,0:T(8,128)(2,1)S(1)}, u32[]{:S(2)}, u32[]{:S(2)}) collective-permute-start(bf16[128,4096]{1,0:T(8,128)(2,1)S(1)} %reshape.59), channel_id=1, source_target_pairs={{0,448},{64,0},{128,64},{192,128},{256,192},{320,256},{384,320},{4... | collective-permute-start | bytes 3145736 | tf_op jit(solution)/shard_map/ppermute | solution.py:84
  117.7 25.5 %collective-permute-start.7 = (bf16[128,4096]{1,0:T(8,128)(2,1)S(1)}, bf16[128,4096]{1,0:T(8,128)(2,1)S(1)}, u32[]{:S(2)}, u32[]{:S(2)}) collective-permute-start(bf16[128,4096]{1,0:T(8,128)(2,1)S(1)} %reshape.59), channel_id=1, source_target_pairs={{0,64},{64,128},{128,192},{192,256},{256,320},{320,384},{384,448},... | collective-permute-start | bytes 3145736 | tf_op jit(solution)/shard_map/ppermute | solution.py:82
  128.8 47.3 %copy-start.2 = (bf16[8,1024,512]{2,1,0:T(8,128)(2,1)}, bf16[8,1024,512]{2,1,0:T(8,128)(2,1)S(1)}, u32[]{:S(2)}) copy-start(bf16[8,1024,512]{2,1,0:T(8,128)(2,1)S(1)} %bitcast_dynamic-update-slice_fusion) | copy-start | bytes 25165828
  143.2 32.0 %collective-permute-start.9 = (bf16[128,4096]{1,0:T(8,128)(2,1)S(1)}, bf16[128,4096]{1,0:T(8,128)(2,1)S(1)}, u32[]{:S(2)}, u32[]{:S(2)}) collective-permute-start(bf16[128,4096]{1,0:T(8,128)(2,1)S(1)} %collective-permute-done.7), channel_id=1, source_target_pairs={{0,64},{64,128},{128,192},{192,256},{256,320},{320,384},{384,448},... | collective-permute-start | bytes 3145736 | tf_op jit(solution)/shard_map/ppermute | solution.py:82
  145.5 24.3 %collective-permute-start.15 = (bf16[128,4096]{1,0:T(8,128)(2,1)S(1)}, bf16[128,4096]{1,0:T(8,128)(2,1)S(1)}, u32[]{:S(2)}, u32[]{:S(2)}) collective-permute-start(bf16[128,4096]{1,0:T(8,128)(2,1)S(1)} %collective-permute-done.14), channel_id=1, source_target_pairs={{0,448},{64,0},{128,64},{192,128},{256,192},{320,256},{384,320},{4... | collective-permute-start | bytes 3145736 | tf_op jit(solution)/shard_map/ppermute | solution.py:84
  150.6 19.3 %collective-permute-start.8 = (bf16[128,128]{1,0:T(8,128)(2,1)S(1)}, bf16[128,128]{1,0:T(8,128)(2,1)S(1)}, u32[]{:S(2)}, u32[]{:S(2)}) collective-permute-start(bf16[128,128]{1,0:T(8,128)(2,1)S(1)} %multiply_convert_fusion.5), channel_id=1, source_target_pairs={{0,448},{64,0},{128,64},{192,128},{256,192},{320,256},{384,320},{4... | collective-permute-start | bytes 98312 | tf_op jit(solution)/shard_map/ppermute | solution.py:83
  153.3 79.7 %collective-permute-start.21 = (bf16[128,128]{1,0:T(8,128)(2,1)S(1)}, bf16[128,128]{1,0:T(8,128)(2,1)S(1)}, u32[]{:S(2)}, u32[]{:S(2)}) collective-permute-start(bf16[128,128]{1,0:T(8,128)(2,1)S(1)} %multiply_convert_fusion), channel_id=1, source_target_pairs={{0,64},{64,128},{128,192},{192,256},{256,320},{320,384},{384,448},... | collective-permute-start | bytes 98312 | tf_op jit(solution)/shard_map/ppermute | solution.py:85
  169.9 24.6 %collective-permute-start.16 = (bf16[128,4096]{1,0:T(8,128)(2,1)S(1)}, bf16[128,4096]{1,0:T(8,128)(2,1)S(1)}, u32[]{:S(2)}, u32[]{:S(2)}) collective-permute-start(bf16[128,4096]{1,0:T(8,128)(2,1)S(1)} %collective-permute-done.15), channel_id=1, source_target_pairs={{0,448},{64,0},{128,64},{192,128},{256,192},{320,256},{384,320},{4... | collective-permute-start | bytes 3145736 | tf_op jit(solution)/shard_map/ppermute | solution.py:84
  176.1 18.3 %collective-permute-start.10 = (bf16[128,128]{1,0:T(8,128)(2,1)S(1)}, bf16[128,128]{1,0:T(8,128)(2,1)S(1)}, u32[]{:S(2)}, u32[]{:S(2)}) collective-permute-start(bf16[128,128]{1,0:T(8,128)(2,1)S(1)} %multiply_convert_fusion.4), channel_id=1, source_target_pairs={{0,384},{64,448},{128,0},{192,64},{256,128},{320,192},{384,256},{4... | collective-permute-start | bytes 98312 | tf_op jit(solution)/shard_map/ppermute | solution.py:83
  178.0 27.4 %collective-permute-start.11 = (bf16[128,4096]{1,0:T(8,128)(2,1)S(1)}, bf16[128,4096]{1,0:T(8,128)(2,1)S(1)}, u32[]{:S(2)}, u32[]{:S(2)}) collective-permute-start(bf16[128,4096]{1,0:T(8,128)(2,1)S(1)} %collective-permute-done.9), channel_id=1, source_target_pairs={{0,64},{64,128},{128,192},{192,256},{256,320},{320,384},{384,448},... | collective-permute-start | bytes 3145736 | tf_op jit(solution)/shard_map/ppermute | solution.py:82
  182.0 51.0 %collective-permute-start.20 = (bf16[128,128]{1,0:T(8,128)(2,1)S(1)}, bf16[128,128]{1,0:T(8,128)(2,1)S(1)}, u32[]{:S(2)}, u32[]{:S(2)}) collective-permute-start(bf16[128,128]{1,0:T(8,128)(2,1)S(1)} %multiply_convert_fusion.1), channel_id=1, source_target_pairs={{0,128},{64,192},{128,256},{192,320},{256,384},{320,448},{384,0},{... | collective-permute-start | bytes 98312 | tf_op jit(solution)/shard_map/ppermute | solution.py:85
  195.3 37.7 %collective-permute-start.19 = (bf16[128,128]{1,0:T(8,128)(2,1)S(1)}, bf16[128,128]{1,0:T(8,128)(2,1)S(1)}, u32[]{:S(2)}, u32[]{:S(2)}) collective-permute-start(bf16[128,128]{1,0:T(8,128)(2,1)S(1)} %multiply_convert_fusion.2), channel_id=1, source_target_pairs={{0,192},{64,256},{128,320},{192,384},{256,448},{320,0},{384,64},{4... | collective-permute-start | bytes 98312 | tf_op jit(solution)/shard_map/ppermute | solution.py:85
  200.5 11.5 %collective-permute-start.17 = (bf16[64,4096]{1,0:T(8,128)(2,1)S(1)}, bf16[64,4096]{1,0:T(8,128)(2,1)S(1)}, u32[]{:S(2)}, u32[]{:S(2)}) collective-permute-start(bf16[64,4096]{1,0:T(8,128)(2,1)S(1)} %slice.9), channel_id=1, source_target_pairs={{0,448},{64,0},{128,64},{192,128},{256,192},{320,256},{384,320},{4... | collective-permute-start | bytes 1572872 | tf_op jit(solution)/shard_map/ppermute | solution.py:88
  206.3 22.3 %collective-permute-start.12 = (bf16[128,128]{1,0:T(8,128)(2,1)S(1)}, bf16[128,128]{1,0:T(8,128)(2,1)S(1)}, u32[]{:S(2)}, u32[]{:S(2)}) collective-permute-start(bf16[128,128]{1,0:T(8,128)(2,1)S(1)} %multiply_convert_fusion.3), channel_id=1, source_target_pairs={{0,320},{64,384},{128,448},{192,0},{256,64},{320,128},{384,192},{4... | collective-permute-start | bytes 98312 | tf_op jit(solution)/shard_map/ppermute | solution.py:83
  212.0 11.6 %collective-permute-start.13 = (bf16[64,4096]{1,0:T(8,128)(2,1)S(1)}, bf16[64,4096]{1,0:T(8,128)(2,1)S(1)}, u32[]{:S(2)}, u32[]{:S(2)}) collective-permute-start(bf16[64,4096]{1,0:T(8,128)(2,1)S(1)} %slice.8), channel_id=1, source_target_pairs={{0,64},{64,128},{128,192},{192,256},{256,320},{320,384},{384,448},... | collective-permute-start | bytes 1572872 | tf_op jit(solution)/shard_map/ppermute | solution.py:87
  224.3 8.7 %collective-permute-start.18 = (bf16[128,128]{1,0:T(8,128)(2,1)S(1)}, bf16[128,128]{1,0:T(8,128)(2,1)S(1)}, u32[]{:S(2)}, u32[]{:S(2)}) collective-permute-start(bf16[128,128]{1,0:T(8,128)(2,1)S(1)} %pad_maximum_fusion), channel_id=1, source_target_pairs={{0,256},{64,320},{128,384},{192,448},{256,0},{320,64},{384,128},{4... | collective-permute-start | bytes 98312 | tf_op jit(solution)/shard_map/ppermute | solution.py:90
  233.4 30.1 %copy-start.6 = (f32[64,8]{0,1:T(8,128)S(1)}, f32[64,8]{0,1:T(8,128)}, u32[]{:S(2)}) copy-start(f32[64,8]{0,1:T(8,128)} %param.10) | copy-start | bytes 6148
  240.7 51.4 %all-to-all-start.2 = ((bf16[64,2,4096]{2,1,0:T(2,128)(2,1)}), bf16[64,2,4096]{2,1,0:T(2,128)(2,1)S(1)}, u32[]{:S(2)}, u32[]{:S(2)}) async-start(bf16[64,2,4096]{2,1,0:T(2,128)(2,1)} %reshape.61), calls=%async_computation.2 | async-start | bytes 2097152 | tf_op jit(solution)/shard_map/all_to_all | solution.py:98

commit v9 on v7

--- a/solution.py
+++ b/solution.py
@@ -56,12 +56,21 @@
     weight_parts = [down_matrix] + [None] * (tensor_count - 1)
     ahead = down_matrix
     behind = down_matrix
+    share = down_matrix.shape[0] // 2
     for step in range(1, tensor_count // 2 + 1):
-        ahead = lax.ppermute(ahead, "tensor", forward)
-        weight_parts[tensor_count - step] = ahead
         if step < tensor_count - step:
+            ahead = lax.ppermute(ahead, "tensor", forward)
+            weight_parts[tensor_count - step] = ahead
             behind = lax.ppermute(behind, "tensor", backward)
             weight_parts[step] = behind
+        else:
+            weight_parts[step] = jnp.concatenate(
+                [
+                    lax.ppermute(ahead[:share], "tensor", forward),
+                    lax.ppermute(behind[share:], "tensor", backward),
+                ],
+                axis=0,
+            )
     down_all = weight_parts
     def front(piece):
         gate_act = jnp.dot(piece, gate_matrix, preferred_element_type=jnp.float32)

time: 281 us -> 283 us (level)
    all_to_all x1, waiting for transfers between devices: 21.7 us -> 0.01 us  [on_device(): lax.all_to_all(send, 'expert', split_axis=0, concat_axis=0, tiled=True)]
    ppermute x7 -> x6, waiting for transfers between devices: 61.6 us -> 82.9 us  [on_device(): ahead = lax.ppermute(ahead, 'tensor', forward)]
    ppermute x7 -> x6, starting transfers between devices: 23.4 us -> 13.2 us  [on_device(): ahead = lax.ppermute(ahead, 'tensor', forward)]
    ppermute x0 -> x2, waiting for transfers between devices: none -> 8.57 us  [the longest x1 5.86 us: on_device(): lax.ppermute(ahead[:share], 'tensor', forward)]
    ppermute x6, waiting for transfers between devices: 8.15 us -> 0.02 us  [on_device(): behind = lax.ppermute(behind, 'tensor', backward)]
    ppermute x0 -> x2, starting transfers between devices: none -> 6.47 us  [the longest x1 4.56 us: on_device(): lax.ppermute(behind[share:], 'tensor', backward)]
    ppermute x1, waiting for transfers between devices: 4.05 us -> 0.87 us  [on_device(): second = lax.ppermute(behind[half:], 'tensor', backward)]
    unnamed x27 -> x33, local copies, waits for them, and re-layouts: 11.1 us -> 9.63 us
  transfers between devices with their start and end apart: 19 -> 20, of which waited for: 15 -> 12; matrix products, arithmetic and copies ran while one was open for 8% -> 8% of each run, Pallas kernels for 0% -> 0%
where the time goes in v9:
time: 283 us; the launch traced here: 282 us
  waiting for transfers between devices  137 us (48%)
  starting transfers between devices  104 us (37%)
  local copies, waits for them, and re-layouts  20.2 us (7%)
  matrix products  15.5 us (5%)
  other arithmetic  4 us (1%)
    ppermute x6, waiting for transfers between devices, on_device(): ahead = lax.ppermute(ahead, 'tensor', forward)  82.9 us
    all_to_all x1, waiting for transfers between devices, on_device(): lax.all_to_all(expert_rows, 'expert', split_axis=0, concat_axis=0, tiled=...  28.3 us
    ppermute x6, starting transfers between devices, on_device(): behind = lax.ppermute(behind, 'tensor', backward)  26.7 us
    all_to_all x1, starting transfers between devices, on_device(): lax.all_to_all(expert_rows, 'expert', split_axis=0, concat_axis=0, tiled=...  21.3 us
    all_to_all x1, starting transfers between devices, on_device(): lax.all_to_all(send, 'expert', split_axis=0, concat_axis=0, tiled=True)  15.7 us
    ppermute x6, starting transfers between devices, on_device(): ahead = lax.ppermute(ahead, 'tensor', forward)  13.2 us
    unnamed x33, local copies, waits for them, and re-layouts  9.63 us
    all_to_all x1, starting transfers between devices, on_device(): lax.all_to_all(attn_partial[0].reshape(tensor_count, row_count, feature_w...  7.77 us
  transfers between devices with their start and end apart: 20, of which 12 were waited for; matrix products, arithmetic and copies ran while one was open for 8% of the time, Pallas kernels for 0%

profile of v9, /device:TPU:1, one launch (start us, length us, event | category | flops | bytes accessed | tf_op | source)
XLA Modules:
  0.0 281.6 jit_solution(8169472640074740173)
XLA Ops:
  0.0 7.8 %all-to-all-start = ((bf16[8,8,4096]{2,1,0:T(8,128)(2,1)}), bf16[8,8,4096]{2,1,0:T(8,128)(2,1)S(1)}, u32[]{:S(2)}, u32[]{:S(2)}) async-start(bf16[8,8,4096]{2,1,0:T(8,128)(2,1)} %bitcast.160), calls=%async_computation | async-start | bytes 1048576 | tf_op jit(solution)/shard_map/all_to_all | solution.py:37
  7.8 3.4 %collective-permute-start.3 = (bf16[1024,512]{1,0:T(8,128)(2,1)}, bf16[1024,512]{1,0:T(8,128)(2,1)S(1)}, u32[]{:S(2)}, u32[]{:S(2)}) collective-permute-start(bf16[1024,512]{1,0:T(8,128)(2,1)} %bitcast.156), channel_id=1, source_target_pairs={{0,64},{64,128},{128,192},{192,256},{256,320},{320,384},{384,448},... | collective-permute-start | bytes 3145736 | tf_op jit(solution)/shard_map/ppermute | solution.py:62
  11.1 3.1 %collective-permute-start = (bf16[1024,512]{1,0:T(8,128)(2,1)}, bf16[1024,512]{1,0:T(8,128)(2,1)}, u32[]{:S(2)}, u32[]{:S(2)}) collective-permute-start(bf16[1024,512]{1,0:T(8,128)(2,1)} %bitcast.157), channel_id=1, source_target_pairs={{0,448},{64,0},{128,64},{192,128},{256,192},{320,256},{384,320},{4... | collective-permute-start | bytes 3145736 | tf_op jit(solution)/shard_map/ppermute | solution.py:64
  15.3 7.5 %all-to-all-done = bf16[8,8,4096]{2,1,0:T(8,128)(2,1)S(1)} async-done(((bf16[8,8,4096]{2,1,0:T(8,128)(2,1)}), bf16[8,8,4096]{2,1,0:T(8,128)(2,1)S(1)}, u32[]{:S(2)}, u32[]{:S(2)}) %all-to-all-start) | async-done | bytes 524320 | tf_op jit(solution)/shard_map/all_to_all | solution.py:37
  22.9 21.4 %collective-permute-done.3 = bf16[1024,512]{1,0:T(8,128)(2,1)S(1)} collective-permute-done((bf16[1024,512]{1,0:T(8,128)(2,1)}, bf16[1024,512]{1,0:T(8,128)(2,1)S(1)}, u32[]{:S(2)}, u32[]{:S(2)}) %collective-permute-start.3) | collective-permute-done | bytes 1048608 | tf_op jit(solution)/shard_map/ppermute | solution.py:62
  46.3 4.6 %collective-permute-start.1 = (bf16[1024,512]{1,0:T(8,128)(2,1)}, bf16[1024,512]{1,0:T(8,128)(2,1)}, u32[]{:S(2)}, u32[]{:S(2)}) collective-permute-start(bf16[1024,512]{1,0:T(8,128)(2,1)} %collective-permute-done), channel_id=1, source_target_pairs={{0,448},{64,0},{128,64},{192,128},{256,192},{320,256},{384,320},{4... | collective-permute-start | bytes 3145736 | tf_op jit(solution)/shard_map/ppermute | solution.py:64
  53.2 2.1 copy.43
  55.2 15.7 %all-to-all-start.1 = ((bf16[64,2,4096]{2,1,0:T(2,128)(2,1)}), bf16[64,2,4096]{2,1,0:T(2,128)(2,1)}, u32[]{:S(2)}, u32[]{:S(2)}) async-start(bf16[64,2,4096]{2,1,0:T(2,128)(2,1)} %copy.43), calls=%async_computation.1 | async-start | bytes 2097152 | tf_op jit(solution)/shard_map/all_to_all | solution.py:53
  71.0 2.1 collective-permute-start.5
  73.1 4.6 %collective-permute-start.2 = (bf16[1024,512]{1,0:T(8,128)(2,1)}, bf16[1024,512]{1,0:T(8,128)(2,1)S(1)}, u32[]{:S(2)}, u32[]{:S(2)}) collective-permute-start(bf16[1024,512]{1,0:T(8,128)(2,1)} %collective-permute-done.1), channel_id=1, source_target_pairs={{0,448},{64,0},{128,64},{192,128},{256,192},{320,256},{384,320},{4... | collective-permute-start | bytes 3145736 | tf_op jit(solution)/shard_map/ppermute | solution.py:64
  77.7 19.7 %collective-permute-done.5 = bf16[1024,512]{1,0:T(8,128)(2,1)S(1)} collective-permute-done((bf16[1024,512]{1,0:T(8,128)(2,1)}, bf16[1024,512]{1,0:T(8,128)(2,1)S(1)}, u32[]{:S(2)}, u32[]{:S(2)}) %collective-permute-start.5) | collective-permute-done | bytes 1048608 | tf_op jit(solution)/shard_map/ppermute | solution.py:62
  102.9 4.6 %collective-permute-start.7 = (bf16[512,512]{1,0:T(8,128)(2,1)}, bf16[512,512]{1,0:T(8,128)(2,1)}, u32[]{:S(2)}, u32[]{:S(2)}) collective-permute-start(bf16[512,512]{1,0:T(8,128)(2,1)} %slice.17), channel_id=1, source_target_pairs={{0,448},{64,0},{128,64},{192,128},{256,192},{320,256},{384,320},{4... | collective-permute-start | bytes 1572872 | tf_op jit(solution)/shard_map/ppermute | solution.py:70
  107.5 5.9 %collective-permute-done.6 = bf16[512,512]{1,0:T(8,128)(2,1)} collective-permute-done((bf16[512,512]{1,0:T(8,128)(2,1)}, bf16[512,512]{1,0:T(8,128)(2,1)}, u32[]{:S(2)}, u32[]{:S(2)}) %collective-permute-start.6) | collective-permute-done | bytes 524320 | tf_op jit(solution)/shard_map/ppermute | solution.py:69
  113.3 2.7 collective-permute-done.7
  116.0 2.2 pad_maximum_fusion
  119.8 2.1 collective-permute-start.11
  121.8 5.3 %collective-permute-start.8 = (bf16[128,4096]{1,0:T(8,128)(2,1)S(1)}, bf16[128,4096]{1,0:T(8,128)(2,1)S(1)}, u32[]{:S(2)}, u32[]{:S(2)}) collective-permute-start(bf16[128,4096]{1,0:T(8,128)(2,1)S(1)} %reshape.57), channel_id=1, source_target_pairs={{0,448},{64,0},{128,64},{192,128},{256,192},{320,256},{384,320},{4... | collective-permute-start | bytes 3145736 | tf_op jit(solution)/shard_map/ppermute | solution.py:90
  132.9 12.0 %collective-permute-done.11 = bf16[128,4096]{1,0:T(8,128)(2,1)S(1)} collective-permute-done((bf16[128,4096]{1,0:T(8,128)(2,1)S(1)}, bf16[128,4096]{1,0:T(8,128)(2,1)S(1)}, u32[]{:S(2)}, u32[]{:S(2)}) %collective-permute-start.11) | collective-permute-done | bytes 1048608 | tf_op jit(solution)/shard_map/ppermute | solution.py:88
  146.8 4.6 %collective-permute-start.9 = (bf16[128,4096]{1,0:T(8,128)(2,1)S(1)}, bf16[128,4096]{1,0:T(8,128)(2,1)S(1)}, u32[]{:S(2)}, u32[]{:S(2)}) collective-permute-start(bf16[128,4096]{1,0:T(8,128)(2,1)S(1)} %collective-permute-done.8), channel_id=1, source_target_pairs={{0,448},{64,0},{128,64},{192,128},{256,192},{320,256},{384,320},{4... | collective-permute-start | bytes 3145736 | tf_op jit(solution)/shard_map/ppermute | solution.py:90
  152.8 15.5 %collective-permute-done.12 = bf16[128,4096]{1,0:T(8,128)(2,1)S(1)} collective-permute-done((bf16[128,4096]{1,0:T(8,128)(2,1)S(1)}, bf16[128,4096]{1,0:T(8,128)(2,1)S(1)}, u32[]{:S(2)}, u32[]{:S(2)}) %collective-permute-start.12) | collective-permute-done | bytes 1048608 | tf_op jit(solution)/shard_map/ppermute | solution.py:88
  170.2 4.6 %collective-permute-start.10 = (bf16[128,4096]{1,0:T(8,128)(2,1)S(1)}, bf16[128,4096]{1,0:T(8,128)(2,1)S(1)}, u32[]{:S(2)}, u32[]{:S(2)}) collective-permute-start(bf16[128,4096]{1,0:T(8,128)(2,1)S(1)} %collective-permute-done.9), channel_id=1, source_target_pairs={{0,448},{64,0},{128,64},{192,128},{256,192},{320,256},{384,320},{4... | collective-permute-start | bytes 3145736 | tf_op jit(solution)/shard_map/ppermute | solution.py:90
  176.5 14.3 %collective-permute-done.13 = bf16[128,4096]{1,0:T(8,128)(2,1)S(1)} collective-permute-done((bf16[128,4096]{1,0:T(8,128)(2,1)S(1)}, bf16[128,4096]{1,0:T(8,128)(2,1)S(1)}, u32[]{:S(2)}, u32[]{:S(2)}) %collective-permute-start.13) | collective-permute-done | bytes 1048608 | tf_op jit(solution)/shard_map/ppermute | solution.py:88
  190.9 1.9 collective-permute-start.14
  192.9 4.8 %collective-permute-start.15 = (bf16[64,4096]{1,0:T(8,128)(2,1)S(1)}, bf16[64,4096]{1,0:T(8,128)(2,1)S(1)}, u32[]{:S(2)}, u32[]{:S(2)}) collective-permute-start(bf16[64,4096]{1,0:T(8,128)(2,1)S(1)} %slice.19), channel_id=1, source_target_pairs={{0,448},{64,0},{128,64},{192,128},{256,192},{320,256},{384,320},{4... | collective-permute-start | bytes 1572872 | tf_op jit(solution)/shard_map/ppermute | solution.py:94
  198.9 3.0 %collective-permute-done.14 = bf16[64,4096]{1,0:T(8,128)(2,1)S(1)} collective-permute-done((bf16[64,4096]{1,0:T(8,128)(2,1)S(1)}, bf16[64,4096]{1,0:T(8,128)(2,1)S(1)}, u32[]{:S(2)}, u32[]{:S(2)}) %collective-permute-start.14) | collective-permute-done | bytes 524320 | tf_op jit(solution)/shard_map/ppermute | solution.py:93
  206.4 6.4 %all-to-all-start.2 = ((bf16[8,128,128]{2,1,0:T(8,128)(2,1)}), bf16[8,128,128]{2,1,0:T(8,128)(2,1)S(1)}, u32[]{:S(2)}, u32[]{:S(2)}) async-start(bf16[8,128,128]{2,1,0:T(8,128)(2,1)} %constant_dynamic-slice_fusion), calls=%async_computation.2 | async-start | bytes 524288 | tf_op jit(solution)/shard_map/all_to_all | solution.py:97
  212.8 2.3 bitcast_dynamic-update-slice_fusion.1
  216.2 5.9 %all-to-all-done.2 = bf16[8,128,128]{2,1,0:T(8,128)(2,1)S(1)} async-done(((bf16[8,128,128]{2,1,0:T(8,128)(2,1)}), bf16[8,128,128]{2,1,0:T(8,128)(2,1)S(1)}, u32[]{:S(2)}, u32[]{:S(2)}) %all-to-all-start.2) | async-done | bytes 262176 | tf_op jit(solution)/shard_map/all_to_all | solution.py:97
  222.4 4.7 %convolution_convert_fusion.1 = bf16[128,8,512]{2,0,1:T(8,128)(2,1)S(1)} fusion(bf16[128,1024,1]{0,1,2:T(8,128)(2,1)S(1)} %bitcast.155, bf16[8,1024,512]{2,1,0:T(8,128)(2,1)} %bitcast_dynamic-update-slice_fusion), kind=kOutput, calls=%fused_computation.5 | convolution fusion | flops 1074266112 | bytes 9699328 | tf_op jit(solution)/shard_map/sh,mhc->smc/dot_general | solution.py:101
  229.6 21.3 %all-to-all-start.3 = ((bf16[64,2,4096]{2,1,0:T(2,128)(2,1)}), bf16[64,2,4096]{2,1,0:T(2,128)(2,1)S(1)}, u32[]{:S(2)}, u32[]{:S(2)}) async-start(bf16[64,2,4096]{2,1,0:T(2,128)(2,1)} %reshape.58), calls=%async_computation.3 | async-start | bytes 2097152 | tf_op jit(solution)/shard_map/all_to_all | solution.py:106
  251.2 28.3 %all-to-all-done.3 = bf16[64,2,4096]{2,1,0:T(2,128)(2,1)S(1)} async-done(((bf16[64,2,4096]{2,1,0:T(2,128)(2,1)}), bf16[64,2,4096]{2,1,0:T(2,128)(2,1)S(1)}, u32[]{:S(2)}, u32[]{:S(2)}) %all-to-all-start.3) | async-done | bytes 1048608 | tf_op jit(solution)/shard_map/all_to_all | solution.py:106
  279.5 2.2 fusion
  (94 shorter events, 34.8 us)
Async XLA Ops:
  0.0 151.5 %copy-start = (bf16[1,4096,128]{2,1,0:T(8,128)(2,1)S(1)}, bf16[1,4096,128]{2,1,0:T(8,128)(2,1)}, u32[]{:S(2)}) copy-start(bf16[1,4096,128]{2,1,0:T(8,128)(2,1)} %param.12) | copy-start | bytes 3145732
  0.0 22.7 %all-to-all-start = ((bf16[8,8,4096]{2,1,0:T(8,128)(2,1)}), bf16[8,8,4096]{2,1,0:T(8,128)(2,1)S(1)}, u32[]{:S(2)}, u32[]{:S(2)}) async-start(bf16[8,8,4096]{2,1,0:T(8,128)(2,1)} %bitcast.160), calls=%async_computation | async-start | bytes 1048576 | tf_op jit(solution)/shard_map/all_to_all | solution.py:37
  7.8 36.6 %collective-permute-start.3 = (bf16[1024,512]{1,0:T(8,128)(2,1)}, bf16[1024,512]{1,0:T(8,128)(2,1)S(1)}, u32[]{:S(2)}, u32[]{:S(2)}) collective-permute-start(bf16[1024,512]{1,0:T(8,128)(2,1)} %bitcast.156), channel_id=1, source_target_pairs={{0,64},{64,128},{128,192},{192,256},{256,320},{320,384},{384,448},... | collective-permute-start | bytes 3145736 | tf_op jit(solution)/shard_map/ppermute | solution.py:62
  11.1 35.1 %collective-permute-start = (bf16[1024,512]{1,0:T(8,128)(2,1)}, bf16[1024,512]{1,0:T(8,128)(2,1)}, u32[]{:S(2)}, u32[]{:S(2)}) collective-permute-start(bf16[1024,512]{1,0:T(8,128)(2,1)} %bitcast.157), channel_id=1, source_target_pairs={{0,448},{64,0},{128,64},{192,128},{256,192},{320,256},{384,320},{4... | collective-permute-start | bytes 3145736 | tf_op jit(solution)/shard_map/ppermute | solution.py:64
  44.3 73.9 %copy-start.7 = (bf16[1024,512]{1,0:T(8,128)(2,1)}, bf16[1024,512]{1,0:T(8,128)(2,1)S(1)}, u32[]{:S(2)}) copy-start(bf16[1024,512]{1,0:T(8,128)(2,1)S(1)} %collective-permute-done.3) | copy-start | bytes 3145732
  44.3 26.7 %collective-permute-start.4 = (bf16[1024,512]{1,0:T(8,128)(2,1)S(1)}, bf16[1024,512]{1,0:T(8,128)(2,1)}, u32[]{:S(2)}, u32[]{:S(2)}) collective-permute-start(bf16[1024,512]{1,0:T(8,128)(2,1)S(1)} %collective-permute-done.3), channel_id=1, source_target_pairs={{0,64},{64,128},{128,192},{192,256},{256,320},{320,384},{384,448},... | collective-permute-start | bytes 3145736 | tf_op jit(solution)/shard_map/ppermute | solution.py:62
  46.3 26.8 %collective-permute-start.1 = (bf16[1024,512]{1,0:T(8,128)(2,1)}, bf16[1024,512]{1,0:T(8,128)(2,1)}, u32[]{:S(2)}, u32[]{:S(2)}) collective-permute-start(bf16[1024,512]{1,0:T(8,128)(2,1)} %collective-permute-done), channel_id=1, source_target_pairs={{0,448},{64,0},{128,64},{192,128},{256,192},{320,256},{384,320},{4... | collective-permute-start | bytes 3145736 | tf_op jit(solution)/shard_map/ppermute | solution.py:64
  55.2 63.0 %all-to-all-start.1 = ((bf16[64,2,4096]{2,1,0:T(2,128)(2,1)}), bf16[64,2,4096]{2,1,0:T(2,128)(2,1)}, u32[]{:S(2)}, u32[]{:S(2)}) async-start(bf16[64,2,4096]{2,1,0:T(2,128)(2,1)} %copy.43), calls=%async_computation.1 | async-start | bytes 2097152 | tf_op jit(solution)/shard_map/all_to_all | solution.py:53
  71.0 61.4 %copy-start.1 = (bf16[1,4096,128]{2,1,0:T(8,128)(2,1)S(1)}, bf16[1,4096,128]{2,1,0:T(8,128)(2,1)}, u32[]{:S(2)}) copy-start(bf16[1,4096,128]{2,1,0:T(8,128)(2,1)} %param.11) | copy-start | bytes 3145732
  71.0 26.3 %collective-permute-start.5 = (bf16[1024,512]{1,0:T(8,128)(2,1)}, bf16[1024,512]{1,0:T(8,128)(2,1)S(1)}, u32[]{:S(2)}, u32[]{:S(2)}) collective-permute-start(bf16[1024,512]{1,0:T(8,128)(2,1)} %collective-permute-done.4), channel_id=1, source_target_pairs={{0,64},{64,128},{128,192},{192,256},{256,320},{320,384},{384,448},... | collective-permute-start | bytes 3145736 | tf_op jit(solution)/shard_map/ppermute | solution.py:62
  73.1 28.0 %collective-permute-start.2 = (bf16[1024,512]{1,0:T(8,128)(2,1)}, bf16[1024,512]{1,0:T(8,128)(2,1)S(1)}, u32[]{:S(2)}, u32[]{:S(2)}) collective-permute-start(bf16[1024,512]{1,0:T(8,128)(2,1)} %collective-permute-done.1), channel_id=1, source_target_pairs={{0,448},{64,0},{128,64},{192,128},{256,192},{320,256},{384,320},{4... | collective-permute-start | bytes 3145736 | tf_op jit(solution)/shard_map/ppermute | solution.py:64
  97.3 1.0 copy-start.4
  99.1 14.2 %collective-permute-start.6 = (bf16[512,512]{1,0:T(8,128)(2,1)}, bf16[512,512]{1,0:T(8,128)(2,1)}, u32[]{:S(2)}, u32[]{:S(2)}) collective-permute-start(bf16[512,512]{1,0:T(8,128)(2,1)} %slice.16), channel_id=1, source_target_pairs={{0,64},{64,128},{128,192},{192,256},{256,320},{320,384},{384,448},... | collective-permute-start | bytes 1572872 | tf_op jit(solution)/shard_map/ppermute | solution.py:69
  101.1 1.0 copy-start.6
  102.9 13.2 %collective-permute-start.7 = (bf16[512,512]{1,0:T(8,128)(2,1)}, bf16[512,512]{1,0:T(8,128)(2,1)}, u32[]{:S(2)}, u32[]{:S(2)}) collective-permute-start(bf16[512,512]{1,0:T(8,128)(2,1)} %slice.17), channel_id=1, source_target_pairs={{0,448},{64,0},{128,64},{192,128},{256,192},{320,256},{384,320},{4... | collective-permute-start | bytes 1572872 | tf_op jit(solution)/shard_map/ppermute | solution.py:70
  119.7 12.6 %copy-start.3 = (bf16[1024,512]{1,0:T(8,128)(2,1)S(1)}, bf16[1024,512]{1,0:T(8,128)(2,1)}, u32[]{:S(2)}) copy-start(bf16[1024,512]{1,0:T(8,128)(2,1)} %pad_maximum_fusion) | copy-start | bytes 3145732
  119.8 31.7 %copy-start.5 = (bf16[1024,512]{1,0:T(8,128)(2,1)S(1)}, bf16[1024,512]{1,0:T(8,128)(2,1)}, u32[]{:S(2)}) copy-start(bf16[1024,512]{1,0:T(8,128)(2,1)} %copy-done.4) | copy-start | bytes 3145732
  119.8 25.1 %collective-permute-start.11 = (bf16[128,4096]{1,0:T(8,128)(2,1)S(1)}, bf16[128,4096]{1,0:T(8,128)(2,1)S(1)}, u32[]{:S(2)}, u32[]{:S(2)}) collective-permute-start(bf16[128,4096]{1,0:T(8,128)(2,1)S(1)} %reshape.57), channel_id=1, source_target_pairs={{0,64},{64,128},{128,192},{192,256},{256,320},{320,384},{384,448},... | collective-permute-start | bytes 3145736 | tf_op jit(solution)/shard_map/ppermute | solution.py:88
  121.8 25.0 %collective-permute-start.8 = (bf16[128,4096]{1,0:T(8,128)(2,1)S(1)}, bf16[128,4096]{1,0:T(8,128)(2,1)S(1)}, u32[]{:S(2)}, u32[]{:S(2)}) collective-permute-start(bf16[128,4096]{1,0:T(8,128)(2,1)S(1)} %reshape.57), channel_id=1, source_target_pairs={{0,448},{64,0},{128,64},{192,128},{256,192},{320,256},{384,320},{4... | collective-permute-start | bytes 3145736 | tf_op jit(solution)/shard_map/ppermute | solution.py:90
  144.9 23.4 %collective-permute-start.12 = (bf16[128,4096]{1,0:T(8,128)(2,1)S(1)}, bf16[128,4096]{1,0:T(8,128)(2,1)S(1)}, u32[]{:S(2)}, u32[]{:S(2)}) collective-permute-start(bf16[128,4096]{1,0:T(8,128)(2,1)S(1)} %collective-permute-done.11), channel_id=1, source_target_pairs={{0,64},{64,128},{128,192},{192,256},{256,320},{320,384},{384,448},... | collective-permute-start | bytes 3145736 | tf_op jit(solution)/shard_map/ppermute | solution.py:88
  146.8 23.4 %collective-permute-start.9 = (bf16[128,4096]{1,0:T(8,128)(2,1)S(1)}, bf16[128,4096]{1,0:T(8,128)(2,1)S(1)}, u32[]{:S(2)}, u32[]{:S(2)}) collective-permute-start(bf16[128,4096]{1,0:T(8,128)(2,1)S(1)} %collective-permute-done.8), channel_id=1, source_target_pairs={{0,448},{64,0},{128,64},{192,128},{256,192},{320,256},{384,320},{4... | collective-permute-start | bytes 3145736 | tf_op jit(solution)/shard_map/ppermute | solution.py:90
  151.5 41.3 %copy-start.2 = (bf16[8,1024,512]{2,1,0:T(8,128)(2,1)}, bf16[8,1024,512]{2,1,0:T(8,128)(2,1)S(1)}, u32[]{:S(2)}) copy-start(bf16[8,1024,512]{2,1,0:T(8,128)(2,1)S(1)} %bitcast_dynamic-update-slice_fusion.2) | copy-start | bytes 25165828
  168.3 22.5 %collective-permute-start.13 = (bf16[128,4096]{1,0:T(8,128)(2,1)S(1)}, bf16[128,4096]{1,0:T(8,128)(2,1)S(1)}, u32[]{:S(2)}, u32[]{:S(2)}) collective-permute-start(bf16[128,4096]{1,0:T(8,128)(2,1)S(1)} %collective-permute-done.12), channel_id=1, source_target_pairs={{0,64},{64,128},{128,192},{192,256},{256,320},{320,384},{384,448},... | collective-permute-start | bytes 3145736 | tf_op jit(solution)/shard_map/ppermute | solution.py:88
  170.2 22.6 %collective-permute-start.10 = (bf16[128,4096]{1,0:T(8,128)(2,1)S(1)}, bf16[128,4096]{1,0:T(8,128)(2,1)S(1)}, u32[]{:S(2)}, u32[]{:S(2)}) collective-permute-start(bf16[128,4096]{1,0:T(8,128)(2,1)S(1)} %collective-permute-done.9), channel_id=1, source_target_pairs={{0,448},{64,0},{128,64},{192,128},{256,192},{320,256},{384,320},{4... | collective-permute-start | bytes 3145736 | tf_op jit(solution)/shard_map/ppermute | solution.py:90
  190.9 11.1 %collective-permute-start.14 = (bf16[64,4096]{1,0:T(8,128)(2,1)S(1)}, bf16[64,4096]{1,0:T(8,128)(2,1)S(1)}, u32[]{:S(2)}, u32[]{:S(2)}) collective-permute-start(bf16[64,4096]{1,0:T(8,128)(2,1)S(1)} %slice.18), channel_id=1, source_target_pairs={{0,64},{64,128},{128,192},{192,256},{256,320},{320,384},{384,448},... | collective-permute-start | bytes 1572872 | tf_op jit(solution)/shard_map/ppermute | solution.py:93
  192.9 10.7 %collective-permute-start.15 = (bf16[64,4096]{1,0:T(8,128)(2,1)S(1)}, bf16[64,4096]{1,0:T(8,128)(2,1)S(1)}, u32[]{:S(2)}, u32[]{:S(2)}) collective-permute-start(bf16[64,4096]{1,0:T(8,128)(2,1)S(1)} %slice.19), channel_id=1, source_target_pairs={{0,448},{64,0},{128,64},{192,128},{256,192},{320,256},{384,320},{4... | collective-permute-start | bytes 1572872 | tf_op jit(solution)/shard_map/ppermute | solution.py:94
  198.9 16.2 %copy-start.8 = (bf16[1024,512]{1,0:T(8,128)(2,1)S(1)}, bf16[1024,512]{1,0:T(8,128)(2,1)}, u32[]{:S(2)}) copy-start(bf16[1024,512]{1,0:T(8,128)(2,1)} %copy-done.7) | copy-start | bytes 3145732
  206.4 15.8 %all-to-all-start.2 = ((bf16[8,128,128]{2,1,0:T(8,128)(2,1)}), bf16[8,128,128]{2,1,0:T(8,128)(2,1)S(1)}, u32[]{:S(2)}, u32[]{:S(2)}) async-start(bf16[8,128,128]{2,1,0:T(8,128)(2,1)} %constant_dynamic-slice_fusion), calls=%async_computation.2 | async-start | bytes 524288 | tf_op jit(solution)/shard_map/all_to_all | solution.py:97
  222.4 28.6 %copy-start.9 = (f32[64,8]{0,1:T(8,128)S(1)}, f32[64,8]{0,1:T(8,128)}, u32[]{:S(2)}) copy-start(f32[64,8]{0,1:T(8,128)} %param.10) | copy-start | bytes 6148
  229.6 49.8 %all-to-all-start.3 = ((bf16[64,2,4096]{2,1,0:T(2,128)(2,1)}), bf16[64,2,4096]{2,1,0:T(2,128)(2,1)S(1)}, u32[]{:S(2)}, u32[]{:S(2)}) async-start(bf16[64,2,4096]{2,1,0:T(2,128)(2,1)} %reshape.58), calls=%async_computation.3 | async-start | bytes 2097152 | tf_op jit(solution)/shard_map/all_to_all | solution.py:106

commit v10 on v7

--- a/solution.py
+++ b/solution.py
@@ -68,7 +68,6 @@
         up_act = jnp.dot(piece, up_matrix, preferred_element_type=jnp.float32)
         return (jax.nn.silu(gate_act) * up_act).astype(jnp.bfloat16)
 
-    down_all, recv = lax.optimization_barrier((down_all, recv))
     own_rows = recv.reshape(expert_count * capacity, feature_width)
     hidden_parts = [front(own_rows)] + [None] * (tensor_count - 1)
     ahead = own_rows

time: 281 us -> 282 us (level)
  starting transfers between devices: 103 us -> 95.8 us
  local copies, waits for them, and re-layouts: 20.1 us -> 25 us
  waiting for transfers between devices: 139 us -> 143 us
    all_to_all x1, waiting for transfers between devices: 21.7 us -> 0.01 us  [on_device(): lax.all_to_all(send, 'expert', split_axis=0, concat_axis=0, tiled=True)]
    ppermute x7, waiting for transfers between devices: 61.6 us -> 78.3 us  [on_device(): ahead = lax.ppermute(ahead, 'tensor', forward)]
    ppermute x6, waiting for transfers between devices: 8.15 us -> 19 us  [on_device(): behind = lax.ppermute(behind, 'tensor', backward)]
    ppermute x7, starting transfers between devices: 23.4 us -> 17.2 us  [on_device(): ahead = lax.ppermute(ahead, 'tensor', forward)]
    ppermute x1, waiting for transfers between devices: 4.05 us -> 0.29 us  [on_device(): second = lax.ppermute(behind[half:], 'tensor', backward)]
    unnamed x27 -> x19, local copies, waits for them, and re-layouts: 11.1 us -> 14.8 us
  transfers between devices with their start and end apart: 19 -> 19, of which waited for: 15 -> 11; matrix products, arithmetic and copies ran while one was open for 8% -> 11% of each run, Pallas kernels for 0% -> 0%
where the time goes in v10:
time: 282 us; the launch traced here: 281 us
  waiting for transfers between devices  143 us (51%)
  starting transfers between devices  95.8 us (34%)
  local copies, waits for them, and re-layouts  25 us (9%)
  matrix products  15.4 us (5%)
    ppermute x7, waiting for transfers between devices, on_device(): ahead = lax.ppermute(ahead, 'tensor', forward)  78.3 us
    all_to_all x1, waiting for transfers between devices, on_device(): lax.all_to_all(expert_rows, 'expert', split_axis=0, concat_axis=0, tiled=...  28.3 us
    ppermute x6, starting transfers between devices, on_device(): behind = lax.ppermute(behind, 'tensor', backward)  21.7 us
    all_to_all x1, starting transfers between devices, on_device(): lax.all_to_all(expert_rows, 'expert', split_axis=0, concat_axis=0, tiled=...  20.8 us
    ppermute x6, waiting for transfers between devices, on_device(): behind = lax.ppermute(behind, 'tensor', backward)  19 us
    ppermute x7, starting transfers between devices, on_device(): ahead = lax.ppermute(ahead, 'tensor', forward)  17.2 us
    all_to_all x1, starting transfers between devices, on_device(): lax.all_to_all(send, 'expert', split_axis=0, concat_axis=0, tiled=True)  16.9 us
    unnamed x19, local copies, waits for them, and re-layouts  14.8 us
  transfers between devices with their start and end apart: 19, of which 11 were waited for; matrix products, arithmetic and copies ran while one was open for 11% of the time, Pallas kernels for 0%

profile of v10, /device:TPU:1, one launch (start us, length us, event | category | flops | bytes accessed | tf_op | source)
XLA Modules:
  0.0 281.0 jit_solution(2735265811664859711)
XLA Ops:
  0.0 7.8 %all-to-all-start = ((bf16[8,8,4096]{2,1,0:T(8,128)(2,1)}), bf16[8,8,4096]{2,1,0:T(8,128)(2,1)S(1)}, u32[]{:S(2)}, u32[]{:S(2)}) async-start(bf16[8,8,4096]{2,1,0:T(8,128)(2,1)} %bitcast.157), calls=%async_computation | async-start | bytes 1048576 | tf_op jit(solution)/shard_map/all_to_all | solution.py:37
  7.8 4.6 %collective-permute-start.8 = (bf16[1024,512]{1,0:T(8,128)(2,1)}, bf16[1024,512]{1,0:T(8,128)(2,1)}, u32[]{:S(2)}, u32[]{:S(2)}) collective-permute-start(bf16[1024,512]{1,0:T(8,128)(2,1)} %bitcast.154), channel_id=1, source_target_pairs={{0,448},{64,0},{128,64},{192,128},{256,192},{320,256},{384,320},{4... | collective-permute-start | bytes 3145736 | tf_op jit(solution)/shard_map/ppermute | solution.py:63
  15.3 7.5 %all-to-all-done = bf16[8,8,4096]{2,1,0:T(8,128)(2,1)S(1)} async-done(((bf16[8,8,4096]{2,1,0:T(8,128)(2,1)}), bf16[8,8,4096]{2,1,0:T(8,128)(2,1)S(1)}, u32[]{:S(2)}, u32[]{:S(2)}) %all-to-all-start) | async-done | bytes 524320 | tf_op jit(solution)/shard_map/all_to_all | solution.py:37
  27.3 16.9 %all-to-all-start.1 = ((bf16[64,2,4096]{2,1,0:T(2,128)(2,1)}), bf16[64,2,4096]{2,1,0:T(2,128)(2,1)}, u32[]{:S(2)}, u32[]{:S(2)}) async-start(bf16[64,2,4096]{2,1,0:T(2,128)(2,1)} %copy.43), calls=%async_computation.1 | async-start | bytes 2097152 | tf_op jit(solution)/shard_map/all_to_all | solution.py:53
  44.2 2.6 collective-permute-start.9
  46.8 3.0 %collective-permute-start.12 = (bf16[1024,512]{1,0:T(8,128)(2,1)}, bf16[1024,512]{1,0:T(8,128)(2,1)}, u32[]{:S(2)}, u32[]{:S(2)}) collective-permute-start(bf16[1024,512]{1,0:T(8,128)(2,1)} %collective-permute-done.11), channel_id=1, source_target_pairs={{0,64},{64,128},{128,192},{192,256},{256,320},{320,384},{384,448},... | collective-permute-start | bytes 3145736 | tf_op jit(solution)/shard_map/ppermute | solution.py:60
  49.8 2.3 constant_dynamic-update-slice_fusion.16
  52.1 19.0 %collective-permute-done.9 = bf16[1024,512]{1,0:T(8,128)(2,1)} collective-permute-done((bf16[1024,512]{1,0:T(8,128)(2,1)}, bf16[1024,512]{1,0:T(8,128)(2,1)}, u32[]{:S(2)}, u32[]{:S(2)}) %collective-permute-start.9) | collective-permute-done | bytes 1048608 | tf_op jit(solution)/shard_map/ppermute | solution.py:63
  71.1 2.7 collective-permute-start.10
  73.8 2.6 collective-permute-start.13
  76.4 2.3 bitcast_dynamic-update-slice_fusion.6
  80.1 3.2 %collective-permute-start.3 = (bf16[128,4096]{1,0:T(8,128)(2,1)S(1)}, bf16[128,4096]{1,0:T(8,128)(2,1)S(1)}, u32[]{:S(2)}, u32[]{:S(2)}) collective-permute-start(bf16[128,4096]{1,0:T(8,128)(2,1)S(1)} %reshape.57), channel_id=1, source_target_pairs={{0,64},{64,128},{128,192},{192,256},{256,320},{320,384},{384,448},... | collective-permute-start | bytes 3145736 | tf_op jit(solution)/shard_map/ppermute | solution.py:78
  83.3 3.3 %collective-permute-start = (bf16[128,4096]{1,0:T(8,128)(2,1)S(1)}, bf16[128,4096]{1,0:T(8,128)(2,1)S(1)}, u32[]{:S(2)}, u32[]{:S(2)}) collective-permute-start(bf16[128,4096]{1,0:T(8,128)(2,1)S(1)} %reshape.57), channel_id=1, source_target_pairs={{0,448},{64,0},{128,64},{192,128},{256,192},{320,256},{384,320},{4... | collective-permute-start | bytes 3145736 | tf_op jit(solution)/shard_map/ppermute | solution.py:80
  86.6 2.3 bitcast_dynamic-update-slice_fusion.5
  89.8 9.8 %collective-permute-done.13 = bf16[1024,512]{1,0:T(8,128)(2,1)} collective-permute-done((bf16[1024,512]{1,0:T(8,128)(2,1)}, bf16[1024,512]{1,0:T(8,128)(2,1)}, u32[]{:S(2)}, u32[]{:S(2)}) %collective-permute-start.13) | collective-permute-done | bytes 1048608 | tf_op jit(solution)/shard_map/ppermute | solution.py:60
  101.8 2.3 bitcast_dynamic-update-slice_fusion.4
  104.1 17.9 %collective-permute-done.3 = bf16[128,4096]{1,0:T(8,128)(2,1)S(1)} collective-permute-done((bf16[128,4096]{1,0:T(8,128)(2,1)S(1)}, bf16[128,4096]{1,0:T(8,128)(2,1)S(1)}, u32[]{:S(2)}, u32[]{:S(2)}) %collective-permute-start.3) | collective-permute-done | bytes 1048608 | tf_op jit(solution)/shard_map/ppermute | solution.py:78
  124.2 4.3 %collective-permute-start.1 = (bf16[128,4096]{1,0:T(8,128)(2,1)S(1)}, bf16[128,4096]{1,0:T(8,128)(2,1)S(1)}, u32[]{:S(2)}, u32[]{:S(2)}) collective-permute-start(bf16[128,4096]{1,0:T(8,128)(2,1)S(1)} %collective-permute-done), channel_id=1, source_target_pairs={{0,448},{64,0},{128,64},{192,128},{256,192},{320,256},{384,320},{4... | collective-permute-start | bytes 3145736 | tf_op jit(solution)/shard_map/ppermute | solution.py:80
  129.8 14.7 %collective-permute-done.14 = bf16[1024,512]{1,0:T(8,128)(2,1)S(1)} collective-permute-done((bf16[1024,512]{1,0:T(8,128)(2,1)}, bf16[1024,512]{1,0:T(8,128)(2,1)S(1)}, u32[]{:S(2)}, u32[]{:S(2)}) %collective-permute-start.14) | collective-permute-done | bytes 1048608 | tf_op jit(solution)/shard_map/ppermute | solution.py:60
  145.5 21.4 %collective-permute-done.4 = bf16[128,4096]{1,0:T(8,128)(2,1)S(1)} collective-permute-done((bf16[128,4096]{1,0:T(8,128)(2,1)S(1)}, bf16[128,4096]{1,0:T(8,128)(2,1)S(1)}, u32[]{:S(2)}, u32[]{:S(2)}) %collective-permute-start.4) | collective-permute-done | bytes 1048608 | tf_op jit(solution)/shard_map/ppermute | solution.py:78
  169.1 4.3 %collective-permute-start.2 = (bf16[128,4096]{1,0:T(8,128)(2,1)S(1)}, bf16[128,4096]{1,0:T(8,128)(2,1)S(1)}, u32[]{:S(2)}, u32[]{:S(2)}) collective-permute-start(bf16[128,4096]{1,0:T(8,128)(2,1)S(1)} %collective-permute-done.1), channel_id=1, source_target_pairs={{0,448},{64,0},{128,64},{192,128},{256,192},{320,256},{384,320},{4... | collective-permute-start | bytes 3145736 | tf_op jit(solution)/shard_map/ppermute | solution.py:80
  173.4 2.3 bitcast_dynamic-update-slice_fusion.2
  177.0 14.5 %collective-permute-done.5 = bf16[128,4096]{1,0:T(8,128)(2,1)S(1)} collective-permute-done((bf16[128,4096]{1,0:T(8,128)(2,1)S(1)}, bf16[128,4096]{1,0:T(8,128)(2,1)S(1)}, u32[]{:S(2)}, u32[]{:S(2)}) %collective-permute-start.5) | collective-permute-done | bytes 1048608 | tf_op jit(solution)/shard_map/ppermute | solution.py:78
  193.6 4.8 %collective-permute-start.7 = (bf16[64,4096]{1,0:T(8,128)(2,1)S(1)}, bf16[64,4096]{1,0:T(8,128)(2,1)S(1)}, u32[]{:S(2)}, u32[]{:S(2)}) collective-permute-start(bf16[64,4096]{1,0:T(8,128)(2,1)S(1)} %slice.9), channel_id=1, source_target_pairs={{0,448},{64,0},{128,64},{192,128},{256,192},{320,256},{384,320},{4... | collective-permute-start | bytes 1572872 | tf_op jit(solution)/shard_map/ppermute | solution.py:84
  199.6 4.5 %collective-permute-done.6 = bf16[64,4096]{1,0:T(8,128)(2,1)S(1)} collective-permute-done((bf16[64,4096]{1,0:T(8,128)(2,1)S(1)}, bf16[64,4096]{1,0:T(8,128)(2,1)S(1)}, u32[]{:S(2)}, u32[]{:S(2)}) %collective-permute-start.6) | collective-permute-done | bytes 524320 | tf_op jit(solution)/shard_map/ppermute | solution.py:83
  208.0 4.7 %all-to-all-start.2 = ((bf16[8,128,128]{2,1,0:T(8,128)(2,1)}), bf16[8,128,128]{2,1,0:T(8,128)(2,1)S(1)}, u32[]{:S(2)}, u32[]{:S(2)}) async-start(bf16[8,128,128]{2,1,0:T(8,128)(2,1)} %constant_dynamic-slice_fusion), calls=%async_computation.2 | async-start | bytes 524288 | tf_op jit(solution)/shard_map/all_to_all | solution.py:87
  212.6 2.3 bitcast_dynamic-update-slice_fusion.1
  214.9 2.3 bitcast_dynamic-update-slice_fusion
  217.2 4.7 %all-to-all-done.2 = bf16[8,128,128]{2,1,0:T(8,128)(2,1)S(1)} async-done(((bf16[8,128,128]{2,1,0:T(8,128)(2,1)}), bf16[8,128,128]{2,1,0:T(8,128)(2,1)S(1)}, u32[]{:S(2)}, u32[]{:S(2)}) %all-to-all-start.2) | async-done | bytes 262176 | tf_op jit(solution)/shard_map/all_to_all | solution.py:87
  222.2 4.7 %convolution_convert_fusion.1 = bf16[128,8,512]{2,0,1:T(8,128)(2,1)S(1)} fusion(bf16[128,1024,1]{0,1,2:T(8,128)(2,1)S(1)} %bitcast.153, bf16[8,1024,512]{2,1,0:T(8,128)(2,1)} %bitcast_dynamic-update-slice_fusion), kind=kOutput, calls=%fused_computation.5 | convolution fusion | flops 1074266112 | bytes 9699328 | tf_op jit(solution)/shard_map/sh,mhc->smc/dot_general | solution.py:91
  229.4 20.8 %all-to-all-start.3 = ((bf16[64,2,4096]{2,1,0:T(2,128)(2,1)}), bf16[64,2,4096]{2,1,0:T(2,128)(2,1)S(1)}, u32[]{:S(2)}, u32[]{:S(2)}) async-start(bf16[64,2,4096]{2,1,0:T(2,128)(2,1)} %reshape.58), calls=%async_computation.3 | async-start | bytes 2097152 | tf_op jit(solution)/shard_map/all_to_all | solution.py:96
  250.5 28.3 %all-to-all-done.3 = bf16[64,2,4096]{2,1,0:T(2,128)(2,1)S(1)} async-done(((bf16[64,2,4096]{2,1,0:T(2,128)(2,1)}), bf16[64,2,4096]{2,1,0:T(2,128)(2,1)S(1)}, u32[]{:S(2)}, u32[]{:S(2)}) %all-to-all-start.3) | async-done | bytes 1048608 | tf_op jit(solution)/shard_map/all_to_all | solution.py:96
  (75 shorter events, 32.2 us)
Async XLA Ops:
  0.0 89.3 %copy-start = (bf16[1,4096,128]{2,1,0:T(8,128)(2,1)S(1)}, bf16[1,4096,128]{2,1,0:T(8,128)(2,1)}, u32[]{:S(2)}) copy-start(bf16[1,4096,128]{2,1,0:T(8,128)(2,1)} %param.12) | copy-start | bytes 3145732
  0.0 88.9 %copy-start.1 = (bf16[1,4096,128]{2,1,0:T(8,128)(2,1)S(1)}, bf16[1,4096,128]{2,1,0:T(8,128)(2,1)}, u32[]{:S(2)}) copy-start(bf16[1,4096,128]{2,1,0:T(8,128)(2,1)} %param.11) | copy-start | bytes 3145732
  0.0 22.7 %all-to-all-start = ((bf16[8,8,4096]{2,1,0:T(8,128)(2,1)}), bf16[8,8,4096]{2,1,0:T(8,128)(2,1)S(1)}, u32[]{:S(2)}, u32[]{:S(2)}) async-start(bf16[8,8,4096]{2,1,0:T(8,128)(2,1)} %bitcast.157), calls=%async_computation | async-start | bytes 1048576 | tf_op jit(solution)/shard_map/all_to_all | solution.py:37
  7.8 36.4 %collective-permute-start.8 = (bf16[1024,512]{1,0:T(8,128)(2,1)}, bf16[1024,512]{1,0:T(8,128)(2,1)}, u32[]{:S(2)}, u32[]{:S(2)}) collective-permute-start(bf16[1024,512]{1,0:T(8,128)(2,1)} %bitcast.154), channel_id=1, source_target_pairs={{0,448},{64,0},{128,64},{192,128},{256,192},{320,256},{384,320},{4... | collective-permute-start | bytes 3145736 | tf_op jit(solution)/shard_map/ppermute | solution.py:63
  12.4 34.5 %collective-permute-start.11 = (bf16[1024,512]{1,0:T(8,128)(2,1)}, bf16[1024,512]{1,0:T(8,128)(2,1)}, u32[]{:S(2)}, u32[]{:S(2)}) collective-permute-start(bf16[1024,512]{1,0:T(8,128)(2,1)} %bitcast.155), channel_id=1, source_target_pairs={{0,64},{64,128},{128,192},{192,256},{256,320},{320,384},{384,448},... | collective-permute-start | bytes 3145736 | tf_op jit(solution)/shard_map/ppermute | solution.py:60
  27.3 51.3 %all-to-all-start.1 = ((bf16[64,2,4096]{2,1,0:T(2,128)(2,1)}), bf16[64,2,4096]{2,1,0:T(2,128)(2,1)}, u32[]{:S(2)}, u32[]{:S(2)}) async-start(bf16[64,2,4096]{2,1,0:T(2,128)(2,1)} %copy.43), calls=%async_computation.1 | async-start | bytes 2097152 | tf_op jit(solution)/shard_map/all_to_all | solution.py:53
  44.2 26.8 %collective-permute-start.9 = (bf16[1024,512]{1,0:T(8,128)(2,1)}, bf16[1024,512]{1,0:T(8,128)(2,1)}, u32[]{:S(2)}, u32[]{:S(2)}) collective-permute-start(bf16[1024,512]{1,0:T(8,128)(2,1)} %collective-permute-done.8), channel_id=1, source_target_pairs={{0,448},{64,0},{128,64},{192,128},{256,192},{320,256},{384,320},{4... | collective-permute-start | bytes 3145736 | tf_op jit(solution)/shard_map/ppermute | solution.py:63
  46.8 26.9 %collective-permute-start.12 = (bf16[1024,512]{1,0:T(8,128)(2,1)}, bf16[1024,512]{1,0:T(8,128)(2,1)}, u32[]{:S(2)}, u32[]{:S(2)}) collective-permute-start(bf16[1024,512]{1,0:T(8,128)(2,1)} %collective-permute-done.11), channel_id=1, source_target_pairs={{0,64},{64,128},{128,192},{192,256},{256,320},{320,384},{384,448},... | collective-permute-start | bytes 3145736 | tf_op jit(solution)/shard_map/ppermute | solution.py:60
  71.1 30.7 %collective-permute-start.10 = (bf16[1024,512]{1,0:T(8,128)(2,1)}, bf16[1024,512]{1,0:T(8,128)(2,1)}, u32[]{:S(2)}, u32[]{:S(2)}) collective-permute-start(bf16[1024,512]{1,0:T(8,128)(2,1)} %collective-permute-done.9), channel_id=1, source_target_pairs={{0,448},{64,0},{128,64},{192,128},{256,192},{320,256},{384,320},{4... | collective-permute-start | bytes 3145736 | tf_op jit(solution)/shard_map/ppermute | solution.py:63
  73.8 25.8 %collective-permute-start.13 = (bf16[1024,512]{1,0:T(8,128)(2,1)}, bf16[1024,512]{1,0:T(8,128)(2,1)}, u32[]{:S(2)}, u32[]{:S(2)}) collective-permute-start(bf16[1024,512]{1,0:T(8,128)(2,1)} %collective-permute-done.12), channel_id=1, source_target_pairs={{0,64},{64,128},{128,192},{192,256},{256,320},{320,384},{384,448},... | collective-permute-start | bytes 3145736 | tf_op jit(solution)/shard_map/ppermute | solution.py:60
  80.1 41.8 %collective-permute-start.3 = (bf16[128,4096]{1,0:T(8,128)(2,1)S(1)}, bf16[128,4096]{1,0:T(8,128)(2,1)S(1)}, u32[]{:S(2)}, u32[]{:S(2)}) collective-permute-start(bf16[128,4096]{1,0:T(8,128)(2,1)S(1)} %reshape.57), channel_id=1, source_target_pairs={{0,64},{64,128},{128,192},{192,256},{256,320},{320,384},{384,448},... | collective-permute-start | bytes 3145736 | tf_op jit(solution)/shard_map/ppermute | solution.py:78
  83.3 40.8 %collective-permute-start = (bf16[128,4096]{1,0:T(8,128)(2,1)S(1)}, bf16[128,4096]{1,0:T(8,128)(2,1)S(1)}, u32[]{:S(2)}, u32[]{:S(2)}) collective-permute-start(bf16[128,4096]{1,0:T(8,128)(2,1)S(1)} %reshape.57), channel_id=1, source_target_pairs={{0,448},{64,0},{128,64},{192,128},{256,192},{320,256},{384,320},{4... | collective-permute-start | bytes 3145736 | tf_op jit(solution)/shard_map/ppermute | solution.py:80
  99.6 44.8 %collective-permute-start.14 = (bf16[1024,512]{1,0:T(8,128)(2,1)}, bf16[1024,512]{1,0:T(8,128)(2,1)S(1)}, u32[]{:S(2)}, u32[]{:S(2)}) collective-permute-start(bf16[1024,512]{1,0:T(8,128)(2,1)} %collective-permute-done.13), channel_id=1, source_target_pairs={{0,64},{64,128},{128,192},{192,256},{256,320},{320,384},{384,448},... | collective-permute-start | bytes 3145736 | tf_op jit(solution)/shard_map/ppermute | solution.py:60
  122.0 44.9 %collective-permute-start.4 = (bf16[128,4096]{1,0:T(8,128)(2,1)S(1)}, bf16[128,4096]{1,0:T(8,128)(2,1)S(1)}, u32[]{:S(2)}, u32[]{:S(2)}) collective-permute-start(bf16[128,4096]{1,0:T(8,128)(2,1)S(1)} %collective-permute-done.3), channel_id=1, source_target_pairs={{0,64},{64,128},{128,192},{192,256},{256,320},{320,384},{384,448},... | collective-permute-start | bytes 3145736 | tf_op jit(solution)/shard_map/ppermute | solution.py:78
  124.2 44.9 %collective-permute-start.1 = (bf16[128,4096]{1,0:T(8,128)(2,1)S(1)}, bf16[128,4096]{1,0:T(8,128)(2,1)S(1)}, u32[]{:S(2)}, u32[]{:S(2)}) collective-permute-start(bf16[128,4096]{1,0:T(8,128)(2,1)S(1)} %collective-permute-done), channel_id=1, source_target_pairs={{0,448},{64,0},{128,64},{192,128},{256,192},{320,256},{384,320},{4... | collective-permute-start | bytes 3145736 | tf_op jit(solution)/shard_map/ppermute | solution.py:80
  166.9 24.6 %collective-permute-start.5 = (bf16[128,4096]{1,0:T(8,128)(2,1)S(1)}, bf16[128,4096]{1,0:T(8,128)(2,1)S(1)}, u32[]{:S(2)}, u32[]{:S(2)}) collective-permute-start(bf16[128,4096]{1,0:T(8,128)(2,1)S(1)} %collective-permute-done.4), channel_id=1, source_target_pairs={{0,64},{64,128},{128,192},{192,256},{256,320},{320,384},{384,448},... | collective-permute-start | bytes 3145736 | tf_op jit(solution)/shard_map/ppermute | solution.py:78
  169.1 24.4 %collective-permute-start.2 = (bf16[128,4096]{1,0:T(8,128)(2,1)S(1)}, bf16[128,4096]{1,0:T(8,128)(2,1)S(1)}, u32[]{:S(2)}, u32[]{:S(2)}) collective-permute-start(bf16[128,4096]{1,0:T(8,128)(2,1)S(1)} %collective-permute-done.1), channel_id=1, source_target_pairs={{0,448},{64,0},{128,64},{192,128},{256,192},{320,256},{384,320},{4... | collective-permute-start | bytes 3145736 | tf_op jit(solution)/shard_map/ppermute | solution.py:80
  191.6 12.6 %collective-permute-start.6 = (bf16[64,4096]{1,0:T(8,128)(2,1)S(1)}, bf16[64,4096]{1,0:T(8,128)(2,1)S(1)}, u32[]{:S(2)}, u32[]{:S(2)}) collective-permute-start(bf16[64,4096]{1,0:T(8,128)(2,1)S(1)} %slice.8), channel_id=1, source_target_pairs={{0,64},{64,128},{128,192},{192,256},{256,320},{320,384},{384,448},... | collective-permute-start | bytes 1572872 | tf_op jit(solution)/shard_map/ppermute | solution.py:83
  193.6 11.5 %collective-permute-start.7 = (bf16[64,4096]{1,0:T(8,128)(2,1)S(1)}, bf16[64,4096]{1,0:T(8,128)(2,1)S(1)}, u32[]{:S(2)}, u32[]{:S(2)}) collective-permute-start(bf16[64,4096]{1,0:T(8,128)(2,1)S(1)} %slice.9), channel_id=1, source_target_pairs={{0,448},{64,0},{128,64},{192,128},{256,192},{320,256},{384,320},{4... | collective-permute-start | bytes 1572872 | tf_op jit(solution)/shard_map/ppermute | solution.py:84
  208.0 14.0 %all-to-all-start.2 = ((bf16[8,128,128]{2,1,0:T(8,128)(2,1)}), bf16[8,128,128]{2,1,0:T(8,128)(2,1)S(1)}, u32[]{:S(2)}, u32[]{:S(2)}) async-start(bf16[8,128,128]{2,1,0:T(8,128)(2,1)} %constant_dynamic-slice_fusion), calls=%async_computation.2 | async-start | bytes 524288 | tf_op jit(solution)/shard_map/all_to_all | solution.py:87
  222.2 28.1 %copy-start.2 = (f32[64,8]{0,1:T(8,128)S(1)}, f32[64,8]{0,1:T(8,128)}, u32[]{:S(2)}) copy-start(f32[64,8]{0,1:T(8,128)} %param.10) | copy-start | bytes 6148
  229.4 49.4 %all-to-all-start.3 = ((bf16[64,2,4096]{2,1,0:T(2,128)(2,1)}), bf16[64,2,4096]{2,1,0:T(2,128)(2,1)S(1)}, u32[]{:S(2)}, u32[]{:S(2)}) async-start(bf16[64,2,4096]{2,1,0:T(2,128)(2,1)} %reshape.58), calls=%async_computation.3 | async-start | bytes 2097152 | tf_op jit(solution)/shard_map/all_to_all | solution.py:96

commit v11 on v7

--- a/solution.py
+++ b/solution.py
@@ -69,6 +69,7 @@
         return (jax.nn.silu(gate_act) * up_act).astype(jnp.bfloat16)
 
     down_all, recv = lax.optimization_barrier((down_all, recv))
+    down_abs = jnp.roll(jnp.stack(down_all), tensor_index, axis=0)
     own_rows = recv.reshape(expert_count * capacity, feature_width)
     hidden_parts = [front(own_rows)] + [None] * (tensor_count - 1)
     ahead = own_rows
@@ -90,9 +91,8 @@
         "tensor", split_axis=0, concat_axis=2, tiled=True,
     )[0]
     expert_sum = jnp.einsum(
-        "sh,mhc->smc", hidden_own, jnp.stack(down_all), preferred_element_type=jnp.float32
+        "sh,jhc->sjc", hidden_own, down_abs, preferred_element_type=jnp.float32
     ).astype(jnp.bfloat16)
-    expert_sum = jnp.roll(expert_sum, tensor_index, axis=1)
     expert_rows = expert_sum.reshape(expert_count, capacity, feature_width)
     returned = lax.all_to_all(expert_rows, "expert", split_axis=0, concat_axis=0, tiled=True)
     returned = returned.reshape(expert_count, capacity, feature_width)

time: 281 us -> 281 us (level)
  waiting for transfers between devices: 139 us -> 125 us
  local copies, waits for them, and re-layouts: 20.1 us -> 28.1 us
  starting transfers between devices: 103 us -> 107 us
    unnamed x27 -> x37, local copies, waits for them, and re-layouts: 11.1 us -> 19.3 us
    ppermute x7, waiting for transfers between devices: 61.6 us -> 54.7 us  [on_device(): ahead = lax.ppermute(ahead, 'tensor', forward)]
    ppermute x6, waiting for transfers between devices: 8.15 us -> 3.4 us  [on_device(): behind = lax.ppermute(behind, 'tensor', backward)]
    ppermute x6, starting transfers between devices: 24 us -> 27 us  [on_device(): behind = lax.ppermute(behind, 'tensor', backward)]
  transfers between devices with their start and end apart: 19 -> 19, of which waited for: 15 -> 14; matrix products, arithmetic and copies ran while one was open for 8% -> 12% of each run, Pallas kernels for 0% -> 0%
where the time goes in v11:
time: 281 us; the launch traced here: 279 us
  waiting for transfers between devices  125 us (44%)
  starting transfers between devices  107 us (38%)
  local copies, waits for them, and re-layouts  28.1 us (10%)
  matrix products  15.4 us (5%)
    ppermute x7, waiting for transfers between devices, on_device(): ahead = lax.ppermute(ahead, 'tensor', forward)  54.7 us
    all_to_all x1, waiting for transfers between devices, on_device(): lax.all_to_all(expert_rows, 'expert', split_axis=0, concat_axis=0, tiled=...  28.3 us
    ppermute x6, starting transfers between devices, on_device(): behind = lax.ppermute(behind, 'tensor', backward)  27 us
    all_to_all x1, starting transfers between devices, on_device(): lax.all_to_all(expert_rows, 'expert', split_axis=0, concat_axis=0, tiled=...  22 us
    ppermute x7, starting transfers between devices, on_device(): ahead = lax.ppermute(ahead, 'tensor', forward)  21.7 us
    all_to_all x1, waiting for transfers between devices, on_device(): lax.all_to_all(send, 'expert', split_axis=0, concat_axis=0, tiled=True)  21.6 us
    unnamed x37, local copies, waits for them, and re-layouts  19.3 us
    all_to_all x1, starting transfers between devices, on_device(): lax.all_to_all(send, 'expert', split_axis=0, concat_axis=0, tiled=True)  16.1 us
  transfers between devices with their start and end apart: 19, of which 14 were waited for; matrix products, arithmetic and copies ran while one was open for 12% of the time, Pallas kernels for 0%

profile of v11, /device:TPU:1, one launch (start us, length us, event | category | flops | bytes accessed | tf_op | source)
XLA Modules:
  0.0 279.1 jit_solution(11466317886568521368)
XLA Ops:
  0.0 4.1 %collective-permute-start.3 = (bf16[1024,512]{1,0:T(8,128)(2,1)}, bf16[1024,512]{1,0:T(8,128)(2,1)S(1)}, u32[]{:S(2)}, u32[]{:S(2)}) collective-permute-start(bf16[1024,512]{1,0:T(8,128)(2,1)} %bitcast.162), channel_id=1, source_target_pairs={{0,64},{64,128},{128,192},{192,256},{256,320},{320,384},{384,448},... | collective-permute-start | bytes 3145736 | tf_op jit(solution)/shard_map/ppermute | solution.py:60
  4.2 5.9 %all-to-all-start = ((bf16[8,8,4096]{2,1,0:T(8,128)(2,1)}), bf16[8,8,4096]{2,1,0:T(8,128)(2,1)}, u32[]{:S(2)}, u32[]{:S(2)}) async-start(bf16[8,8,4096]{2,1,0:T(8,128)(2,1)} %bitcast.168), calls=%async_computation | async-start | bytes 1048576 | tf_op jit(solution)/shard_map/all_to_all | solution.py:37
  10.1 4.6 %collective-permute-start = (bf16[1024,512]{1,0:T(8,128)(2,1)}, bf16[1024,512]{1,0:T(8,128)(2,1)}, u32[]{:S(2)}, u32[]{:S(2)}) collective-permute-start(bf16[1024,512]{1,0:T(8,128)(2,1)} %bitcast.163), channel_id=1, source_target_pairs={{0,448},{64,0},{128,64},{192,128},{256,192},{320,256},{384,320},{4... | collective-permute-start | bytes 3145736 | tf_op jit(solution)/shard_map/ppermute | solution.py:63
  15.5 8.6 %collective-permute-done.3 = bf16[1024,512]{1,0:T(8,128)(2,1)S(1)} collective-permute-done((bf16[1024,512]{1,0:T(8,128)(2,1)}, bf16[1024,512]{1,0:T(8,128)(2,1)S(1)}, u32[]{:S(2)}, u32[]{:S(2)}) %collective-permute-start.3) | collective-permute-done | bytes 1048608 | tf_op jit(solution)/shard_map/ppermute | solution.py:60
  24.1 7.7 %collective-permute-start.4 = (bf16[1024,512]{1,0:T(8,128)(2,1)S(1)}, bf16[1024,512]{1,0:T(8,128)(2,1)S(1)}, u32[]{:S(2)}, u32[]{:S(2)}) collective-permute-start(bf16[1024,512]{1,0:T(8,128)(2,1)S(1)} %collective-permute-done.3), channel_id=1, source_target_pairs={{0,64},{64,128},{128,192},{192,256},{256,320},{320,384},{384,448},... | collective-permute-start | bytes 3145736 | tf_op jit(solution)/shard_map/ppermute | solution.py:60
  32.0 6.9 %all-to-all-done = bf16[8,8,4096]{2,1,0:T(8,128)(2,1)} async-done(((bf16[8,8,4096]{2,1,0:T(8,128)(2,1)}), bf16[8,8,4096]{2,1,0:T(8,128)(2,1)}, u32[]{:S(2)}, u32[]{:S(2)}) %all-to-all-start) | async-done | bytes 524320 | tf_op jit(solution)/shard_map/all_to_all | solution.py:37
  41.2 3.2 %collective-permute-done = bf16[1024,512]{1,0:T(8,128)(2,1)} collective-permute-done((bf16[1024,512]{1,0:T(8,128)(2,1)}, bf16[1024,512]{1,0:T(8,128)(2,1)}, u32[]{:S(2)}, u32[]{:S(2)}) %collective-permute-start) | collective-permute-done | bytes 1048608 | tf_op jit(solution)/shard_map/ppermute | solution.py:63
  44.4 3.9 %collective-permute-start.1 = (bf16[1024,512]{1,0:T(8,128)(2,1)}, bf16[1024,512]{1,0:T(8,128)(2,1)}, u32[]{:S(2)}, u32[]{:S(2)}) collective-permute-start(bf16[1024,512]{1,0:T(8,128)(2,1)} %collective-permute-done), channel_id=1, source_target_pairs={{0,448},{64,0},{128,64},{192,128},{256,192},{320,256},{384,320},{4... | collective-permute-start | bytes 3145736 | tf_op jit(solution)/shard_map/ppermute | solution.py:63
  48.3 13.1 %collective-permute-done.4 = bf16[1024,512]{1,0:T(8,128)(2,1)S(1)} collective-permute-done((bf16[1024,512]{1,0:T(8,128)(2,1)S(1)}, bf16[1024,512]{1,0:T(8,128)(2,1)S(1)}, u32[]{:S(2)}, u32[]{:S(2)}) %collective-permute-start.4) | collective-permute-done | bytes 1048608 | tf_op jit(solution)/shard_map/ppermute | solution.py:60
  61.4 2.0 collective-permute-start.5
  64.6 2.1 copy.43
  66.7 16.1 %all-to-all-start.1 = ((bf16[64,2,4096]{2,1,0:T(2,128)(2,1)}), bf16[64,2,4096]{2,1,0:T(2,128)(2,1)}, u32[]{:S(2)}, u32[]{:S(2)}) async-start(bf16[64,2,4096]{2,1,0:T(2,128)(2,1)} %copy.43), calls=%async_computation.1 | async-start | bytes 2097152 | tf_op jit(solution)/shard_map/all_to_all | solution.py:53
  82.9 4.9 %collective-permute-start.2 = (bf16[1024,512]{1,0:T(8,128)(2,1)}, bf16[1024,512]{1,0:T(8,128)(2,1)}, u32[]{:S(2)}, u32[]{:S(2)}) collective-permute-start(bf16[1024,512]{1,0:T(8,128)(2,1)} %collective-permute-done.1), channel_id=1, source_target_pairs={{0,448},{64,0},{128,64},{192,128},{256,192},{320,256},{384,320},{4... | collective-permute-start | bytes 3145736 | tf_op jit(solution)/shard_map/ppermute | solution.py:63
  87.7 1.9 collective-permute-start.6
  89.7 21.6 %all-to-all-done.1 = bf16[64,2,4096]{2,1,0:T(2,128)(2,1)} async-done(((bf16[64,2,4096]{2,1,0:T(2,128)(2,1)}), bf16[64,2,4096]{2,1,0:T(2,128)(2,1)}, u32[]{:S(2)}, u32[]{:S(2)}) %all-to-all-start.1) | async-done | bytes 1048608 | tf_op jit(solution)/shard_map/all_to_all | solution.py:53
  111.3 2.1 collective-permute-done.6
  114.9 2.1 collective-permute-start.10
  116.9 4.6 %collective-permute-start.7 = (bf16[128,4096]{1,0:T(8,128)(2,1)S(1)}, bf16[128,4096]{1,0:T(8,128)(2,1)S(1)}, u32[]{:S(2)}, u32[]{:S(2)}) collective-permute-start(bf16[128,4096]{1,0:T(8,128)(2,1)S(1)} %reshape.57), channel_id=1, source_target_pairs={{0,448},{64,0},{128,64},{192,128},{256,192},{320,256},{384,320},{4... | collective-permute-start | bytes 3145736 | tf_op jit(solution)/shard_map/ppermute | solution.py:82
  141.4 4.6 %collective-permute-start.8 = (bf16[128,4096]{1,0:T(8,128)(2,1)S(1)}, bf16[128,4096]{1,0:T(8,128)(2,1)S(1)}, u32[]{:S(2)}, u32[]{:S(2)}) collective-permute-start(bf16[128,4096]{1,0:T(8,128)(2,1)S(1)} %collective-permute-done.7), channel_id=1, source_target_pairs={{0,448},{64,0},{128,64},{192,128},{256,192},{320,256},{384,320},{4... | collective-permute-start | bytes 3145736 | tf_op jit(solution)/shard_map/ppermute | solution.py:82
  148.6 14.5 %collective-permute-done.11 = bf16[128,4096]{1,0:T(8,128)(2,1)S(1)} collective-permute-done((bf16[128,4096]{1,0:T(8,128)(2,1)S(1)}, bf16[128,4096]{1,0:T(8,128)(2,1)S(1)}, u32[]{:S(2)}, u32[]{:S(2)}) %collective-permute-start.11) | collective-permute-done | bytes 1048608 | tf_op jit(solution)/shard_map/ppermute | solution.py:80
  165.0 4.6 %collective-permute-start.9 = (bf16[128,4096]{1,0:T(8,128)(2,1)S(1)}, bf16[128,4096]{1,0:T(8,128)(2,1)S(1)}, u32[]{:S(2)}, u32[]{:S(2)}) collective-permute-start(bf16[128,4096]{1,0:T(8,128)(2,1)S(1)} %collective-permute-done.8), channel_id=1, source_target_pairs={{0,448},{64,0},{128,64},{192,128},{256,192},{320,256},{384,320},{4... | collective-permute-start | bytes 3145736 | tf_op jit(solution)/shard_map/ppermute | solution.py:82
  171.4 14.5 %collective-permute-done.12 = bf16[128,4096]{1,0:T(8,128)(2,1)S(1)} collective-permute-done((bf16[128,4096]{1,0:T(8,128)(2,1)S(1)}, bf16[128,4096]{1,0:T(8,128)(2,1)S(1)}, u32[]{:S(2)}, u32[]{:S(2)}) %collective-permute-start.12) | collective-permute-done | bytes 1048608 | tf_op jit(solution)/shard_map/ppermute | solution.py:80
  185.9 1.9 collective-permute-start.13
  188.1 4.6 %collective-permute-start.14 = (bf16[64,4096]{1,0:T(8,128)(2,1)S(1)}, bf16[64,4096]{1,0:T(8,128)(2,1)S(1)}, u32[]{:S(2)}, u32[]{:S(2)}) collective-permute-start(bf16[64,4096]{1,0:T(8,128)(2,1)S(1)} %slice.9), channel_id=1, source_target_pairs={{0,448},{64,0},{128,64},{192,128},{256,192},{320,256},{384,320},{4... | collective-permute-start | bytes 1572872 | tf_op jit(solution)/shard_map/ppermute | solution.py:86
  194.0 3.0 %collective-permute-done.13 = bf16[64,4096]{1,0:T(8,128)(2,1)S(1)} collective-permute-done((bf16[64,4096]{1,0:T(8,128)(2,1)S(1)}, bf16[64,4096]{1,0:T(8,128)(2,1)S(1)}, u32[]{:S(2)}, u32[]{:S(2)}) %collective-permute-start.13) | collective-permute-done | bytes 524320 | tf_op jit(solution)/shard_map/ppermute | solution.py:85
  201.9 8.2 %all-to-all-start.2 = ((bf16[8,128,128]{2,1,0:T(8,128)(2,1)}), bf16[8,128,128]{2,1,0:T(8,128)(2,1)S(1)}, u32[]{:S(2)}, u32[]{:S(2)}) async-start(bf16[8,128,128]{2,1,0:T(8,128)(2,1)} %constant_dynamic-slice_fusion), calls=%async_computation.2 | async-start | bytes 524288 | tf_op jit(solution)/shard_map/all_to_all | solution.py:89
  210.1 2.3 bitcast_dynamic-update-slice_fusion.3
  213.4 6.0 %all-to-all-done.2 = bf16[8,128,128]{2,1,0:T(8,128)(2,1)S(1)} async-done(((bf16[8,128,128]{2,1,0:T(8,128)(2,1)}), bf16[8,128,128]{2,1,0:T(8,128)(2,1)S(1)}, u32[]{:S(2)}, u32[]{:S(2)}) %all-to-all-start.2) | async-done | bytes 262176 | tf_op jit(solution)/shard_map/all_to_all | solution.py:89
  219.6 4.7 %fusion.3 = bf16[128,8,512]{2,0,1:T(8,128)(2,1)S(1)} fusion(bf16[128,1024,1]{0,1,2:T(8,128)(2,1)S(1)} %bitcast.166, bf16[16,1024,512]{2,1,0:T(8,128)(2,1)} %bitcast_dynamic-update-slice_fusion.1, s32[]{:T(128)S(6)} %select_n.35), kind=kOutput, calls=%fused_computation.5 | convolution fusion | flops 1074266112 | bytes 9699332 | tf_op jit(solution)/shard_map/sh,jhc->sjc/dot_general | solution.py:93
  226.4 22.0 %all-to-all-start.3 = ((bf16[64,2,4096]{2,1,0:T(2,128)(2,1)}), bf16[64,2,4096]{2,1,0:T(2,128)(2,1)S(1)}, u32[]{:S(2)}, u32[]{:S(2)}) async-start(bf16[64,2,4096]{2,1,0:T(2,128)(2,1)} %reshape.58), calls=%async_computation.3 | async-start | bytes 2097152 | tf_op jit(solution)/shard_map/all_to_all | solution.py:97
  248.7 28.3 %all-to-all-done.3 = bf16[64,2,4096]{2,1,0:T(2,128)(2,1)S(1)} async-done(((bf16[64,2,4096]{2,1,0:T(2,128)(2,1)}), bf16[64,2,4096]{2,1,0:T(2,128)(2,1)S(1)}, u32[]{:S(2)}, u32[]{:S(2)}) %all-to-all-start.3) | async-done | bytes 1048608 | tf_op jit(solution)/shard_map/all_to_all | solution.py:97
  276.9 2.2 fusion.2
  (92 shorter events, 42.0 us)
Async XLA Ops:
  0.0 147.3 %copy-start = (bf16[1,4096,128]{2,1,0:T(8,128)(2,1)S(1)}, bf16[1,4096,128]{2,1,0:T(8,128)(2,1)}, u32[]{:S(2)}) copy-start(bf16[1,4096,128]{2,1,0:T(8,128)(2,1)} %param.12) | copy-start | bytes 3145732
  0.0 24.1 %collective-permute-start.3 = (bf16[1024,512]{1,0:T(8,128)(2,1)}, bf16[1024,512]{1,0:T(8,128)(2,1)S(1)}, u32[]{:S(2)}, u32[]{:S(2)}) collective-permute-start(bf16[1024,512]{1,0:T(8,128)(2,1)} %bitcast.162), channel_id=1, source_target_pairs={{0,64},{64,128},{128,192},{192,256},{256,320},{320,384},{384,448},... | collective-permute-start | bytes 3145736 | tf_op jit(solution)/shard_map/ppermute | solution.py:60
  4.2 34.7 %all-to-all-start = ((bf16[8,8,4096]{2,1,0:T(8,128)(2,1)}), bf16[8,8,4096]{2,1,0:T(8,128)(2,1)}, u32[]{:S(2)}, u32[]{:S(2)}) async-start(bf16[8,8,4096]{2,1,0:T(8,128)(2,1)} %bitcast.168), calls=%async_computation | async-start | bytes 1048576 | tf_op jit(solution)/shard_map/all_to_all | solution.py:37
  10.1 34.3 %collective-permute-start = (bf16[1024,512]{1,0:T(8,128)(2,1)}, bf16[1024,512]{1,0:T(8,128)(2,1)}, u32[]{:S(2)}, u32[]{:S(2)}) collective-permute-start(bf16[1024,512]{1,0:T(8,128)(2,1)} %bitcast.163), channel_id=1, source_target_pairs={{0,448},{64,0},{128,64},{192,128},{256,192},{320,256},{384,320},{4... | collective-permute-start | bytes 3145736 | tf_op jit(solution)/shard_map/ppermute | solution.py:63
  24.1 39.3 %copy-start.4 = (bf16[1024,512]{1,0:T(8,128)(2,1)}, bf16[1024,512]{1,0:T(8,128)(2,1)S(1)}, u32[]{:S(2)}) copy-start(bf16[1024,512]{1,0:T(8,128)(2,1)S(1)} %collective-permute-done.3) | copy-start | bytes 3145732
  24.1 37.3 %collective-permute-start.4 = (bf16[1024,512]{1,0:T(8,128)(2,1)S(1)}, bf16[1024,512]{1,0:T(8,128)(2,1)S(1)}, u32[]{:S(2)}, u32[]{:S(2)}) collective-permute-start(bf16[1024,512]{1,0:T(8,128)(2,1)S(1)} %collective-permute-done.3), channel_id=1, source_target_pairs={{0,64},{64,128},{128,192},{192,256},{256,320},{320,384},{384,448},... | collective-permute-start | bytes 3145736 | tf_op jit(solution)/shard_map/ppermute | solution.py:60
  44.4 38.4 %collective-permute-start.1 = (bf16[1024,512]{1,0:T(8,128)(2,1)}, bf16[1024,512]{1,0:T(8,128)(2,1)}, u32[]{:S(2)}, u32[]{:S(2)}) collective-permute-start(bf16[1024,512]{1,0:T(8,128)(2,1)} %collective-permute-done), channel_id=1, source_target_pairs={{0,448},{64,0},{128,64},{192,128},{256,192},{320,256},{384,320},{4... | collective-permute-start | bytes 3145736 | tf_op jit(solution)/shard_map/ppermute | solution.py:63
  61.4 49.9 %copy-start.6 = (bf16[1024,512]{1,0:T(8,128)(2,1)}, bf16[1024,512]{1,0:T(8,128)(2,1)S(1)}, u32[]{:S(2)}) copy-start(bf16[1024,512]{1,0:T(8,128)(2,1)S(1)} %collective-permute-done.4) | copy-start | bytes 3145732
  61.4 26.3 %collective-permute-start.5 = (bf16[1024,512]{1,0:T(8,128)(2,1)S(1)}, bf16[1024,512]{1,0:T(8,128)(2,1)}, u32[]{:S(2)}, u32[]{:S(2)}) collective-permute-start(bf16[1024,512]{1,0:T(8,128)(2,1)S(1)} %collective-permute-done.4), channel_id=1, source_target_pairs={{0,64},{64,128},{128,192},{192,256},{256,320},{320,384},{384,448},... | collective-permute-start | bytes 3145736 | tf_op jit(solution)/shard_map/ppermute | solution.py:60
  64.6 72.6 %copy-start.1 = (bf16[1,4096,128]{2,1,0:T(8,128)(2,1)S(1)}, bf16[1,4096,128]{2,1,0:T(8,128)(2,1)}, u32[]{:S(2)}) copy-start(bf16[1,4096,128]{2,1,0:T(8,128)(2,1)} %param.11) | copy-start | bytes 3145732
  66.7 44.6 %all-to-all-start.1 = ((bf16[64,2,4096]{2,1,0:T(2,128)(2,1)}), bf16[64,2,4096]{2,1,0:T(2,128)(2,1)}, u32[]{:S(2)}, u32[]{:S(2)}) async-start(bf16[64,2,4096]{2,1,0:T(2,128)(2,1)} %copy.43), calls=%async_computation.1 | async-start | bytes 2097152 | tf_op jit(solution)/shard_map/all_to_all | solution.py:53
  82.9 28.4 %collective-permute-start.2 = (bf16[1024,512]{1,0:T(8,128)(2,1)}, bf16[1024,512]{1,0:T(8,128)(2,1)}, u32[]{:S(2)}, u32[]{:S(2)}) collective-permute-start(bf16[1024,512]{1,0:T(8,128)(2,1)} %collective-permute-done.1), channel_id=1, source_target_pairs={{0,448},{64,0},{128,64},{192,128},{256,192},{320,256},{384,320},{4... | collective-permute-start | bytes 3145736 | tf_op jit(solution)/shard_map/ppermute | solution.py:63
  87.7 25.7 %collective-permute-start.6 = (bf16[1024,512]{1,0:T(8,128)(2,1)}, bf16[1024,512]{1,0:T(8,128)(2,1)}, u32[]{:S(2)}, u32[]{:S(2)}) collective-permute-start(bf16[1024,512]{1,0:T(8,128)(2,1)} %collective-permute-done.5), channel_id=1, source_target_pairs={{0,64},{64,128},{128,192},{192,256},{256,320},{320,384},{384,448},... | collective-permute-start | bytes 3145736 | tf_op jit(solution)/shard_map/ppermute | solution.py:60
  114.9 17.0 %copy-start.3 = (bf16[1,1024,512]{2,1,0:T(8,128)(2,1)S(1)}, bf16[1,1024,512]{2,1,0:T(8,128)(2,1)}, u32[]{:S(2)}) copy-start(bf16[1,1024,512]{2,1,0:T(8,128)(2,1)} %param.13) | copy-start | bytes 3145732
  114.9 24.6 %collective-permute-start.10 = (bf16[128,4096]{1,0:T(8,128)(2,1)S(1)}, bf16[128,4096]{1,0:T(8,128)(2,1)S(1)}, u32[]{:S(2)}, u32[]{:S(2)}) collective-permute-start(bf16[128,4096]{1,0:T(8,128)(2,1)S(1)} %reshape.57), channel_id=1, source_target_pairs={{0,64},{64,128},{128,192},{192,256},{256,320},{320,384},{384,448},... | collective-permute-start | bytes 3145736 | tf_op jit(solution)/shard_map/ppermute | solution.py:80
  116.9 24.5 %collective-permute-start.7 = (bf16[128,4096]{1,0:T(8,128)(2,1)S(1)}, bf16[128,4096]{1,0:T(8,128)(2,1)S(1)}, u32[]{:S(2)}, u32[]{:S(2)}) collective-permute-start(bf16[128,4096]{1,0:T(8,128)(2,1)S(1)} %reshape.57), channel_id=1, source_target_pairs={{0,448},{64,0},{128,64},{192,128},{256,192},{320,256},{384,320},{4... | collective-permute-start | bytes 3145736 | tf_op jit(solution)/shard_map/ppermute | solution.py:82
  139.5 23.6 %collective-permute-start.11 = (bf16[128,4096]{1,0:T(8,128)(2,1)S(1)}, bf16[128,4096]{1,0:T(8,128)(2,1)S(1)}, u32[]{:S(2)}, u32[]{:S(2)}) collective-permute-start(bf16[128,4096]{1,0:T(8,128)(2,1)S(1)} %collective-permute-done.10), channel_id=1, source_target_pairs={{0,64},{64,128},{128,192},{192,256},{256,320},{320,384},{384,448},... | collective-permute-start | bytes 3145736 | tf_op jit(solution)/shard_map/ppermute | solution.py:80
  141.4 23.6 %collective-permute-start.8 = (bf16[128,4096]{1,0:T(8,128)(2,1)S(1)}, bf16[128,4096]{1,0:T(8,128)(2,1)S(1)}, u32[]{:S(2)}, u32[]{:S(2)}) collective-permute-start(bf16[128,4096]{1,0:T(8,128)(2,1)S(1)} %collective-permute-done.7), channel_id=1, source_target_pairs={{0,448},{64,0},{128,64},{192,128},{256,192},{320,256},{384,320},{4... | collective-permute-start | bytes 3145736 | tf_op jit(solution)/shard_map/ppermute | solution.py:82
  147.3 53.3 %copy-start.2 = (bf16[16,1024,512]{2,1,0:T(8,128)(2,1)}, bf16[16,1024,512]{2,1,0:T(8,128)(2,1)S(1)}, u32[]{:S(2)}) copy-start(bf16[16,1024,512]{2,1,0:T(8,128)(2,1)S(1)} %bitcast_dynamic-update-slice_fusion.5) | copy-start | bytes 50331652
  148.6 63.7 %copy-start.5 = (bf16[1024,512]{1,0:T(8,128)(2,1)S(1)}, bf16[1024,512]{1,0:T(8,128)(2,1)}, u32[]{:S(2)}) copy-start(bf16[1024,512]{1,0:T(8,128)(2,1)} %copy-done.4) | copy-start | bytes 3145732
  163.1 22.8 %collective-permute-start.12 = (bf16[128,4096]{1,0:T(8,128)(2,1)S(1)}, bf16[128,4096]{1,0:T(8,128)(2,1)S(1)}, u32[]{:S(2)}, u32[]{:S(2)}) collective-permute-start(bf16[128,4096]{1,0:T(8,128)(2,1)S(1)} %collective-permute-done.11), channel_id=1, source_target_pairs={{0,64},{64,128},{128,192},{192,256},{256,320},{320,384},{384,448},... | collective-permute-start | bytes 3145736 | tf_op jit(solution)/shard_map/ppermute | solution.py:80
  165.0 23.0 %collective-permute-start.9 = (bf16[128,4096]{1,0:T(8,128)(2,1)S(1)}, bf16[128,4096]{1,0:T(8,128)(2,1)S(1)}, u32[]{:S(2)}, u32[]{:S(2)}) collective-permute-start(bf16[128,4096]{1,0:T(8,128)(2,1)S(1)} %collective-permute-done.8), channel_id=1, source_target_pairs={{0,448},{64,0},{128,64},{192,128},{256,192},{320,256},{384,320},{4... | collective-permute-start | bytes 3145736 | tf_op jit(solution)/shard_map/ppermute | solution.py:82
  185.9 11.1 %collective-permute-start.13 = (bf16[64,4096]{1,0:T(8,128)(2,1)S(1)}, bf16[64,4096]{1,0:T(8,128)(2,1)S(1)}, u32[]{:S(2)}, u32[]{:S(2)}) collective-permute-start(bf16[64,4096]{1,0:T(8,128)(2,1)S(1)} %slice.8), channel_id=1, source_target_pairs={{0,64},{64,128},{128,192},{192,256},{256,320},{320,384},{384,448},... | collective-permute-start | bytes 1572872 | tf_op jit(solution)/shard_map/ppermute | solution.py:85
  188.1 10.9 %collective-permute-start.14 = (bf16[64,4096]{1,0:T(8,128)(2,1)S(1)}, bf16[64,4096]{1,0:T(8,128)(2,1)S(1)}, u32[]{:S(2)}, u32[]{:S(2)}) collective-permute-start(bf16[64,4096]{1,0:T(8,128)(2,1)S(1)} %slice.9), channel_id=1, source_target_pairs={{0,448},{64,0},{128,64},{192,128},{256,192},{320,256},{384,320},{4... | collective-permute-start | bytes 1572872 | tf_op jit(solution)/shard_map/ppermute | solution.py:86
  197.4 51.0 %copy-start.7 = (f32[64,8]{0,1:T(8,128)S(1)}, f32[64,8]{0,1:T(8,128)}, u32[]{:S(2)}) copy-start(f32[64,8]{0,1:T(8,128)} %param.10) | copy-start | bytes 6148
  201.9 17.5 %all-to-all-start.2 = ((bf16[8,128,128]{2,1,0:T(8,128)(2,1)}), bf16[8,128,128]{2,1,0:T(8,128)(2,1)S(1)}, u32[]{:S(2)}, u32[]{:S(2)}) async-start(bf16[8,128,128]{2,1,0:T(8,128)(2,1)} %constant_dynamic-slice_fusion), calls=%async_computation.2 | async-start | bytes 524288 | tf_op jit(solution)/shard_map/all_to_all | solution.py:89
  226.4 50.5 %all-to-all-start.3 = ((bf16[64,2,4096]{2,1,0:T(2,128)(2,1)}), bf16[64,2,4096]{2,1,0:T(2,128)(2,1)S(1)}, u32[]{:S(2)}, u32[]{:S(2)}) async-start(bf16[64,2,4096]{2,1,0:T(2,128)(2,1)} %reshape.58), calls=%async_computation.3 | async-start | bytes 2097152 | tf_op jit(solution)/shard_map/all_to_all | solution.py:97

commit v12 on v7

--- a/solution.py
+++ b/solution.py
@@ -38,6 +38,7 @@
         attn_partial[0].reshape(tensor_count, row_count, feature_width),
         "tensor", split_axis=0, concat_axis=0, tiled=True,
     )
+    down_first, parts = lax.optimization_barrier((down_matrix, parts))
     summed = jnp.sum(parts.astype(jnp.float32), axis=0)
     restored = normalize_dequant(summed, norm_gain, QB)
 
@@ -53,9 +54,9 @@
     recv = lax.all_to_all(send, "expert", split_axis=0, concat_axis=0, tiled=True)
     forward = [(i, (i + 1) % tensor_count) for i in range(tensor_count)]
     backward = [(i, (i - 1) % tensor_count) for i in range(tensor_count)]
-    weight_parts = [down_matrix] + [None] * (tensor_count - 1)
-    ahead = down_matrix
-    behind = down_matrix
+    weight_parts = [down_first] + [None] * (tensor_count - 1)
+    ahead = down_first
+    behind = down_first
     for step in range(1, tensor_count // 2 + 1):
         ahead = lax.ppermute(ahead, "tensor", forward)
         weight_parts[tensor_count - step] = ahead

time: 281 us -> 287 us (1.021)
  blocking collectives: 0 us -> 22.3 us
  starting transfers between devices: 103 us -> 85.5 us
    all_to_all x0 -> x1, blocking collectives: none -> 22.3 us  [on_device(): lax.all_to_all(attn_partial[0].reshape(tensor_count, row_count, feature_w...]
    ppermute x7, waiting for transfers between devices: 61.6 us -> 80 us  [on_device(): ahead = lax.ppermute(ahead, 'tensor', forward)]
    all_to_all x1, starting transfers between devices: 22 us -> 10.8 us  [on_device(): lax.all_to_all(expert_rows, 'expert', split_axis=0, concat_axis=0, tiled=...]
    ppermute x7, starting transfers between devices: 23.4 us -> 13.4 us  [on_device(): ahead = lax.ppermute(ahead, 'tensor', forward)]
    ppermute x6, waiting for transfers between devices: 8.15 us -> 0.02 us  [on_device(): behind = lax.ppermute(behind, 'tensor', backward)]
    all_to_all x1 -> x0, waiting for transfers between devices: 6.77 us -> none  [on_device(): lax.all_to_all(attn_partial[0].reshape(tensor_count, row_count, feature_w...]
    all_to_all x1, starting transfers between devices: 16 us -> 22.3 us  [on_device(): lax.all_to_all(send, 'expert', split_axis=0, concat_axis=0, tiled=True)]
    all_to_all x1 -> x0, starting transfers between devices: 5.93 us -> none  [on_device(): lax.all_to_all(attn_partial[0].reshape(tensor_count, row_count, feature_w...]
  transfers between devices with their start and end apart: 19 -> 18, of which waited for: 15 -> 11; matrix products, arithmetic and copies ran while one was open for 8% -> 8% of each run, Pallas kernels for 0% -> 0%
where the time goes in v12:
time: 287 us; the launch traced here: 286 us
  waiting for transfers between devices  141 us (49%)
  starting transfers between devices  85.5 us (30%)
  blocking collectives  22.3 us (8%)
  local copies, waits for them, and re-layouts  20.1 us (7%)
  matrix products  15.5 us (5%)
    ppermute x7, waiting for transfers between devices, on_device(): ahead = lax.ppermute(ahead, 'tensor', forward)  80 us
    all_to_all x1, waiting for transfers between devices, on_device(): lax.all_to_all(expert_rows, 'expert', split_axis=0, concat_axis=0, tiled=...  28.3 us
    ppermute x6, starting transfers between devices, on_device(): behind = lax.ppermute(behind, 'tensor', backward)  27.7 us
    all_to_all x1, blocking collectives, on_device(): lax.all_to_all(attn_partial[0].reshape(tensor_count, row_count, feature_w...  22.3 us
    all_to_all x1, starting transfers between devices, on_device(): lax.all_to_all(send, 'expert', split_axis=0, concat_axis=0, tiled=True)  22.3 us
    all_to_all x1, waiting for transfers between devices, on_device(): lax.all_to_all(send, 'expert', split_axis=0, concat_axis=0, tiled=True)  21.7 us
    ppermute x7, starting transfers between devices, on_device(): ahead = lax.ppermute(ahead, 'tensor', forward)  13.4 us
    unnamed x27, local copies, waits for them, and re-layouts  11.2 us
  transfers between devices with their start and end apart: 18, of which 11 were waited for; matrix products, arithmetic and copies ran while one was open for 8% of the time, Pallas kernels for 0%

profile of v12, /device:TPU:1, one launch (start us, length us, event | category | flops | bytes accessed | tf_op | source)
XLA Modules:
  0.0 286.2 jit_solution(1697366286836205253)
XLA Ops:
  0.0 22.3 %all_to_all.30 = bf16[8,8,4096]{2,1,0:T(8,128)(2,1)S(1)} all-to-all(bf16[8,8,4096]{2,1,0:T(8,128)(2,1)} %bitcast.160), channel_id=1, replica_groups=mesh['tensor'=8,'expert'=64] {'tensor'}, dimensions={0} | all-to-all | bytes 1048576 | tf_op jit(solution)/shard_map/all_to_all | solution.py:37
  22.3 1.9 collective-permute-start.3
  25.0 4.6 %collective-permute-start = (bf16[1024,512]{1,0:T(8,128)(2,1)}, bf16[1024,512]{1,0:T(8,128)(2,1)}, u32[]{:S(2)}, u32[]{:S(2)}) collective-permute-start(bf16[1024,512]{1,0:T(8,128)(2,1)} %bitcast.157), channel_id=1, source_target_pairs={{0,448},{64,0},{128,64},{192,128},{256,192},{320,256},{384,320},{4... | collective-permute-start | bytes 3145736 | tf_op jit(solution)/shard_map/ppermute | solution.py:64
  29.6 16.7 %collective-permute-done.3 = bf16[1024,512]{1,0:T(8,128)(2,1)S(1)} collective-permute-done((bf16[1024,512]{1,0:T(8,128)(2,1)}, bf16[1024,512]{1,0:T(8,128)(2,1)S(1)}, u32[]{:S(2)}, u32[]{:S(2)}) %collective-permute-start.3) | collective-permute-done | bytes 1048608 | tf_op jit(solution)/shard_map/ppermute | solution.py:61
  46.3 1.9 collective-permute-start.4
  49.7 4.6 %collective-permute-start.1 = (bf16[1024,512]{1,0:T(8,128)(2,1)}, bf16[1024,512]{1,0:T(8,128)(2,1)}, u32[]{:S(2)}, u32[]{:S(2)}) collective-permute-start(bf16[1024,512]{1,0:T(8,128)(2,1)} %collective-permute-done), channel_id=1, source_target_pairs={{0,448},{64,0},{128,64},{192,128},{256,192},{320,256},{384,320},{4... | collective-permute-start | bytes 3145736 | tf_op jit(solution)/shard_map/ppermute | solution.py:64
  54.3 15.2 %collective-permute-done.4 = bf16[1024,512]{1,0:T(8,128)(2,1)} collective-permute-done((bf16[1024,512]{1,0:T(8,128)(2,1)S(1)}, bf16[1024,512]{1,0:T(8,128)(2,1)}, u32[]{:S(2)}, u32[]{:S(2)}) %collective-permute-start.4) | collective-permute-done | bytes 1048608 | tf_op jit(solution)/shard_map/ppermute | solution.py:61
  69.4 1.9 collective-permute-start.5
  72.6 2.1 copy.43
  74.7 22.3 %all-to-all-start.1 = ((bf16[64,2,4096]{2,1,0:T(2,128)(2,1)}), bf16[64,2,4096]{2,1,0:T(2,128)(2,1)S(1)}, u32[]{:S(2)}, u32[]{:S(2)}) async-start(bf16[64,2,4096]{2,1,0:T(2,128)(2,1)} %copy.43), calls=%async_computation.1 | async-start | bytes 2097152 | tf_op jit(solution)/shard_map/all_to_all | solution.py:54
  97.0 4.9 %collective-permute-start.2 = (bf16[1024,512]{1,0:T(8,128)(2,1)}, bf16[1024,512]{1,0:T(8,128)(2,1)}, u32[]{:S(2)}, u32[]{:S(2)}) collective-permute-start(bf16[1024,512]{1,0:T(8,128)(2,1)} %collective-permute-done.1), channel_id=1, source_target_pairs={{0,448},{64,0},{128,64},{192,128},{256,192},{320,256},{384,320},{4... | collective-permute-start | bytes 3145736 | tf_op jit(solution)/shard_map/ppermute | solution.py:64
  101.8 1.9 collective-permute-start.6
  103.8 21.7 %all-to-all-done.1 = bf16[64,2,4096]{2,1,0:T(2,128)(2,1)S(1)} async-done(((bf16[64,2,4096]{2,1,0:T(2,128)(2,1)}), bf16[64,2,4096]{2,1,0:T(2,128)(2,1)S(1)}, u32[]{:S(2)}, u32[]{:S(2)}) %all-to-all-start.1) | async-done | bytes 1048608 | tf_op jit(solution)/shard_map/all_to_all | solution.py:54
  126.5 2.7 collective-permute-done.6
  130.7 1.9 collective-permute-start.10
  132.7 4.6 %collective-permute-start.7 = (bf16[128,4096]{1,0:T(8,128)(2,1)S(1)}, bf16[128,4096]{1,0:T(8,128)(2,1)S(1)}, u32[]{:S(2)}, u32[]{:S(2)}) collective-permute-start(bf16[128,4096]{1,0:T(8,128)(2,1)S(1)} %reshape.57), channel_id=1, source_target_pairs={{0,448},{64,0},{128,64},{192,128},{256,192},{320,256},{384,320},{4... | collective-permute-start | bytes 3145736 | tf_op jit(solution)/shard_map/ppermute | solution.py:82
  144.2 12.8 %collective-permute-done.10 = bf16[128,4096]{1,0:T(8,128)(2,1)S(1)} collective-permute-done((bf16[128,4096]{1,0:T(8,128)(2,1)S(1)}, bf16[128,4096]{1,0:T(8,128)(2,1)S(1)}, u32[]{:S(2)}, u32[]{:S(2)}) %collective-permute-start.10) | collective-permute-done | bytes 1048608 | tf_op jit(solution)/shard_map/ppermute | solution.py:80
  157.0 1.9 collective-permute-start.11
  158.9 4.6 %collective-permute-start.8 = (bf16[128,4096]{1,0:T(8,128)(2,1)S(1)}, bf16[128,4096]{1,0:T(8,128)(2,1)S(1)}, u32[]{:S(2)}, u32[]{:S(2)}) collective-permute-start(bf16[128,4096]{1,0:T(8,128)(2,1)S(1)} %collective-permute-done.7), channel_id=1, source_target_pairs={{0,448},{64,0},{128,64},{192,128},{256,192},{320,256},{384,320},{4... | collective-permute-start | bytes 3145736 | tf_op jit(solution)/shard_map/ppermute | solution.py:82
  166.1 16.2 %collective-permute-done.11 = bf16[128,4096]{1,0:T(8,128)(2,1)S(1)} collective-permute-done((bf16[128,4096]{1,0:T(8,128)(2,1)S(1)}, bf16[128,4096]{1,0:T(8,128)(2,1)S(1)}, u32[]{:S(2)}, u32[]{:S(2)}) %collective-permute-start.11) | collective-permute-done | bytes 1048608 | tf_op jit(solution)/shard_map/ppermute | solution.py:80
  184.3 4.6 %collective-permute-start.9 = (bf16[128,4096]{1,0:T(8,128)(2,1)S(1)}, bf16[128,4096]{1,0:T(8,128)(2,1)S(1)}, u32[]{:S(2)}, u32[]{:S(2)}) collective-permute-start(bf16[128,4096]{1,0:T(8,128)(2,1)S(1)} %collective-permute-done.8), channel_id=1, source_target_pairs={{0,448},{64,0},{128,64},{192,128},{256,192},{320,256},{384,320},{4... | collective-permute-start | bytes 3145736 | tf_op jit(solution)/shard_map/ppermute | solution.py:82
  190.6 16.3 %collective-permute-done.12 = bf16[128,4096]{1,0:T(8,128)(2,1)S(1)} collective-permute-done((bf16[128,4096]{1,0:T(8,128)(2,1)S(1)}, bf16[128,4096]{1,0:T(8,128)(2,1)S(1)}, u32[]{:S(2)}, u32[]{:S(2)}) %collective-permute-start.12) | collective-permute-done | bytes 1048608 | tf_op jit(solution)/shard_map/ppermute | solution.py:80
  206.9 1.9 collective-permute-start.13
  208.9 4.8 %collective-permute-start.14 = (bf16[64,4096]{1,0:T(8,128)(2,1)S(1)}, bf16[64,4096]{1,0:T(8,128)(2,1)S(1)}, u32[]{:S(2)}, u32[]{:S(2)}) collective-permute-start(bf16[64,4096]{1,0:T(8,128)(2,1)S(1)} %slice.9), channel_id=1, source_target_pairs={{0,448},{64,0},{128,64},{192,128},{256,192},{320,256},{384,320},{4... | collective-permute-start | bytes 1572872 | tf_op jit(solution)/shard_map/ppermute | solution.py:86
  215.0 4.3 %collective-permute-done.13 = bf16[64,4096]{1,0:T(8,128)(2,1)S(1)} collective-permute-done((bf16[64,4096]{1,0:T(8,128)(2,1)S(1)}, bf16[64,4096]{1,0:T(8,128)(2,1)S(1)}, u32[]{:S(2)}, u32[]{:S(2)}) %collective-permute-start.13) | collective-permute-done | bytes 524320 | tf_op jit(solution)/shard_map/ppermute | solution.py:85
  223.2 4.7 %all-to-all-start.2 = ((bf16[8,128,128]{2,1,0:T(8,128)(2,1)}), bf16[8,128,128]{2,1,0:T(8,128)(2,1)S(1)}, u32[]{:S(2)}, u32[]{:S(2)}) async-start(bf16[8,128,128]{2,1,0:T(8,128)(2,1)} %constant_dynamic-slice_fusion), calls=%async_computation.2 | async-start | bytes 524288 | tf_op jit(solution)/shard_map/all_to_all | solution.py:89
  227.9 2.3 bitcast_dynamic-update-slice_fusion.1
  231.2 5.9 %all-to-all-done.2 = bf16[8,128,128]{2,1,0:T(8,128)(2,1)S(1)} async-done(((bf16[8,128,128]{2,1,0:T(8,128)(2,1)}), bf16[8,128,128]{2,1,0:T(8,128)(2,1)S(1)}, u32[]{:S(2)}, u32[]{:S(2)}) %all-to-all-start.2) | async-done | bytes 262176 | tf_op jit(solution)/shard_map/all_to_all | solution.py:89
  237.4 4.7 %convolution_convert_fusion.1 = bf16[128,8,512]{2,0,1:T(8,128)(2,1)S(1)} fusion(bf16[128,1024,1]{0,1,2:T(8,128)(2,1)S(1)} %bitcast.155, bf16[8,1024,512]{2,1,0:T(8,128)(2,1)} %bitcast_dynamic-update-slice_fusion), kind=kOutput, calls=%fused_computation.5 | convolution fusion | flops 1074266112 | bytes 9699328 | tf_op jit(solution)/shard_map/sh,mhc->smc/dot_general | solution.py:93
  244.6 10.8 %all-to-all-start.3 = ((bf16[64,2,4096]{2,1,0:T(2,128)(2,1)}), bf16[64,2,4096]{2,1,0:T(2,128)(2,1)S(1)}, u32[]{:S(2)}, u32[]{:S(2)}) async-start(bf16[64,2,4096]{2,1,0:T(2,128)(2,1)} %reshape.58), calls=%async_computation.3 | async-start | bytes 2097152 | tf_op jit(solution)/shard_map/all_to_all | solution.py:98
  255.7 28.3 %all-to-all-done.3 = bf16[64,2,4096]{2,1,0:T(2,128)(2,1)S(1)} async-done(((bf16[64,2,4096]{2,1,0:T(2,128)(2,1)}), bf16[64,2,4096]{2,1,0:T(2,128)(2,1)S(1)}, u32[]{:S(2)}, u32[]{:S(2)}) %all-to-all-start.3) | async-done | bytes 1048608 | tf_op jit(solution)/shard_map/all_to_all | solution.py:98
  284.0 2.2 fusion
  (82 shorter events, 28.3 us)
Async XLA Ops:
  0.0 164.8 %copy-start = (bf16[1,4096,128]{2,1,0:T(8,128)(2,1)S(1)}, bf16[1,4096,128]{2,1,0:T(8,128)(2,1)}, u32[]{:S(2)}) copy-start(bf16[1,4096,128]{2,1,0:T(8,128)(2,1)} %param.12) | copy-start | bytes 3145732
  22.3 24.1 %collective-permute-start.3 = (bf16[1024,512]{1,0:T(8,128)(2,1)}, bf16[1024,512]{1,0:T(8,128)(2,1)S(1)}, u32[]{:S(2)}, u32[]{:S(2)}) collective-permute-start(bf16[1024,512]{1,0:T(8,128)(2,1)} %bitcast.156), channel_id=1, source_target_pairs={{0,64},{64,128},{128,192},{192,256},{256,320},{320,384},{384,448},... | collective-permute-start | bytes 3145736 | tf_op jit(solution)/shard_map/ppermute | solution.py:61
  25.0 24.7 %collective-permute-start = (bf16[1024,512]{1,0:T(8,128)(2,1)}, bf16[1024,512]{1,0:T(8,128)(2,1)}, u32[]{:S(2)}, u32[]{:S(2)}) collective-permute-start(bf16[1024,512]{1,0:T(8,128)(2,1)} %bitcast.157), channel_id=1, source_target_pairs={{0,448},{64,0},{128,64},{192,128},{256,192},{320,256},{384,320},{4... | collective-permute-start | bytes 3145736 | tf_op jit(solution)/shard_map/ppermute | solution.py:64
  46.3 25.0 %copy-start.4 = (bf16[1024,512]{1,0:T(8,128)(2,1)}, bf16[1024,512]{1,0:T(8,128)(2,1)S(1)}, u32[]{:S(2)}) copy-start(bf16[1024,512]{1,0:T(8,128)(2,1)S(1)} %collective-permute-done.3) | copy-start | bytes 3145732
  46.3 23.1 %collective-permute-start.4 = (bf16[1024,512]{1,0:T(8,128)(2,1)S(1)}, bf16[1024,512]{1,0:T(8,128)(2,1)}, u32[]{:S(2)}, u32[]{:S(2)}) collective-permute-start(bf16[1024,512]{1,0:T(8,128)(2,1)S(1)} %collective-permute-done.3), channel_id=1, source_target_pairs={{0,64},{64,128},{128,192},{192,256},{256,320},{320,384},{384,448},... | collective-permute-start | bytes 3145736 | tf_op jit(solution)/shard_map/ppermute | solution.py:61
  49.7 47.3 %collective-permute-start.1 = (bf16[1024,512]{1,0:T(8,128)(2,1)}, bf16[1024,512]{1,0:T(8,128)(2,1)}, u32[]{:S(2)}, u32[]{:S(2)}) collective-permute-start(bf16[1024,512]{1,0:T(8,128)(2,1)} %collective-permute-done), channel_id=1, source_target_pairs={{0,448},{64,0},{128,64},{192,128},{256,192},{320,256},{384,320},{4... | collective-permute-start | bytes 3145736 | tf_op jit(solution)/shard_map/ppermute | solution.py:64
  69.4 32.4 %collective-permute-start.5 = (bf16[1024,512]{1,0:T(8,128)(2,1)}, bf16[1024,512]{1,0:T(8,128)(2,1)}, u32[]{:S(2)}, u32[]{:S(2)}) collective-permute-start(bf16[1024,512]{1,0:T(8,128)(2,1)} %collective-permute-done.4), channel_id=1, source_target_pairs={{0,64},{64,128},{128,192},{192,256},{256,320},{320,384},{384,448},... | collective-permute-start | bytes 3145736 | tf_op jit(solution)/shard_map/ppermute | solution.py:61
  72.6 71.1 %copy-start.1 = (bf16[1,4096,128]{2,1,0:T(8,128)(2,1)S(1)}, bf16[1,4096,128]{2,1,0:T(8,128)(2,1)}, u32[]{:S(2)}) copy-start(bf16[1,4096,128]{2,1,0:T(8,128)(2,1)} %param.11) | copy-start | bytes 3145732
  74.7 50.8 %all-to-all-start.1 = ((bf16[64,2,4096]{2,1,0:T(2,128)(2,1)}), bf16[64,2,4096]{2,1,0:T(2,128)(2,1)S(1)}, u32[]{:S(2)}, u32[]{:S(2)}) async-start(bf16[64,2,4096]{2,1,0:T(2,128)(2,1)} %copy.43), calls=%async_computation.1 | async-start | bytes 2097152 | tf_op jit(solution)/shard_map/all_to_all | solution.py:54
  97.0 28.5 %collective-permute-start.2 = (bf16[1024,512]{1,0:T(8,128)(2,1)}, bf16[1024,512]{1,0:T(8,128)(2,1)}, u32[]{:S(2)}, u32[]{:S(2)}) collective-permute-start(bf16[1024,512]{1,0:T(8,128)(2,1)} %collective-permute-done.1), channel_id=1, source_target_pairs={{0,448},{64,0},{128,64},{192,128},{256,192},{320,256},{384,320},{4... | collective-permute-start | bytes 3145736 | tf_op jit(solution)/shard_map/ppermute | solution.py:64
  101.8 27.4 %collective-permute-start.6 = (bf16[1024,512]{1,0:T(8,128)(2,1)}, bf16[1024,512]{1,0:T(8,128)(2,1)}, u32[]{:S(2)}, u32[]{:S(2)}) collective-permute-start(bf16[1024,512]{1,0:T(8,128)(2,1)} %collective-permute-done.5), channel_id=1, source_target_pairs={{0,64},{64,128},{128,192},{192,256},{256,320},{320,384},{384,448},... | collective-permute-start | bytes 3145736 | tf_op jit(solution)/shard_map/ppermute | solution.py:61
  125.5 1.0 copy-start.3
  130.7 26.2 %collective-permute-start.10 = (bf16[128,4096]{1,0:T(8,128)(2,1)S(1)}, bf16[128,4096]{1,0:T(8,128)(2,1)S(1)}, u32[]{:S(2)}, u32[]{:S(2)}) collective-permute-start(bf16[128,4096]{1,0:T(8,128)(2,1)S(1)} %reshape.57), channel_id=1, source_target_pairs={{0,64},{64,128},{128,192},{192,256},{256,320},{320,384},{384,448},... | collective-permute-start | bytes 3145736 | tf_op jit(solution)/shard_map/ppermute | solution.py:80
  132.7 26.2 %collective-permute-start.7 = (bf16[128,4096]{1,0:T(8,128)(2,1)S(1)}, bf16[128,4096]{1,0:T(8,128)(2,1)S(1)}, u32[]{:S(2)}, u32[]{:S(2)}) collective-permute-start(bf16[128,4096]{1,0:T(8,128)(2,1)S(1)} %reshape.57), channel_id=1, source_target_pairs={{0,448},{64,0},{128,64},{192,128},{256,192},{320,256},{384,320},{4... | collective-permute-start | bytes 3145736 | tf_op jit(solution)/shard_map/ppermute | solution.py:82
  157.0 25.4 %collective-permute-start.11 = (bf16[128,4096]{1,0:T(8,128)(2,1)S(1)}, bf16[128,4096]{1,0:T(8,128)(2,1)S(1)}, u32[]{:S(2)}, u32[]{:S(2)}) collective-permute-start(bf16[128,4096]{1,0:T(8,128)(2,1)S(1)} %collective-permute-done.10), channel_id=1, source_target_pairs={{0,64},{64,128},{128,192},{192,256},{256,320},{320,384},{384,448},... | collective-permute-start | bytes 3145736 | tf_op jit(solution)/shard_map/ppermute | solution.py:80
  158.9 25.4 %collective-permute-start.8 = (bf16[128,4096]{1,0:T(8,128)(2,1)S(1)}, bf16[128,4096]{1,0:T(8,128)(2,1)S(1)}, u32[]{:S(2)}, u32[]{:S(2)}) collective-permute-start(bf16[128,4096]{1,0:T(8,128)(2,1)S(1)} %collective-permute-done.7), channel_id=1, source_target_pairs={{0,448},{64,0},{128,64},{192,128},{256,192},{320,256},{384,320},{4... | collective-permute-start | bytes 3145736 | tf_op jit(solution)/shard_map/ppermute | solution.py:82
  164.8 44.1 %copy-start.2 = (bf16[8,1024,512]{2,1,0:T(8,128)(2,1)}, bf16[8,1024,512]{2,1,0:T(8,128)(2,1)S(1)}, u32[]{:S(2)}) copy-start(bf16[8,1024,512]{2,1,0:T(8,128)(2,1)S(1)} %bitcast_dynamic-update-slice_fusion.2) | copy-start | bytes 25165828
  182.3 24.5 %collective-permute-start.12 = (bf16[128,4096]{1,0:T(8,128)(2,1)S(1)}, bf16[128,4096]{1,0:T(8,128)(2,1)S(1)}, u32[]{:S(2)}, u32[]{:S(2)}) collective-permute-start(bf16[128,4096]{1,0:T(8,128)(2,1)S(1)} %collective-permute-done.11), channel_id=1, source_target_pairs={{0,64},{64,128},{128,192},{192,256},{256,320},{320,384},{384,448},... | collective-permute-start | bytes 3145736 | tf_op jit(solution)/shard_map/ppermute | solution.py:80
  184.3 24.6 %collective-permute-start.9 = (bf16[128,4096]{1,0:T(8,128)(2,1)S(1)}, bf16[128,4096]{1,0:T(8,128)(2,1)S(1)}, u32[]{:S(2)}, u32[]{:S(2)}) collective-permute-start(bf16[128,4096]{1,0:T(8,128)(2,1)S(1)} %collective-permute-done.8), channel_id=1, source_target_pairs={{0,448},{64,0},{128,64},{192,128},{256,192},{320,256},{384,320},{4... | collective-permute-start | bytes 3145736 | tf_op jit(solution)/shard_map/ppermute | solution.py:82
  206.9 12.4 %collective-permute-start.13 = (bf16[64,4096]{1,0:T(8,128)(2,1)S(1)}, bf16[64,4096]{1,0:T(8,128)(2,1)S(1)}, u32[]{:S(2)}, u32[]{:S(2)}) collective-permute-start(bf16[64,4096]{1,0:T(8,128)(2,1)S(1)} %slice.8), channel_id=1, source_target_pairs={{0,64},{64,128},{128,192},{192,256},{256,320},{320,384},{384,448},... | collective-permute-start | bytes 1572872 | tf_op jit(solution)/shard_map/ppermute | solution.py:85
  208.9 11.4 %collective-permute-start.14 = (bf16[64,4096]{1,0:T(8,128)(2,1)S(1)}, bf16[64,4096]{1,0:T(8,128)(2,1)S(1)}, u32[]{:S(2)}, u32[]{:S(2)}) collective-permute-start(bf16[64,4096]{1,0:T(8,128)(2,1)S(1)} %slice.9), channel_id=1, source_target_pairs={{0,448},{64,0},{128,64},{192,128},{256,192},{320,256},{384,320},{4... | collective-permute-start | bytes 1572872 | tf_op jit(solution)/shard_map/ppermute | solution.py:86
  214.9 15.2 %copy-start.5 = (bf16[1024,512]{1,0:T(8,128)(2,1)S(1)}, bf16[1024,512]{1,0:T(8,128)(2,1)}, u32[]{:S(2)}) copy-start(bf16[1024,512]{1,0:T(8,128)(2,1)} %copy-done.4) | copy-start | bytes 3145732
  223.2 14.0 %all-to-all-start.2 = ((bf16[8,128,128]{2,1,0:T(8,128)(2,1)}), bf16[8,128,128]{2,1,0:T(8,128)(2,1)S(1)}, u32[]{:S(2)}, u32[]{:S(2)}) async-start(bf16[8,128,128]{2,1,0:T(8,128)(2,1)} %constant_dynamic-slice_fusion), calls=%async_computation.2 | async-start | bytes 524288 | tf_op jit(solution)/shard_map/all_to_all | solution.py:89
  237.4 18.1 %copy-start.6 = (f32[64,8]{0,1:T(8,128)S(1)}, f32[64,8]{0,1:T(8,128)}, u32[]{:S(2)}) copy-start(f32[64,8]{0,1:T(8,128)} %param.10) | copy-start | bytes 6148
  244.6 39.4 %all-to-all-start.3 = ((bf16[64,2,4096]{2,1,0:T(2,128)(2,1)}), bf16[64,2,4096]{2,1,0:T(2,128)(2,1)S(1)}, u32[]{:S(2)}, u32[]{:S(2)}) async-start(bf16[64,2,4096]{2,1,0:T(2,128)(2,1)} %reshape.58), calls=%async_computation.3 | async-start | bytes 2097152 | tf_op jit(solution)/shard_map/all_to_all | solution.py:98
